TPU v7x, 1024 devices: a whole 8x8x8 slice. The times are simulated.
1024 devices in a mesh: dp: 16 (over y, x_hi), pipe: 8 (over x_lo, core), seq: 8 (over z).
Axes of the slice: x: 8 (x_hi: 2, x_lo: 4; x = x_hi * 4 + x_lo), y: 8, z: 8, core: 2. Of those that a mesh axis runs over, the one named last changes fastest.
Arguments:
- query_proj: bfloat16 [8, 16, 1024, 2048], P('pipe', 'dp', 'seq'), may hold values from -6 to 6
- key_proj: bfloat16 [8, 16, 1024, 1024], P('pipe', 'dp', 'seq'), may hold values from -6 to 6
- value_proj: bfloat16 [8, 16, 1024, 1024], P('pipe', 'dp', 'seq'), may hold values from -24 to 24
- out_grad: bfloat16 [8, 16, 1024, 2048], P('pipe', 'dp', 'seq'), may hold values from -12 to 12
- lowest_key_index: int32 [8, 16, 1024], P('pipe', 'dp'), may hold values from 0 to 1023, as said below
- query_gain: float32 [8, 128], P('pipe'), may hold values from 0.1 to 1.9
- key_gain: float32 [8, 128], P('pipe'), may hold values from 0.1 to 1.9
Outputs:
- query_grad: bfloat16 [8, 16, 1024, 2048], P('pipe', 'dp', 'seq')
- key_grad: bfloat16 [8, 16, 1024, 1024], P('pipe', 'dp', 'seq')
- value_grad: bfloat16 [8, 16, 1024, 1024], P('pipe', 'dp', 'seq')
- query_gain_grad: float32 [8, 128], P('pipe')
- key_gain_grad: float32 [8, 128], P('pipe')
Inputs may be any that keep to these rules, and one draw needn't show every extreme that they name: Query i may see keys lowest_key_index[i] to i: lowest_key_index never decreases along the tokens of a block, lowest_key_index[i] <= i and i - lowest_key_index[i] < 128; lowest_key_index[i] is i - 127 or the first token of i's document, whichever is larger.
All inputs are finite; a program needn't handle non-finite values.
Results may differ from a plain program's by a relative error of at most 0.0073.
Values may be sent and summed in bfloat16 or wider, within the bound.
No kernel may reach another device: no remote copies, remote signals or barrier semaphores. Data moves between devices by JAX's collectives and lax.ppermute only.
A program may use at most 32 MiB of HBM per device.

v0:
```python
import jax
import jax.numpy as jnp
from jax import lax
from jax.sharding import PartitionSpec as P

WINDOW = 128


epsilon = 1e-06
score_scale = 168.0 ** (-0.5)


def passed_along(x, axis, by):
    devices = lax.axis_size(axis)
    return lax.ppermute(x, axis, [(i, (i + by) % devices) for i in range(devices)])


def normalize(values, gain):
    inverse = lax.rsqrt(jnp.mean(values * values, axis=-1, keepdims=True) + epsilon)
    unit = values * inverse
    return (unit, inverse, (unit * gain).astype(jnp.bfloat16))


def norm_back(grad_normed, unit, inverse, gain):
    grad_unit = grad_normed * gain
    centered = grad_unit - unit * jnp.mean(grad_unit * unit, axis=-1, keepdims=True)
    return inverse * centered


def on_device(query_proj, key_proj, value_proj, out_grad, lowest_key_index, query_gain, key_gain):
    local_tokens = query_proj.shape[2]
    query_width = query_proj.shape[3]
    key_width = key_proj.shape[3]
    query_local = query_proj.reshape(local_tokens, query_width)
    key_local = key_proj.reshape(local_tokens, key_width)
    value_local = value_proj.reshape(local_tokens, key_width)
    grad_local = out_grad.reshape(local_tokens, query_width)
    arrived = passed_along(grad_local, "pipe", -1)
    query_heads, key_heads, value_heads = (
        lax.all_to_all(query_local, "seq", split_axis=1, concat_axis=0, tiled=True),
        lax.all_to_all(key_local, "seq", split_axis=1, concat_axis=0, tiled=True),
        lax.all_to_all(value_local, "seq", split_axis=1, concat_axis=0, tiled=True),
    )
    grad_heads = lax.all_to_all(arrived, "seq", split_axis=1, concat_axis=0, tiled=True)
    total = query_heads.shape[0]
    head_dim = query_gain.shape[1]
    groups = key_heads.shape[1] // head_dim
    ratio = query_heads.shape[1] // (groups * head_dim)
    floor_row = lowest_key_index.reshape(total)
    query_scale = query_gain.reshape(head_dim)
    key_scale = key_gain.reshape(head_dim)
    query_unit, query_inverse, query_normed = normalize(
        query_heads.astype(jnp.float32).reshape(total, groups, ratio, head_dim), query_scale
    )
    key_unit, key_inverse, key_normed = normalize(
        key_heads.astype(jnp.float32).reshape(total, groups, head_dim), key_scale
    )
    query_lay = jnp.transpose(query_normed, (1, 2, 0, 3))
    grad_lay = jnp.transpose(grad_heads.reshape(total, groups, ratio, head_dim), (1, 2, 0, 3))
    key_lay = jnp.transpose(key_normed, (1, 0, 2))
    value_lay = jnp.transpose(value_heads.reshape(total, groups, head_dim), (1, 0, 2))
    block_rows = 2 * WINDOW
    query_parts = []
    key_acc = jnp.zeros((groups, total, head_dim), jnp.float32)
    value_acc = jnp.zeros((groups, total, head_dim), jnp.float32)
    for block in range(total // block_rows):
        first = block * block_rows
        stop = first + block_rows
        key_first = max(first - WINDOW, 0)
        query_tile = query_lay[:, :, first:stop]
        grad_tile = grad_lay[:, :, first:stop]
        key_tile = key_lay[:, key_first:stop]
        value_tile = value_lay[:, key_first:stop]
        key_places = jnp.arange(key_first, stop, dtype=jnp.int32)
        query_places = jnp.arange(first, stop, dtype=jnp.int32)
        visible = (key_places[None, :] <= query_places[:, None]) & (
            key_places[None, :] >= floor_row[first:stop, None]
        )
        scores = (
            jnp.einsum("grqd,gkd->grqk", query_tile, key_tile, preferred_element_type=jnp.float32)
            * score_scale
        )
        exp_scores = jnp.where(visible, jnp.exp(scores), jnp.zeros_like(scores))
        weights = exp_scores / jnp.sum(exp_scores, axis=-1, keepdims=True)
        weights_reduced = weights.astype(jnp.bfloat16)
        attended = jnp.einsum(
            "grqk,gkd->grqd", weights_reduced, value_tile, preferred_element_type=jnp.float32
        )
        delta_col = jnp.sum(grad_tile.astype(jnp.float32) * attended, axis=-1, keepdims=True)
        prob_grad = jnp.einsum(
            "grqd,gkd->grqk", grad_tile, value_tile, preferred_element_type=jnp.float32
        )
        logit_gradient = (weights * (prob_grad - delta_col) * score_scale).astype(jnp.bfloat16)
        query_parts.append(
            jnp.einsum(
                "grqk,gkd->grqd", logit_gradient, key_tile, preferred_element_type=jnp.float32
            )
        )
        key_acc = key_acc.at[:, key_first:stop].add(
            jnp.einsum(
                "grqk,grqd->gkd", logit_gradient, query_tile, preferred_element_type=jnp.float32
            )
        )
        value_acc = value_acc.at[:, key_first:stop].add(
            jnp.einsum(
                "grqk,grqd->gkd", weights_reduced, grad_tile, preferred_element_type=jnp.float32
            )
        )
    query_normed_grad = jnp.transpose(jnp.concatenate(query_parts, axis=2), (2, 0, 1, 3))
    key_normed_grad = jnp.transpose(key_acc, (1, 0, 2))
    value_rows = jnp.transpose(value_acc, (1, 0, 2))
    query_grad = (
        norm_back(query_normed_grad, query_unit, query_inverse, query_scale)
        .astype(jnp.bfloat16)
        .reshape(total, groups * ratio * head_dim)
    )
    key_grad = (
        norm_back(key_normed_grad, key_unit, key_inverse, key_scale)
        .astype(jnp.bfloat16)
        .reshape(total, groups * head_dim)
    )
    value_grad = value_rows.astype(jnp.bfloat16).reshape(total, groups * head_dim)
    query_term = jnp.sum(query_normed_grad * query_unit, axis=(0, 1, 2))
    key_term = jnp.sum(key_normed_grad * key_unit, axis=(0, 1))
    query_sum, key_sum = lax.psum((query_term, key_term), ("dp", "seq"))
    query_back, key_back, value_back = (
        lax.all_to_all(query_grad, "seq", split_axis=0, concat_axis=1, tiled=True),
        lax.all_to_all(key_grad, "seq", split_axis=0, concat_axis=1, tiled=True),
        lax.all_to_all(value_grad, "seq", split_axis=0, concat_axis=1, tiled=True),
    )
    return (
        query_back.reshape(1, 1, local_tokens, query_width),
        key_back.reshape(1, 1, local_tokens, key_width),
        value_back.reshape(1, 1, local_tokens, key_width),
        query_sum.reshape(1, head_dim),
        key_sum.reshape(1, head_dim),
    )


def solution(mesh):
    return jax.shard_map(
        on_device,
        mesh=mesh,
        in_specs=(
            P("pipe", "dp", "seq", None),
            P("pipe", "dp", "seq", None),
            P("pipe", "dp", "seq", None),
            P("pipe", "dp", "seq", None),
            P("pipe", "dp", None),
            P("pipe", None),
            P("pipe", None),
        ),
        out_specs=(
            P("pipe", "dp", "seq", None),
            P("pipe", "dp", "seq", None),
            P("pipe", "dp", "seq", None),
            P("pipe", None),
            P("pipe", None),
        ),
        check_vma=False,
    )
```

profile of v0, /device:TPU:2, one launch (start us, length us, event | category | flops | bytes accessed | tf_op | source)
XLA Modules:
  0.0 570.5 jit_solution(7331009648178389668)
XLA Ops:
  0.6 1.0 copy.138
  1.7 0.7 copy.90
  2.4 16.7 %all-to-all-start.1 = ((bf16[128,8,128]{2,0,1:T(8,128)(2,1)}), bf16[128,8,128]{2,0,1:T(8,128)(2,1)S(1)}, u32[]{:S(2)}, u32[]{:S(2)}) async-start(bf16[128,8,128]{2,0,1:T(8,128)(2,1)} %copy.90), calls=%async_computation.1 | async-start | bytes 524288 | tf_op jit(solution)/shard_map/all_to_all | solution.py:41
  19.1 1.9 collective-permute-start
  21.1 0.7 fusion.53
  21.8 1.0 copy.87
  22.8 0.7 copy.94
  23.7 0.8 compare_and_fusion.1
  24.5 6.5 %all-to-all-done.1 = bf16[128,8,128]{2,0,1:T(8,128)(2,1)S(1)} async-done(((bf16[128,8,128]{2,0,1:T(8,128)(2,1)}), bf16[128,8,128]{2,0,1:T(8,128)(2,1)S(1)}, u32[]{:S(2)}, u32[]{:S(2)}) %all-to-all-start.1) | async-done | bytes 262176 | tf_op jit(solution)/shard_map/all_to_all | solution.py:41
  31.0 3.5 all-to-all-start
  34.5 0.8 compare_and_fusion.2
  35.5 0.8 convert_element_type.175
  36.3 0.7 copy-done.18
  37.2 1.0 copy.91
  38.2 12.1 %all-to-all-done = bf16[128,8,256]{0,2,1:T(8,128)(2,1)S(1)} async-done(((bf16[128,8,256]{0,2,1:T(8,128)(2,1)}), bf16[128,8,256]{0,2,1:T(8,128)(2,1)S(1)}, u32[]{:S(2)}, u32[]{:S(2)}) %all-to-all-start) | async-done | bytes 524320 | tf_op jit(solution)/shard_map/all_to_all | solution.py:40
  50.4 4.1 all-to-all-start.2
  54.6 0.6 copy.88
  55.4 0.3 copy.89
  55.9 0.6 copy-done.19
  56.5 0.3 fusion.42
  56.9 0.4 fusion.46
  57.3 1.3 fusion.48
  58.7 1.3 fusion.50
  60.0 9.6 %all-to-all-done.2 = bf16[128,8,256]{0,2,1:T(8,128)(2,1)} async-done(((bf16[128,8,256]{0,2,1:T(8,128)(2,1)}), bf16[128,8,256]{0,2,1:T(8,128)(2,1)}, u32[]{:S(2)}, u32[]{:S(2)}) %all-to-all-start.2) | async-done | bytes 524320 | tf_op jit(solution)/shard_map/all_to_all | solution.py:44
  69.5 3.4 all-to-all-start.3
  73.0 2.0 fusion.52
  74.9 1.4 copy.92
  76.3 1.0 reshape.811
  77.3 1.3 copy.93
  78.6 1.3 convolution_bitcast_fusion.14
  79.9 3.4 all-to-all-done.3
  83.3 1.4 fusion.38
  84.7 0.4 fusion.41
  85.4 0.7 copy-done.12
  86.1 1.0 convolution_bitcast_fusion
  87.0 0.4 fusion.40
  87.7 1.0 convolution_bitcast_fusion.2
  88.7 0.4 fusion.39
  89.3 0.8 copy-done.2
  90.3 0.9 copy-done.10
  91.5 0.5 copy-done.7
  92.0 0.3 fusion.37
  92.4 0.3 fusion.35
  93.1 0.7 copy-done.1
  93.8 0.7 multiply_reduce_fusion.3
  94.5 1.0 multiply_convert_fusion.2
  95.6 3.7 all-to-all-start.5
  99.3 1.4 fusion.30
  100.7 0.3 fusion.28
  101.4 0.7 convert_element_type.170
  102.8 0.7 copy-done.4
  103.8 0.7 copy-done.5
  104.6 0.6 multiply_reduce_fusion
  105.2 4.5 all-to-all-done.5
  109.7 3.4 all-to-all-start.6
  113.2 0.7 multiply_convert_fusion
  114.2 0.9 copy.107
  115.1 8.4 %all-to-all-done.6 = bf16[8,128,128]{2,1,0:T(8,128)(2,1)S(1)} async-done(((bf16[8,128,128]{2,1,0:T(8,128)(2,1)}), bf16[8,128,128]{2,1,0:T(8,128)(2,1)S(1)}, u32[]{:S(2)}, u32[]{:S(2)}) %all-to-all-start.6) | async-done | bytes 262176 | tf_op jit(solution)/shard_map/all_to_all | solution.py:129
  123.5 3.5 all-to-all-start.4
  127.1 0.6 copy-done.22
  127.7 439.8 %all-reduce.2 = (f32[1,128]{1,0:T(1,128)}, f32[1,128]{1,0:T(1,128)}) all-reduce(f32[1,128]{1,0:T(1,128)S(1)} %bitcast.338, f32[1,128]{1,0:T(1,128)S(1)} %bitcast.337), channel_id=1, replica_groups=mesh['dp'=16,'pipe'=8,'seq'=8] {'dp','seq'}, use_global_device_ids=true, to_apply=%region_13.14 | all-reduce | flops 256 | bytes 2048 | tf_op jit(solution)/shard_map/psum | solution.py:125
  567.7 0.8 reshape.831
  568.7 0.8 reshape.836
  569.5 1.0 copy.116
  (75 shorter events, 4.7 us)
Async XLA Ops:
  1.6 17.5 %copy-start.23 = (bf16[1,1,128,2048]{3,2,1,0:T(8,128)(2,1)S(1)}, bf16[1,1,128,2048]{3,2,1,0:T(8,128)(2,1)}, u32[]{:S(2)}) copy-start(bf16[1,1,128,2048]{3,2,1,0:T(8,128)(2,1)} %param.26) | copy-start | bytes 1572868
  1.6 20.1 %copy-start.14 = (bf16[1,1,128,2048]{3,2,1,0:T(8,128)(2,1)S(1)}, bf16[1,1,128,2048]{3,2,1,0:T(8,128)(2,1)}, u32[]{:S(2)}) copy-start(bf16[1,1,128,2048]{3,2,1,0:T(8,128)(2,1)} %param.23) | copy-start | bytes 1572868
  2.4 28.6 %all-to-all-start.1 = ((bf16[128,8,128]{2,0,1:T(8,128)(2,1)}), bf16[128,8,128]{2,0,1:T(8,128)(2,1)S(1)}, u32[]{:S(2)}, u32[]{:S(2)}) async-start(bf16[128,8,128]{2,0,1:T(8,128)(2,1)} %copy.90), calls=%async_computation.1 | async-start | bytes 524288 | tf_op jit(solution)/shard_map/all_to_all | solution.py:41
  19.1 2.0 copy-start.21
  19.1 18.1 %collective-permute-start = (bf16[128,2048]{1,0:T(8,128)(2,1)S(1)}, bf16[128,2048]{1,0:T(8,128)(2,1)S(1)}, u32[]{:S(2)}, u32[]{:S(2)}) collective-permute-start(bf16[128,2048]{1,0:T(8,128)(2,1)S(1)} %bitcast.339), channel_id=1, source_target_pairs={{0,56},{8,0},{16,8},{24,16},{32,24},{40,32},{48,40},{56,48},{1,57}... | collective-permute-start | bytes 1572872 | tf_op jit(solution)/shard_map/ppermute | solution.py:15
  21.8 1.0 copy-start.15
  31.0 19.4 %all-to-all-start = ((bf16[128,8,256]{0,2,1:T(8,128)(2,1)}), bf16[128,8,256]{0,2,1:T(8,128)(2,1)S(1)}, u32[]{:S(2)}, u32[]{:S(2)}) async-start(bf16[128,8,256]{0,2,1:T(8,128)(2,1)} %bitcast), calls=%async_computation | async-start | bytes 1048576 | tf_op jit(solution)/shard_map/all_to_all | solution.py:40
  36.3 0.7 copy-start.18
  37.2 21.5 %copy-start.11 = (bf16[1,1024,128]{2,1,0:T(8,128)(2,1)}, bf16[1,1024,128]{2,1,0:T(8,128)(2,1)S(1)}, u32[]{:S(2)}) copy-start(bf16[1,1024,128]{2,1,0:T(8,128)(2,1)S(1)} %fusion.44) | copy-start | bytes 786436
  50.4 19.2 %all-to-all-start.2 = ((bf16[128,8,256]{0,2,1:T(8,128)(2,1)}), bf16[128,8,256]{0,2,1:T(8,128)(2,1)}, u32[]{:S(2)}, u32[]{:S(2)}) async-start(bf16[128,8,256]{0,2,1:T(8,128)(2,1)} %bitcast.14), calls=%async_computation.2 | async-start | bytes 1048576 | tf_op jit(solution)/shard_map/all_to_all | solution.py:44
  55.8 0.7 copy-start.19
  56.8 16.1 %copy-start.9 = (bf16[1,2,1024,128]{3,2,1,0:T(8,128)(2,1)}, bf16[1,2,1024,128]{3,2,1,0:T(8,128)(2,1)S(1)}, u32[]{:S(2)}) copy-start(bf16[1,2,1024,128]{3,2,1,0:T(8,128)(2,1)S(1)} %fusion.42) | copy-start | bytes 1572868
  57.3 1.4 copy-start.16
  60.0 13.0 %copy-start.17 = (pred[256,256]{0,1:T(8,128)(4,1)S(1)}, pred[256,256]{0,1:T(8,128)(4,1)}, u32[]{:S(2)}) copy-start(pred[256,256]{0,1:T(8,128)(4,1)} %fusion.53) | copy-start | bytes 196612
  69.5 13.8 %all-to-all-start.3 = ((bf16[128,8,128]{2,0,1:T(8,128)(2,1)}), bf16[128,8,128]{2,0,1:T(8,128)(2,1)S(1)}, u32[]{:S(2)}, u32[]{:S(2)}) async-start(bf16[128,8,128]{2,0,1:T(8,128)(2,1)} %copy.94), calls=%async_computation.3 | async-start | bytes 524288 | tf_op jit(solution)/shard_map/all_to_all | solution.py:42
  85.1 1.0 copy-start.12
  87.4 1.3 copy-start
  89.0 1.1 copy-start.2
  90.1 1.9 copy-start.3
  90.1 1.2 copy-start.10
  91.3 0.7 copy-start.7
  92.7 1.0 copy-start.1
  95.6 14.2 %all-to-all-start.5 = ((bf16[8,128,128]{2,1,0:T(8,128)(2,1)}), bf16[8,128,128]{2,1,0:T(8,128)(2,1)S(1)}, u32[]{:S(2)}, u32[]{:S(2)}) async-start(bf16[8,128,128]{2,1,0:T(8,128)(2,1)} %bitcast.71), calls=%async_computation.5 | async-start | bytes 524288 | tf_op jit(solution)/shard_map/all_to_all | solution.py:128
  101.4 1.0 copy-start.8
  101.4 1.1 copy-start.13
  102.6 1.0 copy-start.4
  103.5 0.9 copy-start.5
  103.6 1.0 copy-start.6
  103.6 1.0 copy-start.20
  109.7 13.8 %all-to-all-start.6 = ((bf16[8,128,128]{2,1,0:T(8,128)(2,1)}), bf16[8,128,128]{2,1,0:T(8,128)(2,1)S(1)}, u32[]{:S(2)}, u32[]{:S(2)}) async-start(bf16[8,128,128]{2,1,0:T(8,128)(2,1)} %bitcast.83), calls=%async_computation.6 | async-start | bytes 524288 | tf_op jit(solution)/shard_map/all_to_all | solution.py:129
  123.5 445.9 %all-to-all-start.4 = ((bf16[8,128,256]{1,2,0:T(8,128)(2,1)}), bf16[8,128,256]{1,2,0:T(8,128)(2,1)S(1)}, u32[]{:S(2)}, u32[]{:S(2)}) async-start(bf16[8,128,256]{1,2,0:T(8,128)(2,1)} %copy.107), calls=%async_computation.4 | async-start | bytes 1048576 | tf_op jit(solution)/shard_map/all_to_all | solution.py:127
  127.0 0.7 copy-start.22
where the time goes:
time: 572 us; the launch traced here: 570 us
  blocking collectives  440 us (77%)
  waiting for transfers between devices  44.6 us (8%)
  starting transfers between devices  40.3 us (7%)
  local copies, waits for them, and re-layouts  21.2 us (4%)
  matrix products  15.5 us (3%)
  other arithmetic  8.02 us (1%)
    psum x1, blocking collectives, on_device(): query_sum, key_sum = lax.psum((query_term, key_term), ('dp', 'seq'))  440 us
    all_to_all x1, starting transfers between devices, on_device(): lax.all_to_all(key_local, 'seq', split_axis=1, concat_axis=0, tiled=True)  16.7 us
    all_to_all x1, waiting for transfers between devices, on_device(): lax.all_to_all(query_local, 'seq', split_axis=1, concat_axis=0, tiled=True)  12.1 us
  transfers between devices with their start and end apart: 8, of which 6 were waited for; matrix products, arithmetic and copies ran while one was open for 5% of the time, Pallas kernels for 0%

commit v1 on v0

--- a/solution.py
+++ b/solution.py
@@ -122,7 +122,12 @@
     value_grad = value_rows.astype(jnp.bfloat16).reshape(total, groups * head_dim)
     query_term = jnp.sum(query_normed_grad * query_unit, axis=(0, 1, 2))
     key_term = jnp.sum(key_normed_grad * key_unit, axis=(0, 1))
-    query_sum, key_sum = lax.psum((query_term, key_term), ("dp", "seq"))
+    pipe_index = lax.axis_index("pipe")
+    slots = jnp.zeros((lax.axis_size("pipe"), 2, head_dim), jnp.float32)
+    slots = lax.dynamic_update_slice(slots, jnp.stack([query_term, key_term])[None], (pipe_index, 0, 0))
+    summed = lax.psum(slots, ("dp", "pipe", "seq"))
+    picked = lax.dynamic_slice(summed, (pipe_index, 0, 0), (1, 2, head_dim))
+    query_sum, key_sum = picked[0, 0], picked[0, 1]
     query_back, key_back, value_back = (
         lax.all_to_all(query_grad, "seq", split_axis=0, concat_axis=1, tiled=True),
         lax.all_to_all(key_grad, "seq", split_axis=0, concat_axis=1, tiled=True),

time: 572 us -> 249 us (0.44)
  the two profiles are of different devices: /device:TPU:2 before, /device:TPU:1 now
where the time goes in v1:
time: 249 us; the launch traced here: 247 us
  blocking collectives  122 us (49%)
  starting transfers between devices  42.5 us (17%)
  waiting for transfers between devices  36.7 us (15%)
  local copies, waits for them, and re-layouts  21.7 us (9%)
  matrix products  15.5 us (6%)
  other arithmetic  8.04 us (3%)
    psum x1, blocking collectives, on_device(): summed = lax.psum(slots, ('dp', 'pipe', 'seq'))  122 us
    all_to_all x1, starting transfers between devices, on_device(): lax.all_to_all(key_local, 'seq', split_axis=1, concat_axis=0, tiled=True)  17.2 us
    all_to_all x1, waiting for transfers between devices, on_device(): lax.all_to_all(query_local, 'seq', split_axis=1, concat_axis=0, tiled=True)  11.2 us
    unnamed x55, local copies, waits for them, and re-layouts  10.7 us
    all_to_all x1, waiting for transfers between devices, on_device(): lax.all_to_all(arrived, 'seq', split_axis=1, concat_axis=0, tiled=True)  8.73 us
    all_to_all x1, waiting for transfers between devices, on_device(): lax.all_to_all(value_grad, 'seq', split_axis=0, concat_axis=1, tiled=True)  7.12 us
    div x4, matrix products, on_device(): weights = exp_scores / jnp.sum(exp_scores, axis=-1, keepdims=True)  5.01 us
  transfers between devices with their start and end apart: 8, of which 6 were waited for; matrix products, arithmetic and copies ran while one was open for 11% of the time, Pallas kernels for 0%

profile of v1, /device:TPU:1, one launch (start us, length us, event | category | flops | bytes accessed | tf_op | source)
XLA Modules:
  0.0 247.2 jit_solution(9559973167658670181)
XLA Ops:
  0.6 1.0 copy.138
  1.7 0.7 copy.90
  2.4 17.2 %all-to-all-start.1 = ((bf16[128,8,128]{2,0,1:T(8,128)(2,1)}), bf16[128,8,128]{2,0,1:T(8,128)(2,1)S(1)}, u32[]{:S(2)}, u32[]{:S(2)}) async-start(bf16[128,8,128]{2,0,1:T(8,128)(2,1)} %copy.90), calls=%async_computation.1 | async-start | bytes 524288 | tf_op jit(solution)/shard_map/all_to_all | solution.py:41
  19.7 2.9 %collective-permute-start = (bf16[128,2048]{1,0:T(8,128)(2,1)S(1)}, bf16[128,2048]{1,0:T(8,128)(2,1)S(1)}, u32[]{:S(2)}, u32[]{:S(2)}) collective-permute-start(bf16[128,2048]{1,0:T(8,128)(2,1)S(1)} %bitcast.347), channel_id=1, source_target_pairs={{0,56},{8,0},{16,8},{24,16},{32,24},{40,32},{48,40},{56,48},{1,57}... | collective-permute-start | bytes 1572872 | tf_op jit(solution)/shard_map/ppermute | solution.py:15
  22.6 0.7 fusion.53
  23.3 1.0 copy.87
  24.3 0.7 copy.94
  25.2 0.8 compare_and_fusion.1
  26.0 4.0 %all-to-all-done.1 = bf16[128,8,128]{2,0,1:T(8,128)(2,1)S(1)} async-done(((bf16[128,8,128]{2,0,1:T(8,128)(2,1)}), bf16[128,8,128]{2,0,1:T(8,128)(2,1)S(1)}, u32[]{:S(2)}, u32[]{:S(2)}) %all-to-all-start.1) | async-done | bytes 262176 | tf_op jit(solution)/shard_map/all_to_all | solution.py:41
  30.0 3.5 %all-to-all-start = ((bf16[128,8,256]{0,2,1:T(8,128)(2,1)}), bf16[128,8,256]{0,2,1:T(8,128)(2,1)S(1)}, u32[]{:S(2)}, u32[]{:S(2)}) async-start(bf16[128,8,256]{0,2,1:T(8,128)(2,1)} %bitcast), calls=%async_computation | async-start | bytes 1048576 | tf_op jit(solution)/shard_map/all_to_all | solution.py:40
  33.5 0.8 compare_and_fusion.2
  34.5 0.8 convert_element_type.175
  35.4 0.7 copy-done.18
  36.2 1.0 copy.91
  37.3 11.2 %all-to-all-done = bf16[128,8,256]{0,2,1:T(8,128)(2,1)S(1)} async-done(((bf16[128,8,256]{0,2,1:T(8,128)(2,1)}), bf16[128,8,256]{0,2,1:T(8,128)(2,1)S(1)}, u32[]{:S(2)}, u32[]{:S(2)}) %all-to-all-start) | async-done | bytes 524320 | tf_op jit(solution)/shard_map/all_to_all | solution.py:40
  48.4 4.1 %all-to-all-start.2 = ((bf16[128,8,256]{0,2,1:T(8,128)(2,1)}), bf16[128,8,256]{0,2,1:T(8,128)(2,1)}, u32[]{:S(2)}, u32[]{:S(2)}) async-start(bf16[128,8,256]{0,2,1:T(8,128)(2,1)} %bitcast.14), calls=%async_computation.2 | async-start | bytes 1048576 | tf_op jit(solution)/shard_map/all_to_all | solution.py:44
  52.7 0.6 copy.88
  53.5 0.3 copy.89
  53.9 0.6 copy-done.19
  54.6 0.3 fusion.42
  54.9 0.4 fusion.46
  55.4 1.3 fusion.48
  56.7 1.3 fusion.50
  58.0 8.7 %all-to-all-done.2 = bf16[128,8,256]{0,2,1:T(8,128)(2,1)} async-done(((bf16[128,8,256]{0,2,1:T(8,128)(2,1)}), bf16[128,8,256]{0,2,1:T(8,128)(2,1)}, u32[]{:S(2)}, u32[]{:S(2)}) %all-to-all-start.2) | async-done | bytes 524320 | tf_op jit(solution)/shard_map/all_to_all | solution.py:44
  66.8 3.4 %all-to-all-start.3 = ((bf16[128,8,128]{2,0,1:T(8,128)(2,1)}), bf16[128,8,128]{2,0,1:T(8,128)(2,1)S(1)}, u32[]{:S(2)}, u32[]{:S(2)}) async-start(bf16[128,8,128]{2,0,1:T(8,128)(2,1)} %copy.94), calls=%async_computation.3 | async-start | bytes 524288 | tf_op jit(solution)/shard_map/all_to_all | solution.py:42
  70.2 2.0 fusion.52
  72.2 1.4 copy.92
  73.5 1.0 reshape.805
  74.6 1.3 copy.93
  75.9 1.3 convolution_bitcast_fusion.14
  77.1 2.3 all-to-all-done.3
  79.4 1.4 fusion.38
  80.8 0.4 fusion.41
  81.5 0.7 copy-done.12
  82.2 1.0 convolution_bitcast_fusion
  83.1 0.4 fusion.40
  83.8 1.0 convolution_bitcast_fusion.2
  84.8 0.4 fusion.39
  85.4 0.8 copy-done.2
  86.4 0.9 copy-done.10
  87.6 0.5 copy-done.7
  88.1 0.3 fusion.37
  89.1 0.7 copy-done.1
  89.9 0.7 multiply_reduce_fusion.3
  90.6 1.0 multiply_convert_fusion.2
  91.6 4.3 %all-to-all-start.5 = ((bf16[8,128,128]{2,1,0:T(8,128)(2,1)}), bf16[8,128,128]{2,1,0:T(8,128)(2,1)S(1)}, u32[]{:S(2)}, u32[]{:S(2)}) async-start(bf16[8,128,128]{2,1,0:T(8,128)(2,1)} %bitcast.71), calls=%async_computation.5 | async-start | bytes 524288 | tf_op jit(solution)/shard_map/all_to_all | solution.py:133
  96.0 1.4 fusion.30
  97.4 0.3 fusion.28
  98.1 0.7 convert_element_type.170
  99.5 0.7 copy-done.4
  100.5 0.7 copy-done.5
  101.2 0.6 multiply_reduce_fusion
  101.9 3.4 %all-to-all-done.5 = bf16[8,128,128]{2,1,0:T(8,128)(2,1)S(1)} async-done(((bf16[8,128,128]{2,1,0:T(8,128)(2,1)}), bf16[8,128,128]{2,1,0:T(8,128)(2,1)S(1)}, u32[]{:S(2)}, u32[]{:S(2)}) %all-to-all-start.5) | async-done | bytes 262176 | tf_op jit(solution)/shard_map/all_to_all | solution.py:133
  105.3 3.6 %all-to-all-start.6 = ((bf16[8,128,128]{2,1,0:T(8,128)(2,1)}), bf16[8,128,128]{2,1,0:T(8,128)(2,1)S(1)}, u32[]{:S(2)}, u32[]{:S(2)}) async-start(bf16[8,128,128]{2,1,0:T(8,128)(2,1)} %bitcast.83), calls=%async_computation.6 | async-start | bytes 524288 | tf_op jit(solution)/shard_map/all_to_all | solution.py:134
  108.9 0.7 multiply_convert_fusion
  109.9 0.9 copy.107
  110.8 7.1 %all-to-all-done.6 = bf16[8,128,128]{2,1,0:T(8,128)(2,1)S(1)} async-done(((bf16[8,128,128]{2,1,0:T(8,128)(2,1)}), bf16[8,128,128]{2,1,0:T(8,128)(2,1)S(1)}, u32[]{:S(2)}, u32[]{:S(2)}) %all-to-all-start.6) | async-done | bytes 262176 | tf_op jit(solution)/shard_map/all_to_all | solution.py:134
  117.9 3.5 %all-to-all-start.4 = ((bf16[8,128,256]{1,2,0:T(8,128)(2,1)}), bf16[8,128,256]{1,2,0:T(8,128)(2,1)S(1)}, u32[]{:S(2)}, u32[]{:S(2)}) async-start(bf16[8,128,256]{1,2,0:T(8,128)(2,1)} %copy.107), calls=%async_computation.4 | async-start | bytes 1048576 | tf_op jit(solution)/shard_map/all_to_all | solution.py:132
  121.5 0.6 copy-done.22
  122.1 121.6 %psum.7 = f32[8,2,128]{2,1,0:T(2,128)S(1)} all-reduce(f32[8,2,128]{2,1,0:T(2,128)S(1)} %constant_dynamic-update-slice_fusion), channel_id=1, replica_groups=mesh['dp'=16,'pipe'=8,'seq'=8] {'dp','pipe','seq'}, use_global_device_ids=true, to_apply=%region_14.15 | all-reduce | flops 2048 | bytes 16384 | tf_op jit(solution)/shard_map/psum | solution.py:128
  243.7 0.5 slice_bitcast_fusion.52
  244.4 0.8 reshape.825
  245.4 0.8 reshape.830
  246.2 1.0 copy.116
  (79 shorter events, 5.1 us)
Async XLA Ops:
  1.6 18.0 %copy-start.23 = (bf16[1,1,128,2048]{3,2,1,0:T(8,128)(2,1)S(1)}, bf16[1,1,128,2048]{3,2,1,0:T(8,128)(2,1)}, u32[]{:S(2)}) copy-start(bf16[1,1,128,2048]{3,2,1,0:T(8,128)(2,1)} %param.26) | copy-start | bytes 1572868
  1.6 21.6 %copy-start.14 = (bf16[1,1,128,2048]{3,2,1,0:T(8,128)(2,1)S(1)}, bf16[1,1,128,2048]{3,2,1,0:T(8,128)(2,1)}, u32[]{:S(2)}) copy-start(bf16[1,1,128,2048]{3,2,1,0:T(8,128)(2,1)} %param.23) | copy-start | bytes 1572868
  2.4 27.6 %all-to-all-start.1 = ((bf16[128,8,128]{2,0,1:T(8,128)(2,1)}), bf16[128,8,128]{2,0,1:T(8,128)(2,1)S(1)}, u32[]{:S(2)}, u32[]{:S(2)}) async-start(bf16[128,8,128]{2,0,1:T(8,128)(2,1)} %copy.90), calls=%async_computation.1 | async-start | bytes 524288 | tf_op jit(solution)/shard_map/all_to_all | solution.py:41
  19.6 2.9 %copy-start.21 = (s32[1,1,1024]{2,1,0:T(1,128)S(1)}, s32[1,1,1024]{2,1,0:T(1,128)}, u32[]{:S(2)}) copy-start(s32[1,1,1024]{2,1,0:T(1,128)} %param.27) | copy-start | bytes 12292
  19.7 16.6 %collective-permute-start = (bf16[128,2048]{1,0:T(8,128)(2,1)S(1)}, bf16[128,2048]{1,0:T(8,128)(2,1)S(1)}, u32[]{:S(2)}, u32[]{:S(2)}) collective-permute-start(bf16[128,2048]{1,0:T(8,128)(2,1)S(1)} %bitcast.347), channel_id=1, source_target_pairs={{0,56},{8,0},{16,8},{24,16},{32,24},{40,32},{48,40},{56,48},{1,57}... | collective-permute-start | bytes 1572872 | tf_op jit(solution)/shard_map/ppermute | solution.py:15
  23.3 1.0 copy-start.15
  30.0 18.4 %all-to-all-start = ((bf16[128,8,256]{0,2,1:T(8,128)(2,1)}), bf16[128,8,256]{0,2,1:T(8,128)(2,1)S(1)}, u32[]{:S(2)}, u32[]{:S(2)}) async-start(bf16[128,8,256]{0,2,1:T(8,128)(2,1)} %bitcast), calls=%async_computation | async-start | bytes 1048576 | tf_op jit(solution)/shard_map/all_to_all | solution.py:40
  35.4 0.7 copy-start.18
  36.2 20.5 %copy-start.11 = (bf16[1,1024,128]{2,1,0:T(8,128)(2,1)}, bf16[1,1024,128]{2,1,0:T(8,128)(2,1)S(1)}, u32[]{:S(2)}) copy-start(bf16[1,1024,128]{2,1,0:T(8,128)(2,1)S(1)} %fusion.44) | copy-start | bytes 786436
  48.4 18.3 %all-to-all-start.2 = ((bf16[128,8,256]{0,2,1:T(8,128)(2,1)}), bf16[128,8,256]{0,2,1:T(8,128)(2,1)}, u32[]{:S(2)}, u32[]{:S(2)}) async-start(bf16[128,8,256]{0,2,1:T(8,128)(2,1)} %bitcast.14), calls=%async_computation.2 | async-start | bytes 1048576 | tf_op jit(solution)/shard_map/all_to_all | solution.py:44
  53.9 0.7 copy-start.19
  54.9 15.3 %copy-start.9 = (bf16[1,2,1024,128]{3,2,1,0:T(8,128)(2,1)}, bf16[1,2,1024,128]{3,2,1,0:T(8,128)(2,1)S(1)}, u32[]{:S(2)}) copy-start(bf16[1,2,1024,128]{3,2,1,0:T(8,128)(2,1)S(1)} %fusion.42) | copy-start | bytes 1572868
  55.4 1.4 copy-start.16
  58.0 12.2 %copy-start.17 = (pred[256,256]{0,1:T(8,128)(4,1)S(1)}, pred[256,256]{0,1:T(8,128)(4,1)}, u32[]{:S(2)}) copy-start(pred[256,256]{0,1:T(8,128)(4,1)} %fusion.53) | copy-start | bytes 196612
  66.8 12.7 %all-to-all-start.3 = ((bf16[128,8,128]{2,0,1:T(8,128)(2,1)}), bf16[128,8,128]{2,0,1:T(8,128)(2,1)S(1)}, u32[]{:S(2)}, u32[]{:S(2)}) async-start(bf16[128,8,128]{2,0,1:T(8,128)(2,1)} %copy.94), calls=%async_computation.3 | async-start | bytes 524288 | tf_op jit(solution)/shard_map/all_to_all | solution.py:42
  81.2 1.0 copy-start.12
  83.5 1.3 copy-start
  85.1 1.1 copy-start.2
  86.2 1.9 copy-start.3
  86.2 1.2 copy-start.10
  87.4 0.7 copy-start.7
  88.8 1.0 copy-start.1
  91.6 13.6 %all-to-all-start.5 = ((bf16[8,128,128]{2,1,0:T(8,128)(2,1)}), bf16[8,128,128]{2,1,0:T(8,128)(2,1)S(1)}, u32[]{:S(2)}, u32[]{:S(2)}) async-start(bf16[8,128,128]{2,1,0:T(8,128)(2,1)} %bitcast.71), calls=%async_computation.5 | async-start | bytes 524288 | tf_op jit(solution)/shard_map/all_to_all | solution.py:133
  98.1 1.0 copy-start.8
  98.1 1.1 copy-start.13
  99.2 1.0 copy-start.4
  100.2 0.9 copy-start.5
  100.2 1.0 copy-start.6
  100.2 1.0 copy-start.20
  105.3 12.7 %all-to-all-start.6 = ((bf16[8,128,128]{2,1,0:T(8,128)(2,1)}), bf16[8,128,128]{2,1,0:T(8,128)(2,1)S(1)}, u32[]{:S(2)}, u32[]{:S(2)}) async-start(bf16[8,128,128]{2,1,0:T(8,128)(2,1)} %bitcast.83), calls=%async_computation.6 | async-start | bytes 524288 | tf_op jit(solution)/shard_map/all_to_all | solution.py:134
  117.9 128.3 %all-to-all-start.4 = ((bf16[8,128,256]{1,2,0:T(8,128)(2,1)}), bf16[8,128,256]{1,2,0:T(8,128)(2,1)S(1)}, u32[]{:S(2)}, u32[]{:S(2)}) async-start(bf16[8,128,256]{1,2,0:T(8,128)(2,1)} %copy.107), calls=%async_computation.4 | async-start | bytes 1048576 | tf_op jit(solution)/shard_map/all_to_all | solution.py:132
  121.4 0.7 copy-start.22

commit v2 on v0

--- a/solution.py
+++ b/solution.py
@@ -13,6 +13,16 @@
 def passed_along(x, axis, by):
     devices = lax.axis_size(axis)
     return lax.ppermute(x, axis, [(i, (i + by) % devices) for i in range(devices)])
+
+
+def summed_over(x, axes):
+    for axis in axes:
+        devices = lax.axis_size(axis)
+        step = 1
+        while step < devices:
+            x = x + lax.ppermute(x, axis, [(i, i ^ step) for i in range(devices)])
+            step *= 2
+    return x
 
 
 def normalize(values, gain):
@@ -122,7 +132,8 @@
     value_grad = value_rows.astype(jnp.bfloat16).reshape(total, groups * head_dim)
     query_term = jnp.sum(query_normed_grad * query_unit, axis=(0, 1, 2))
     key_term = jnp.sum(key_normed_grad * key_unit, axis=(0, 1))
-    query_sum, key_sum = lax.psum((query_term, key_term), ("dp", "seq"))
+    both = summed_over(jnp.stack([query_term, key_term]), ("seq", "dp"))
+    query_sum, key_sum = both[0], both[1]
     query_back, key_back, value_back = (
         lax.all_to_all(query_grad, "seq", split_axis=0, concat_axis=1, tiled=True),
         lax.all_to_all(key_grad, "seq", split_axis=0, concat_axis=1, tiled=True),

time: 572 us -> 188 us (0.33)
  blocking collectives: 440 us -> 0 us
  starting transfers between devices: 40.3 us -> 74.7 us
  waiting for transfers between devices: 44.6 us -> 66 us
    psum x1 -> x0, blocking collectives: 440 us -> none  [on_device(): query_sum, key_sum = lax.psum((query_term, key_term), ('dp', 'seq'))]
    ppermute x0 -> x7, starting transfers between devices: none -> 34.4 us  [summed_over(): x = x + lax.ppermute(x, axis, [(i, i ^ step) for i in range(devices)])]
    ppermute x0 -> x7, waiting for transfers between devices: none -> 21.4 us  [summed_over(): x = x + lax.ppermute(x, axis, [(i, i ^ step) for i in range(devices)])]
  transfers between devices with their start and end apart: 8 -> 15, of which waited for: 6 -> 13; matrix products, arithmetic and copies ran while one was open for 5% -> 14% of each run, Pallas kernels for 0% -> 0%
where the time goes in v2:
time: 188 us; the launch traced here: 186 us
  starting transfers between devices  74.7 us (40%)
  waiting for transfers between devices  66 us (35%)
  local copies, waits for them, and re-layouts  21 us (11%)
  matrix products  15.5 us (8%)
  other arithmetic  7.73 us (4%)
    ppermute x7, starting transfers between devices, summed_over(): x = x + lax.ppermute(x, axis, [(i, i ^ step) for i in range(devices)])  34.4 us
    ppermute x7, waiting for transfers between devices, summed_over(): x = x + lax.ppermute(x, axis, [(i, i ^ step) for i in range(devices)])  21.4 us
    all_to_all x1, starting transfers between devices, on_device(): lax.all_to_all(key_local, 'seq', split_axis=1, concat_axis=0, tiled=True)  16.7 us
    all_to_all x1, waiting for transfers between devices, on_device(): lax.all_to_all(query_local, 'seq', split_axis=1, concat_axis=0, tiled=True)  12.1 us
    unnamed x55, local copies, waits for them, and re-layouts  10 us
    all_to_all x1, waiting for transfers between devices, on_device(): lax.all_to_all(arrived, 'seq', split_axis=1, concat_axis=0, tiled=True)  9.57 us
    all_to_all x1, waiting for transfers between devices, on_device(): lax.all_to_all(value_grad, 'seq', split_axis=0, concat_axis=1, tiled=True)  8.44 us
    all_to_all x1, waiting for transfers between devices, on_device(): lax.all_to_all(key_local, 'seq', split_axis=1, concat_axis=0, tiled=True)  6.44 us
  transfers between devices with their start and end apart: 15, of which 13 were waited for; matrix products, arithmetic and copies ran while one was open for 14% of the time, Pallas kernels for 0%

profile of v2, /device:TPU:2, one launch (start us, length us, event | category | flops | bytes accessed | tf_op | source)
XLA Modules:
  0.0 186.1 jit_solution(11445762062016094654)
XLA Ops:
  0.6 1.0 copy.138
  1.7 0.7 copy.90
  2.4 16.7 %all-to-all-start.1 = ((bf16[128,8,128]{2,0,1:T(8,128)(2,1)}), bf16[128,8,128]{2,0,1:T(8,128)(2,1)S(1)}, u32[]{:S(2)}, u32[]{:S(2)}) async-start(bf16[128,8,128]{2,0,1:T(8,128)(2,1)} %copy.90), calls=%async_computation.1 | async-start | bytes 524288 | tf_op jit(solution)/shard_map/all_to_all | solution.py:51
  19.1 1.9 %collective-permute-start = (bf16[128,2048]{1,0:T(8,128)(2,1)S(1)}, bf16[128,2048]{1,0:T(8,128)(2,1)S(1)}, u32[]{:S(2)}, u32[]{:S(2)}) collective-permute-start(bf16[128,2048]{1,0:T(8,128)(2,1)S(1)} %bitcast.343), channel_id=1, source_target_pairs={{0,56},{8,0},{16,8},{24,16},{32,24},{40,32},{48,40},{56,48},{1,57}... | collective-permute-start | bytes 1572872 | tf_op jit(solution)/shard_map/ppermute | solution.py:15
  21.1 0.7 fusion.53
  21.8 1.0 copy.87
  22.8 0.7 copy.94
  23.7 0.8 compare_and_fusion.1
  24.5 6.4 %all-to-all-done.1 = bf16[128,8,128]{2,0,1:T(8,128)(2,1)S(1)} async-done(((bf16[128,8,128]{2,0,1:T(8,128)(2,1)}), bf16[128,8,128]{2,0,1:T(8,128)(2,1)S(1)}, u32[]{:S(2)}, u32[]{:S(2)}) %all-to-all-start.1) | async-done | bytes 262176 | tf_op jit(solution)/shard_map/all_to_all | solution.py:51
  31.0 3.5 %all-to-all-start = ((bf16[128,8,256]{0,2,1:T(8,128)(2,1)}), bf16[128,8,256]{0,2,1:T(8,128)(2,1)S(1)}, u32[]{:S(2)}, u32[]{:S(2)}) async-start(bf16[128,8,256]{0,2,1:T(8,128)(2,1)} %bitcast), calls=%async_computation | async-start | bytes 1048576 | tf_op jit(solution)/shard_map/all_to_all | solution.py:50
  34.5 0.8 compare_and_fusion.2
  35.5 0.8 convert_element_type.175
  36.3 0.7 copy-done.18
  37.2 1.0 copy.91
  38.2 12.1 %all-to-all-done = bf16[128,8,256]{0,2,1:T(8,128)(2,1)S(1)} async-done(((bf16[128,8,256]{0,2,1:T(8,128)(2,1)}), bf16[128,8,256]{0,2,1:T(8,128)(2,1)S(1)}, u32[]{:S(2)}, u32[]{:S(2)}) %all-to-all-start) | async-done | bytes 524320 | tf_op jit(solution)/shard_map/all_to_all | solution.py:50
  50.4 4.1 %all-to-all-start.2 = ((bf16[128,8,256]{0,2,1:T(8,128)(2,1)}), bf16[128,8,256]{0,2,1:T(8,128)(2,1)}, u32[]{:S(2)}, u32[]{:S(2)}) async-start(bf16[128,8,256]{0,2,1:T(8,128)(2,1)} %bitcast.14), calls=%async_computation.2 | async-start | bytes 1048576 | tf_op jit(solution)/shard_map/all_to_all | solution.py:54
  55.9 0.6 copy-done.20
  57.3 1.3 fusion.48
  58.7 1.3 fusion.50
  60.0 9.6 %all-to-all-done.2 = bf16[128,8,256]{0,2,1:T(8,128)(2,1)} async-done(((bf16[128,8,256]{0,2,1:T(8,128)(2,1)}), bf16[128,8,256]{0,2,1:T(8,128)(2,1)}, u32[]{:S(2)}, u32[]{:S(2)}) %all-to-all-start.2) | async-done | bytes 524320 | tf_op jit(solution)/shard_map/all_to_all | solution.py:54
  69.5 3.4 %all-to-all-start.3 = ((bf16[128,8,128]{2,0,1:T(8,128)(2,1)}), bf16[128,8,128]{2,0,1:T(8,128)(2,1)S(1)}, u32[]{:S(2)}, u32[]{:S(2)}) async-start(bf16[128,8,128]{2,0,1:T(8,128)(2,1)} %copy.94), calls=%async_computation.3 | async-start | bytes 524288 | tf_op jit(solution)/shard_map/all_to_all | solution.py:52
  73.0 2.0 %fusion.52 = f32[2,256,256]{1,2,0:T(8,128)} fusion(pred[256,256]{0,1:T(8,128)(4,1)S(1)} %copy-done.17, bf16[1,2,1024,128]{3,2,1,0:T(8,128)(2,1)S(1)} %fusion.42, bf16[1,1024,128]{2,1,0:T(8,128)(2,1)} %copy-done.11), kind=kOutput, calls=%fused_computation.92 | convolution fusion | flops 33948416 | bytes 786432 | tf_op jit(solution)/shard_map/div | solution.py:94
  74.9 1.4 copy.92
  76.3 1.0 reshape.805
  77.3 1.3 copy.93
  78.6 1.3 convolution_bitcast_fusion.14
  79.9 3.4 %all-to-all-done.3 = bf16[128,8,128]{2,0,1:T(8,128)(2,1)S(1)} async-done(((bf16[128,8,128]{2,0,1:T(8,128)(2,1)}), bf16[128,8,128]{2,0,1:T(8,128)(2,1)S(1)}, u32[]{:S(2)}, u32[]{:S(2)}) %all-to-all-start.3) | async-done | bytes 262176 | tf_op jit(solution)/shard_map/all_to_all | solution.py:52
  83.3 1.4 fusion.38
  85.4 0.7 copy-done.12
  86.1 1.0 convolution_bitcast_fusion
  87.7 1.0 convolution_bitcast_fusion.2
  89.3 0.8 copy-done.2
  90.3 0.9 copy-done.10
  93.0 0.7 copy-done.1
  94.1 1.0 multiply_convert_fusion.2
  95.2 3.7 %all-to-all-start.5 = ((bf16[8,128,128]{2,1,0:T(8,128)(2,1)}), bf16[8,128,128]{2,1,0:T(8,128)(2,1)S(1)}, u32[]{:S(2)}, u32[]{:S(2)}) async-start(bf16[8,128,128]{2,1,0:T(8,128)(2,1)} %bitcast.71), calls=%async_computation.5 | async-start | bytes 524288 | tf_op jit(solution)/shard_map/all_to_all | solution.py:139
  98.9 1.4 fusion.30
  101.0 0.7 convert_element_type.170
  102.4 0.7 copy-done.4
  103.4 0.7 copy-done.5
  104.2 0.6 multiply_reduce_fusion
  104.8 4.5 %all-to-all-done.5 = bf16[8,128,128]{2,1,0:T(8,128)(2,1)S(1)} async-done(((bf16[8,128,128]{2,1,0:T(8,128)(2,1)}), bf16[8,128,128]{2,1,0:T(8,128)(2,1)S(1)}, u32[]{:S(2)}, u32[]{:S(2)}) %all-to-all-start.5) | async-done | bytes 262176 | tf_op jit(solution)/shard_map/all_to_all | solution.py:139
  109.3 3.4 %all-to-all-start.6 = ((bf16[8,128,128]{2,1,0:T(8,128)(2,1)}), bf16[8,128,128]{2,1,0:T(8,128)(2,1)S(1)}, u32[]{:S(2)}, u32[]{:S(2)}) async-start(bf16[8,128,128]{2,1,0:T(8,128)(2,1)} %bitcast.83), calls=%async_computation.6 | async-start | bytes 524288 | tf_op jit(solution)/shard_map/all_to_all | solution.py:140
  112.8 0.7 multiply_convert_fusion
  113.8 0.9 copy.107
  114.7 8.4 %all-to-all-done.6 = bf16[8,128,128]{2,1,0:T(8,128)(2,1)S(1)} async-done(((bf16[8,128,128]{2,1,0:T(8,128)(2,1)}), bf16[8,128,128]{2,1,0:T(8,128)(2,1)S(1)}, u32[]{:S(2)}, u32[]{:S(2)}) %all-to-all-start.6) | async-done | bytes 262176 | tf_op jit(solution)/shard_map/all_to_all | solution.py:140
  123.1 3.5 %all-to-all-start.4 = ((bf16[8,128,256]{1,2,0:T(8,128)(2,1)}), bf16[8,128,256]{1,2,0:T(8,128)(2,1)S(1)}, u32[]{:S(2)}, u32[]{:S(2)}) async-start(bf16[8,128,256]{1,2,0:T(8,128)(2,1)} %copy.107), calls=%async_computation.4 | async-start | bytes 1048576 | tf_op jit(solution)/shard_map/all_to_all | solution.py:138
  126.7 3.8 %collective-permute-start.1 = (f32[2,128]{1,0:T(2,128)S(1)}, f32[2,128]{1,0:T(2,128)S(1)}, u32[]{:S(2)}, u32[]{:S(2)}) collective-permute-start(f32[2,128]{1,0:T(2,128)S(1)} %pad_maximum_fusion), channel_id=1, source_target_pairs={{0,1},{1,0},{2,3},{3,2},{4,5},{5,4},{6,7},{7,6},{8,9},{9,8},{10,11... | collective-permute-start | bytes 3080 | tf_op jit(solution)/shard_map/ppermute | solution.py:23
  130.5 5.5 %collective-permute-done.1 = f32[2,128]{1,0:T(2,128)S(1)} collective-permute-done((f32[2,128]{1,0:T(2,128)S(1)}, f32[2,128]{1,0:T(2,128)S(1)}, u32[]{:S(2)}, u32[]{:S(2)}) %collective-permute-start.1) | collective-permute-done | bytes 1056 | tf_op jit(solution)/shard_map/ppermute | solution.py:23
  135.9 2.1 %collective-permute-start.2 = (f32[2,128]{1,0:T(2,128)S(1)}, f32[2,128]{1,0:T(2,128)S(1)}, u32[]{:S(2)}, u32[]{:S(2)}) collective-permute-start(f32[2,128]{1,0:T(2,128)S(1)} %fusion.90), channel_id=1, source_target_pairs={{0,2},{1,3},{2,0},{3,1},{4,6},{5,7},{6,4},{7,5},{8,10},{9,11},{10,... | collective-permute-start | bytes 3080 | tf_op jit(solution)/shard_map/ppermute | solution.py:23
  138.1 4.2 %collective-permute-done.2 = f32[2,128]{1,0:T(2,128)S(1)} collective-permute-done((f32[2,128]{1,0:T(2,128)S(1)}, f32[2,128]{1,0:T(2,128)S(1)}, u32[]{:S(2)}, u32[]{:S(2)}) %collective-permute-start.2) | collective-permute-done | bytes 1056 | tf_op jit(solution)/shard_map/ppermute | solution.py:23
  142.3 5.5 %collective-permute-start.3 = (f32[2,128]{1,0:T(2,128)S(1)}, f32[2,128]{1,0:T(2,128)S(1)}, u32[]{:S(2)}, u32[]{:S(2)}) collective-permute-start(f32[2,128]{1,0:T(2,128)S(1)} %fusion.101), channel_id=1, source_target_pairs={{0,4},{1,5},{2,6},{3,7},{4,0},{5,1},{6,2},{7,3},{8,12},{9,13},{10,... | collective-permute-start | bytes 3080 | tf_op jit(solution)/shard_map/ppermute | solution.py:23
  147.8 3.9 %collective-permute-done.3 = f32[2,128]{1,0:T(2,128)S(1)} collective-permute-done((f32[2,128]{1,0:T(2,128)S(1)}, f32[2,128]{1,0:T(2,128)S(1)}, u32[]{:S(2)}, u32[]{:S(2)}) %collective-permute-start.3) | collective-permute-done | bytes 1056 | tf_op jit(solution)/shard_map/ppermute | solution.py:23
  151.7 6.5 %collective-permute-start.4 = (f32[2,128]{1,0:T(2,128)S(1)}, f32[2,128]{1,0:T(2,128)S(1)}, u32[]{:S(2)}, u32[]{:S(2)}) collective-permute-start(f32[2,128]{1,0:T(2,128)S(1)} %add.190), channel_id=1, source_target_pairs={{0,64},{64,0},{128,192},{192,128},{256,320},{320,256},{384,448},{4... | collective-permute-start | bytes 3080 | tf_op jit(solution)/shard_map/ppermute | solution.py:23
  158.2 2.9 %collective-permute-done.4 = f32[2,128]{1,0:T(2,128)S(1)} collective-permute-done((f32[2,128]{1,0:T(2,128)S(1)}, f32[2,128]{1,0:T(2,128)S(1)}, u32[]{:S(2)}, u32[]{:S(2)}) %collective-permute-start.4) | collective-permute-done | bytes 1056 | tf_op jit(solution)/shard_map/ppermute | solution.py:23
  161.1 3.6 %collective-permute-start.5 = (f32[2,128]{1,0:T(2,128)S(1)}, f32[2,128]{1,0:T(2,128)S(1)}, u32[]{:S(2)}, u32[]{:S(2)}) collective-permute-start(f32[2,128]{1,0:T(2,128)S(1)} %add.191), channel_id=1, source_target_pairs={{0,128},{64,192},{128,0},{192,64},{256,384},{320,448},{384,256},{4... | collective-permute-start | bytes 3080 | tf_op jit(solution)/shard_map/ppermute | solution.py:23
  164.7 1.8 collective-permute-done.5
  166.5 4.7 %collective-permute-start.6 = (f32[2,128]{1,0:T(2,128)S(1)}, f32[2,128]{1,0:T(2,128)S(1)}, u32[]{:S(2)}, u32[]{:S(2)}) collective-permute-start(f32[2,128]{1,0:T(2,128)S(1)} %add.192), channel_id=1, source_target_pairs={{0,256},{64,320},{128,384},{192,448},{256,0},{320,64},{384,128},{4... | collective-permute-start | bytes 3080 | tf_op jit(solution)/shard_map/ppermute | solution.py:23
  171.2 1.6 collective-permute-done.6
  172.9 8.2 %collective-permute-start.7 = (f32[2,128]{1,0:T(2,128)S(1)}, f32[2,128]{1,0:T(2,128)S(1)}, u32[]{:S(2)}, u32[]{:S(2)}) collective-permute-start(f32[2,128]{1,0:T(2,128)S(1)} %add.193), channel_id=1, source_target_pairs={{0,512},{64,576},{128,640},{192,704},{256,768},{320,832},{384,896}... | collective-permute-start | bytes 3080 | tf_op jit(solution)/shard_map/ppermute | solution.py:23
  181.1 1.5 collective-permute-done.7
  183.3 0.8 reshape.825
  184.3 0.8 reshape.830
  185.1 1.0 copy.116
  (97 shorter events, 9.8 us)
Async XLA Ops:
  1.6 17.5 %copy-start.23 = (bf16[1,1,128,2048]{3,2,1,0:T(8,128)(2,1)S(1)}, bf16[1,1,128,2048]{3,2,1,0:T(8,128)(2,1)}, u32[]{:S(2)}) copy-start(bf16[1,1,128,2048]{3,2,1,0:T(8,128)(2,1)} %param.26) | copy-start | bytes 1572868
  1.6 20.1 %copy-start.14 = (bf16[1,1,128,2048]{3,2,1,0:T(8,128)(2,1)S(1)}, bf16[1,1,128,2048]{3,2,1,0:T(8,128)(2,1)}, u32[]{:S(2)}) copy-start(bf16[1,1,128,2048]{3,2,1,0:T(8,128)(2,1)} %param.23) | copy-start | bytes 1572868
  2.4 28.6 %all-to-all-start.1 = ((bf16[128,8,128]{2,0,1:T(8,128)(2,1)}), bf16[128,8,128]{2,0,1:T(8,128)(2,1)S(1)}, u32[]{:S(2)}, u32[]{:S(2)}) async-start(bf16[128,8,128]{2,0,1:T(8,128)(2,1)} %copy.90), calls=%async_computation.1 | async-start | bytes 524288 | tf_op jit(solution)/shard_map/all_to_all | solution.py:51
  19.1 2.0 %copy-start.22 = (s32[1,1,1024]{2,1,0:T(1,128)S(1)}, s32[1,1,1024]{2,1,0:T(1,128)}, u32[]{:S(2)}) copy-start(s32[1,1,1024]{2,1,0:T(1,128)} %param.27) | copy-start | bytes 12292
  19.1 18.1 %collective-permute-start = (bf16[128,2048]{1,0:T(8,128)(2,1)S(1)}, bf16[128,2048]{1,0:T(8,128)(2,1)S(1)}, u32[]{:S(2)}, u32[]{:S(2)}) collective-permute-start(bf16[128,2048]{1,0:T(8,128)(2,1)S(1)} %bitcast.343), channel_id=1, source_target_pairs={{0,56},{8,0},{16,8},{24,16},{32,24},{40,32},{48,40},{56,48},{1,57}... | collective-permute-start | bytes 1572872 | tf_op jit(solution)/shard_map/ppermute | solution.py:15
  21.8 1.0 copy-start.15
  31.0 19.4 %all-to-all-start = ((bf16[128,8,256]{0,2,1:T(8,128)(2,1)}), bf16[128,8,256]{0,2,1:T(8,128)(2,1)S(1)}, u32[]{:S(2)}, u32[]{:S(2)}) async-start(bf16[128,8,256]{0,2,1:T(8,128)(2,1)} %bitcast), calls=%async_computation | async-start | bytes 1048576 | tf_op jit(solution)/shard_map/all_to_all | solution.py:50
  36.3 0.7 copy-start.18
  37.2 21.4 %copy-start.11 = (bf16[1,1024,128]{2,1,0:T(8,128)(2,1)}, bf16[1,1024,128]{2,1,0:T(8,128)(2,1)S(1)}, u32[]{:S(2)}) copy-start(bf16[1,1024,128]{2,1,0:T(8,128)(2,1)S(1)} %fusion.44) | copy-start | bytes 786436
  50.4 19.2 %all-to-all-start.2 = ((bf16[128,8,256]{0,2,1:T(8,128)(2,1)}), bf16[128,8,256]{0,2,1:T(8,128)(2,1)}, u32[]{:S(2)}, u32[]{:S(2)}) async-start(bf16[128,8,256]{0,2,1:T(8,128)(2,1)} %bitcast.14), calls=%async_computation.2 | async-start | bytes 1048576 | tf_op jit(solution)/shard_map/all_to_all | solution.py:54
  55.8 0.7 copy-start.20
  56.8 16.1 %copy-start.9 = (bf16[1,2,1024,128]{3,2,1,0:T(8,128)(2,1)}, bf16[1,2,1024,128]{3,2,1,0:T(8,128)(2,1)S(1)}, u32[]{:S(2)}) copy-start(bf16[1,2,1024,128]{3,2,1,0:T(8,128)(2,1)S(1)} %fusion.42) | copy-start | bytes 1572868
  57.3 1.4 copy-start.16
  60.0 13.0 %copy-start.17 = (pred[256,256]{0,1:T(8,128)(4,1)S(1)}, pred[256,256]{0,1:T(8,128)(4,1)}, u32[]{:S(2)}) copy-start(pred[256,256]{0,1:T(8,128)(4,1)} %fusion.53) | copy-start | bytes 196612
  69.5 13.8 %all-to-all-start.3 = ((bf16[128,8,128]{2,0,1:T(8,128)(2,1)}), bf16[128,8,128]{2,0,1:T(8,128)(2,1)S(1)}, u32[]{:S(2)}, u32[]{:S(2)}) async-start(bf16[128,8,128]{2,0,1:T(8,128)(2,1)} %copy.94), calls=%async_computation.3 | async-start | bytes 524288 | tf_op jit(solution)/shard_map/all_to_all | solution.py:52
  85.1 1.0 copy-start.12
  87.4 1.3 copy-start
  89.0 1.1 copy-start.2
  90.1 1.9 %copy-start.3 = (bf16[2,256,384]{2,1,0:T(8,128)(2,1)}, bf16[2,256,384]{2,1,0:T(8,128)(2,1)S(1)}, u32[]{:S(2)}) copy-start(bf16[2,256,384]{2,1,0:T(8,128)(2,1)S(1)} %fusion.12) | copy-start | bytes 1179652
  90.1 1.2 copy-start.10
  91.3 0.7 copy-start.7
  92.7 1.0 copy-start.1
  93.0 0.7 copy-start.19
  95.2 14.2 %all-to-all-start.5 = ((bf16[8,128,128]{2,1,0:T(8,128)(2,1)}), bf16[8,128,128]{2,1,0:T(8,128)(2,1)S(1)}, u32[]{:S(2)}, u32[]{:S(2)}) async-start(bf16[8,128,128]{2,1,0:T(8,128)(2,1)} %bitcast.71), calls=%async_computation.5 | async-start | bytes 524288 | tf_op jit(solution)/shard_map/all_to_all | solution.py:139
  101.0 1.0 copy-start.8
  101.0 1.1 copy-start.13
  102.2 1.0 copy-start.4
  103.1 0.9 copy-start.5
  103.1 1.0 copy-start.6
  103.2 1.0 copy-start.21
  109.3 13.8 %all-to-all-start.6 = ((bf16[8,128,128]{2,1,0:T(8,128)(2,1)}), bf16[8,128,128]{2,1,0:T(8,128)(2,1)S(1)}, u32[]{:S(2)}, u32[]{:S(2)}) async-start(bf16[8,128,128]{2,1,0:T(8,128)(2,1)} %bitcast.83), calls=%async_computation.6 | async-start | bytes 524288 | tf_op jit(solution)/shard_map/all_to_all | solution.py:140
  123.1 62.0 %all-to-all-start.4 = ((bf16[8,128,256]{1,2,0:T(8,128)(2,1)}), bf16[8,128,256]{1,2,0:T(8,128)(2,1)S(1)}, u32[]{:S(2)}, u32[]{:S(2)}) async-start(bf16[8,128,256]{1,2,0:T(8,128)(2,1)} %copy.107), calls=%async_computation.4 | async-start | bytes 1048576 | tf_op jit(solution)/shard_map/all_to_all | solution.py:138
  126.7 9.3 %collective-permute-start.1 = (f32[2,128]{1,0:T(2,128)S(1)}, f32[2,128]{1,0:T(2,128)S(1)}, u32[]{:S(2)}, u32[]{:S(2)}) collective-permute-start(f32[2,128]{1,0:T(2,128)S(1)} %pad_maximum_fusion), channel_id=1, source_target_pairs={{0,1},{1,0},{2,3},{3,2},{4,5},{5,4},{6,7},{7,6},{8,9},{9,8},{10,11... | collective-permute-start | bytes 3080 | tf_op jit(solution)/shard_map/ppermute | solution.py:23
  135.9 6.4 %collective-permute-start.2 = (f32[2,128]{1,0:T(2,128)S(1)}, f32[2,128]{1,0:T(2,128)S(1)}, u32[]{:S(2)}, u32[]{:S(2)}) collective-permute-start(f32[2,128]{1,0:T(2,128)S(1)} %fusion.90), channel_id=1, source_target_pairs={{0,2},{1,3},{2,0},{3,1},{4,6},{5,7},{6,4},{7,5},{8,10},{9,11},{10,... | collective-permute-start | bytes 3080 | tf_op jit(solution)/shard_map/ppermute | solution.py:23
  142.3 9.4 %collective-permute-start.3 = (f32[2,128]{1,0:T(2,128)S(1)}, f32[2,128]{1,0:T(2,128)S(1)}, u32[]{:S(2)}, u32[]{:S(2)}) collective-permute-start(f32[2,128]{1,0:T(2,128)S(1)} %fusion.101), channel_id=1, source_target_pairs={{0,4},{1,5},{2,6},{3,7},{4,0},{5,1},{6,2},{7,3},{8,12},{9,13},{10,... | collective-permute-start | bytes 3080 | tf_op jit(solution)/shard_map/ppermute | solution.py:23
  151.7 9.4 %collective-permute-start.4 = (f32[2,128]{1,0:T(2,128)S(1)}, f32[2,128]{1,0:T(2,128)S(1)}, u32[]{:S(2)}, u32[]{:S(2)}) collective-permute-start(f32[2,128]{1,0:T(2,128)S(1)} %add.190), channel_id=1, source_target_pairs={{0,64},{64,0},{128,192},{192,128},{256,320},{320,256},{384,448},{4... | collective-permute-start | bytes 3080 | tf_op jit(solution)/shard_map/ppermute | solution.py:23
  161.1 5.5 %collective-permute-start.5 = (f32[2,128]{1,0:T(2,128)S(1)}, f32[2,128]{1,0:T(2,128)S(1)}, u32[]{:S(2)}, u32[]{:S(2)}) collective-permute-start(f32[2,128]{1,0:T(2,128)S(1)} %add.191), channel_id=1, source_target_pairs={{0,128},{64,192},{128,0},{192,64},{256,384},{320,448},{384,256},{4... | collective-permute-start | bytes 3080 | tf_op jit(solution)/shard_map/ppermute | solution.py:23
  166.5 6.3 %collective-permute-start.6 = (f32[2,128]{1,0:T(2,128)S(1)}, f32[2,128]{1,0:T(2,128)S(1)}, u32[]{:S(2)}, u32[]{:S(2)}) collective-permute-start(f32[2,128]{1,0:T(2,128)S(1)} %add.192), channel_id=1, source_target_pairs={{0,256},{64,320},{128,384},{192,448},{256,0},{320,64},{384,128},{4... | collective-permute-start | bytes 3080 | tf_op jit(solution)/shard_map/ppermute | solution.py:23
  172.9 9.7 %collective-permute-start.7 = (f32[2,128]{1,0:T(2,128)S(1)}, f32[2,128]{1,0:T(2,128)S(1)}, u32[]{:S(2)}, u32[]{:S(2)}) collective-permute-start(f32[2,128]{1,0:T(2,128)S(1)} %add.193), channel_id=1, source_target_pairs={{0,512},{64,576},{128,640},{192,704},{256,768},{320,832},{384,896}... | collective-permute-start | bytes 3080 | tf_op jit(solution)/shard_map/ppermute | solution.py:23

commit v3 on v0

v3 whole, which is shorter than its diff:
```python
import functools

import jax
import jax.numpy as jnp
from jax import lax
from jax.experimental import pallas as pl
from jax.experimental.pallas import tpu as pltpu
from jax.sharding import PartitionSpec as P

epsilon = 1e-06
score_scale = 168.0 ** (-0.5)


def summed_over(x, axes):
    devices = 1
    for axis in axes:
        devices *= lax.axis_size(axis)
    copies = jnp.broadcast_to(x[None], (devices,) + x.shape)
    return jnp.sum(lax.all_to_all(copies, axes, 0, 0, tiled=True), axis=0)


def shifted(x, axis, by):
    devices = lax.axis_size(axis)
    pairs = [(i, i + by) for i in range(devices) if 0 <= i + by < devices]
    return lax.ppermute(x, axis, pairs)


def normalize(values, gain):
    inverse = lax.rsqrt(jnp.mean(values * values, axis=-1, keepdims=True) + epsilon)
    unit = values * inverse
    return (unit, inverse, (unit * gain).astype(jnp.bfloat16))


def norm_back(grad_normed, unit, inverse, gain):
    grad_unit = grad_normed * gain
    centered = grad_unit - unit * jnp.mean(grad_unit * unit, axis=-1, keepdims=True)
    return inverse * centered


def window_kernel(ratio, head_dim, lo_ref, q_ref, k_ref, v_ref, up_ref, dq_ref, dk_ref, dv_ref):
    rows = q_ref.shape[0]
    keys = k_ref.shape[0]
    keys_f = k_ref[...]
    values = v_ref[...]
    col = lax.broadcasted_iota(jnp.int32, (rows, keys), 1)
    row = lax.broadcasted_iota(jnp.int32, (rows, keys), 0)
    visible = (col >= lo_ref[...]) & (col <= row + (keys - rows))
    dk = jnp.zeros((keys, head_dim), jnp.float32)
    dv = jnp.zeros((keys, head_dim), jnp.float32)
    for h in range(ratio):
        cols = slice(h * head_dim, (h + 1) * head_dim)
        q = q_ref[:, cols]
        up = up_ref[:, cols]
        scores = lax.dot_general(q, keys_f, (((1,), (1,)), ((), ())), preferred_element_type=jnp.float32) * score_scale
        exp_scores = jnp.where(visible, jnp.exp(scores), 0.0)
        weights = exp_scores / jnp.sum(exp_scores, axis=-1, keepdims=True)
        weights_low = weights.astype(jnp.bfloat16)
        attended = jnp.dot(weights_low, values, preferred_element_type=jnp.float32)
        delta = jnp.sum(up.astype(jnp.float32) * attended, axis=-1, keepdims=True)
        prob_grad = lax.dot_general(up, values, (((1,), (1,)), ((), ())), preferred_element_type=jnp.float32)
        score_grad = weights * (prob_grad - delta) * score_scale
        dq_ref[:, cols] = jnp.dot(score_grad.astype(jnp.bfloat16), keys_f, preferred_element_type=jnp.float32)
        dk = dk + jnp.dot(score_grad.T.astype(jnp.bfloat16), q, preferred_element_type=jnp.float32)
        dv = dv + jnp.dot(weights.T.astype(jnp.bfloat16), up, preferred_element_type=jnp.float32)
    dk_ref[...] = dk
    dv_ref[...] = dv


def window_attention(lo_rel, query_normed, key_cat, value_cat, upstream, ratio, head_dim):
    rows, query_width = query_normed.shape
    keys, key_width = key_cat.shape
    groups = key_width // head_dim
    qw = ratio * head_dim
    flops = 12 * rows * keys * head_dim * ratio * groups
    return pl.pallas_call(
        functools.partial(window_kernel, ratio, head_dim),
        grid=(groups,),
        in_specs=[
            pl.BlockSpec((rows, 1), lambda g: (0, 0)),
            pl.BlockSpec((rows, qw), lambda g: (0, g)),
            pl.BlockSpec((keys, head_dim), lambda g: (0, g)),
            pl.BlockSpec((keys, head_dim), lambda g: (0, g)),
            pl.BlockSpec((rows, qw), lambda g: (0, g)),
        ],
        out_specs=[
            pl.BlockSpec((rows, qw), lambda g: (0, g)),
            pl.BlockSpec((keys, head_dim), lambda g: (0, g)),
            pl.BlockSpec((keys, head_dim), lambda g: (0, g)),
        ],
        out_shape=[
            jax.ShapeDtypeStruct((rows, query_width), jnp.float32),
            jax.ShapeDtypeStruct((keys, key_width), jnp.float32),
            jax.ShapeDtypeStruct((keys, key_width), jnp.float32),
        ],
        cost_estimate=pl.CostEstimate(
            flops=flops,
            transcendentals=rows * keys * ratio * groups,
            bytes_accessed=2 * (2 * rows * query_width + 2 * keys * key_width) + 4 * (rows * query_width + 2 * keys * key_width),
        ),
    )(lo_rel, query_normed, key_cat, value_cat, upstream)


def on_device(query_proj, key_proj, value_proj, out_grad, lowest_key_index, query_gain, key_gain):
    rows = query_proj.shape[2]
    query_width = query_proj.shape[3]
    key_width = key_proj.shape[3]
    head_dim = query_gain.shape[1]
    groups = key_width // head_dim
    heads = query_width // head_dim
    ratio = heads // groups
    query_local = query_proj.reshape(rows, query_width)
    key_local = key_proj.reshape(rows, key_width)
    value_local = value_proj.reshape(rows, key_width)
    pipe_devices = lax.axis_size("pipe")
    upstream = lax.ppermute(
        out_grad.reshape(rows, query_width), "pipe", [(i, (i - 1) % pipe_devices) for i in range(pipe_devices)]
    )
    halo = shifted(jnp.stack([key_local, value_local]), "seq", 1)
    query_scale = query_gain.reshape(head_dim)
    key_scale = key_gain.reshape(head_dim)
    query_unit, query_inverse, query_normed = normalize(
        query_local.astype(jnp.float32).reshape(rows, heads, head_dim), query_scale
    )
    key_unit, key_inverse, key_normed = normalize(
        key_local.astype(jnp.float32).reshape(rows, groups, head_dim), key_scale
    )
    prev_unit, _, prev_normed = normalize(halo[0].astype(jnp.float32).reshape(rows, groups, head_dim), key_scale)
    key_cat = jnp.concatenate([prev_normed.reshape(rows, key_width), key_normed.reshape(rows, key_width)], axis=0)
    value_cat = jnp.concatenate([halo[1], value_local], axis=0)
    block = lax.axis_index("seq")
    first = block * rows
    lo_rel = (lax.dynamic_slice(lowest_key_index.reshape(-1), (first,), (rows,)) - (first - rows)).reshape(rows, 1)
    query_normed_grad, key_parts, value_parts = window_attention(
        lo_rel, query_normed.reshape(rows, query_width), key_cat, value_cat, upstream, ratio, head_dim
    )
    back = shifted(jnp.stack([key_parts[:rows], value_parts[:rows]]), "seq", -1)
    key_normed_grad = (key_parts[rows:] + back[0]).reshape(rows, groups, head_dim)
    value_rows = value_parts[rows:] + back[1]
    query_normed_grad = query_normed_grad.reshape(rows, heads, head_dim)
    query_term = jnp.sum(query_normed_grad * query_unit, axis=(0, 1))
    key_term = jnp.sum(key_parts[rows:].reshape(rows, groups, head_dim) * key_unit, axis=(0, 1)) + jnp.sum(
        key_parts[:rows].reshape(rows, groups, head_dim) * prev_unit, axis=(0, 1)
    )
    both = summed_over(jnp.stack([query_term, key_term]), ("dp", "seq"))
    query_grad = norm_back(query_normed_grad, query_unit, query_inverse, query_scale).astype(jnp.bfloat16)
    key_grad = norm_back(key_normed_grad, key_unit, key_inverse, key_scale).astype(jnp.bfloat16)
    value_grad = value_rows.astype(jnp.bfloat16)
    return (
        query_grad.reshape(1, 1, rows, query_width),
        key_grad.reshape(1, 1, rows, key_width),
        value_grad.reshape(1, 1, rows, key_width),
        both[0].reshape(1, head_dim),
        both[1].reshape(1, head_dim),
    )


def solution(mesh):
    return jax.shard_map(
        on_device,
        mesh=mesh,
        in_specs=(
            P("pipe", "dp", "seq", None),
            P("pipe", "dp", "seq", None),
            P("pipe", "dp", "seq", None),
            P("pipe", "dp", "seq", None),
            P("pipe", "dp", None),
            P("pipe", None),
            P("pipe", None),
        ),
        out_specs=(
            P("pipe", "dp", "seq", None),
            P("pipe", "dp", "seq", None),
            P("pipe", "dp", "seq", None),
            P("pipe", None),
            P("pipe", None),
        ),
        check_vma=False,
    )
```

time: 572 us -> 117 us (0.20)
  blocking collectives: 440 us -> 0 us
  matrix products: 15.5 us -> 0 us
  waiting for transfers between devices: 44.6 us -> 31.6 us
  Pallas kernels: 0 us -> 10.1 us
  other arithmetic: 8.02 us -> 18.1 us
  starting transfers between devices: 40.3 us -> 34.4 us
    psum x1 -> x0, blocking collectives: 440 us -> none  [on_device(): query_sum, key_sum = lax.psum((query_term, key_term), ('dp', 'seq'))]
    all_to_all x7 -> x1, waiting for transfers between devices: 44.6 us -> 11.8 us  [summed_over(): return jnp.sum(lax.all_to_all(copies, axes, 0, 0, tiled=True), axis=0)]
    ppermute x1 -> x3, waiting for transfers between devices: 0.01 us -> 19.9 us  [the longest x2 19.8 us: shifted(): return lax.ppermute(x, axis, pairs)]
    all_to_all x7 -> x1, starting transfers between devices: 38.3 us -> 25.3 us  [summed_over(): return jnp.sum(lax.all_to_all(copies, axes, 0, 0, tiled=True), axis=0)]
    dot_general x20 -> x0, matrix products: 10.5 us -> none  [the longest x4 3.33 us: on_device(): jnp.einsum('grqk,grqd->gkd', weights_reduced, grad_tile, preferred_elemen...]
    pallas_call x0 -> x1, Pallas kernels: none -> 10.1 us  [window_attention(): pl.pallas_call(functools.partial(window_kernel, ratio, head_dim), grid=(g...]
    mul x0 -> x11, local copies, waits for them, and re-layouts: none -> 7.82 us  [the longest x4 4.04 us: norm_back(): unit * jnp.mean(grad_unit * unit, axis=-1, keepdims=True)]
    ppermute x1 -> x3, starting transfers between devices: 1.92 us -> 9.16 us  [the longest x2 7.25 us: shifted(): return lax.ppermute(x, axis, pairs)]
  transfers between devices with their start and end apart: 8 -> 4, of which waited for: 6 -> 3; matrix products, arithmetic and copies ran while one was open for 5% -> 21% of each run, Pallas kernels for 0% -> 0%
where the time goes in v3:
time: 117 us; the launch traced here: 116 us
  starting transfers between devices  34.4 us (29%)
  waiting for transfers between devices  31.6 us (27%)
  local copies, waits for them, and re-layouts  20.3 us (17%)
  other arithmetic  18.1 us (15%)
  Pallas kernels  10.1 us (9%)
    all_to_all x1, starting transfers between devices, summed_over(): return jnp.sum(lax.all_to_all(copies, axes, 0, 0, tiled=True), axis=0)  25.3 us
    ppermute x2, waiting for transfers between devices, shifted(): return lax.ppermute(x, axis, pairs)  19.8 us
    all_to_all x1, waiting for transfers between devices, summed_over(): return jnp.sum(lax.all_to_all(copies, axes, 0, 0, tiled=True), axis=0)  11.8 us
    pallas_call x1, Pallas kernels, window_attention(): pl.pallas_call(functools.partial(window_kernel, ratio, head_dim), grid=(g...  10.1 us
    ppermute x2, starting transfers between devices, shifted(): return lax.ppermute(x, axis, pairs)  7.25 us
    unnamed x43, local copies, waits for them, and re-layouts  6.32 us
    mul x4, local copies, waits for them, and re-layouts, norm_back(): unit * jnp.mean(grad_unit * unit, axis=-1, keepdims=True)  4.04 us
    convert_element_type x2, other arithmetic, normalize(): return (unit, inverse, (unit * gain).astype(jnp.bfloat16))  2.65 us
  transfers between devices with their start and end apart: 4, of which 3 were waited for; matrix products, arithmetic and copies ran while one was open for 21% of the time, Pallas kernels for 0%

profile of v3, /device:TPU:2, one launch (start us, length us, event | category | flops | bytes accessed | tf_op | source)
XLA Modules:
  0.0 115.5 jit_solution(17111167877199124513)
XLA Ops:
  0.6 1.9 %pad_maximum_fusion.1 = bf16[2,128,1024]{2,1,0:T(8,128)(2,1)} fusion(bf16[1,128,1024]{2,1,0:T(8,128)(2,1)} %bitcast.128, bf16[1,128,1024]{2,1,0:T(8,128)(2,1)} %bitcast.122), kind=kLoop, calls=%fused_computation.32 | loop fusion | flops 262144 | bytes 1048576 | tf_op jit(solution)/shard_map/stack | solution.py:118
  2.6 6.0 %collective-permute-start = (bf16[2,128,1024]{2,1,0:T(8,128)(2,1)}, bf16[2,128,1024]{2,1,0:T(8,128)(2,1)}, u32[]{:S(2)}, u32[]{:S(2)}) collective-permute-start(bf16[2,128,1024]{2,1,0:T(8,128)(2,1)} %pad_maximum_fusion.1), channel_id=1, source_target_pairs={{0,1},{1,2},{2,3},{3,4},{4,5},{5,6},{6,7},{8,9},{9,10},{10,11},{11... | collective-permute-start | bytes 1572872 | tf_op jit(solution)/shard_map/ppermute | solution.py:25
  8.5 1.9 %collective-permute-start.1 = (bf16[128,2048]{1,0:T(8,128)(2,1)}, bf16[128,2048]{1,0:T(8,128)(2,1)}, u32[]{:S(2)}, u32[]{:S(2)}) collective-permute-start(bf16[128,2048]{1,0:T(8,128)(2,1)} %bitcast.12), channel_id=1, source_target_pairs={{0,56},{8,0},{16,8},{24,16},{32,24},{40,32},{48,40},{56,48},{1,57}... | collective-permute-start | bytes 1572872 | tf_op jit(solution)/shard_map/ppermute | solution.py:115
  10.5 0.1 copy.36
  10.6 0.0 copy-start.3
  10.7 0.8 copy-done.6
  11.4 0.2 multiply_reduce_fusion.6
  11.7 0.7 copy-done.17
  12.4 0.1 convert_bitcast_fusion.1
  12.5 0.2 copy.32
  12.7 0.3 multiply_reduce_fusion.2
  13.1 0.0 copy-start.16
  13.1 0.6 copy-done.16
  13.7 0.7 subtract_bitcast_fusion
  14.4 0.1 copy.24
  14.5 0.7 copy.25.lo_ref
  15.2 0.2 mul.218
  15.4 1.1 mul.233
  16.5 0.3 mul.197
  16.8 1.2 mul.198
  18.0 1.2 %multiply_convert_fusion.q_ref = bf16[128,2048]{1,0:T(8,128)(2,1)} fusion(f32[16,8,16,128]{3,2,1,0:T(8,128)S(1)} %bitcast.115, bf16[1,1,128,2048]{3,2,1,0:T(8,128)(2,1)S(1)} %copy-done.3, f32[2048]{0:T(1024)S(1)} %broadcast_bitcast_fusion), kind=kLoop, calls=%fused_computation.12 | loop fusion | flops 1048576 | bytes 2105344 | tf_op jit(solution)/shard_map/convert_element_type | solution.py:31
  19.2 0.1 collective-permute-done
  19.2 1.0 fusion.6
  20.2 0.1 copy.34
  20.3 0.8 reduce_sum.103
  21.2 0.9 copy.21
  22.1 0.8 copy.22
  22.8 1.0 mul.209
  23.9 1.5 %multiply_convert_fusion.2 = (bf16[128,1024]{1,0:T(8,128)(2,1)S(1)}, bf16[128,1024]{1,0:T(8,128)(2,1)S(1)}) fusion(f32[16,8,8,128]{3,2,1,0:T(8,128)S(1)} %bitcast.125, f32[1024]{0:T(1024)S(1)} %broadcast_bitcast_fusion.1, bf16[2,128,1024]{2,1,0:T(8,128)(2,1)} %collective-permute-done, f32[16,8,8,128]{3,2,1,0:T(8,128)S(1)} %bitcast.120, ...), kind=kLoop, calls=%fused_computation.41 | loop fusion | flops 1048576 | bytes 2101248 | tf_op jit(solution)/shard_map/convert_element_type | solution.py:31
  25.4 0.8 pad_maximum_fusion.2.k_ref
  26.2 1.0 slice_bitcast_fusion.4
  27.2 0.0 copy-done.15
  27.2 0.8 pad_maximum_fusion.3.v_ref
  28.1 0.0 collective-permute-done.1.up_ref
  28.1 10.1 %shard_map.110 = (f32[128,2048]{1,0:T(8,128)}, f32[256,1024]{1,0:T(8,128)}, f32[256,1024]{1,0:T(8,128)}) custom-call(s32[128,1]{1,0:T(8,128)} %copy.25.lo_ref, bf16[128,2048]{1,0:T(8,128)(2,1)} %multiply_convert_fusion.q_ref, bf16[256,1024]{1,0:T(8,128)(2,1)} %pad_maximum_fusion.2.k_ref, bf16[256,1024]{1,0:T(8,128)(2,1)} %pad_maximum_fusion.3.v_ref, ...), custom_call_target="tpu_custom_call" | custom-call | flops 805306368 | bytes 5242880 | tf_op jit(solution)/shard_map/pallas_call | solution.py:75
  38.2 1.3 %slice_bitcast_fusion.2 = (f32[1,128,1024]{2,1,0:T(8,128)S(1)}, f32[1,128,1024]{2,1,0:T(8,128)S(1)}) fusion(f32[256,1024]{1,0:T(8,128)} %get-tuple-element.10, f32[256,1024]{1,0:T(8,128)} %get-tuple-element.9), kind=kLoop, calls=%fused_computation.38 | loop fusion | bytes 2097152 | tf_op jit(solution)/shard_map/stack | solution.py:136
  39.5 1.1 pad_maximum_fusion
  40.6 1.3 %collective-permute-start.2 = (f32[2,128,1024]{2,1,0:T(8,128)}, f32[2,128,1024]{2,1,0:T(8,128)}, u32[]{:S(2)}, u32[]{:S(2)}) collective-permute-start(f32[2,128,1024]{2,1,0:T(8,128)} %pad_maximum_fusion), channel_id=1, source_target_pairs={{1,0},{2,1},{3,2},{4,3},{5,4},{6,5},{7,6},{9,8},{10,9},{11,10},{12... | collective-permute-start | bytes 3145736 | tf_op jit(solution)/shard_map/ppermute | solution.py:25
  41.9 0.2 copy.38
  42.1 0.1 bitcast_multiply_fusion
  42.2 0.6 multiply_reduce_fusion.1
  42.9 1.3 %mul.229 = f32[128,16,128]{2,1,0:T(8,128)} broadcast(f32[128,16]{1,0:T(8,128)S(1)} %broadcast_multiply_fusion), dimensions={0,1} | broadcast | bytes 1056768 | tf_op jit(solution)/shard_map/mul | solution.py:36
  44.2 2.4 %mul.230 = f32[1,1,128,2048]{3,2,1,0:T(8,128)} reshape(f32[128,16,128]{2,1,0:T(8,128)} %mul.229) | data formatting | bytes 2097152 | tf_op jit(solution)/shard_map/mul | solution.py:36
  46.7 0.5 multiply_reduce_fusion
  47.2 0.7 copy-done.11
  47.9 0.3 copy-done.12
  48.2 1.1 fusion.4
  49.3 19.8 %collective-permute-done.2 = f32[2,128,1024]{2,1,0:T(8,128)} collective-permute-done((f32[2,128,1024]{2,1,0:T(8,128)}, f32[2,128,1024]{2,1,0:T(8,128)}, u32[]{:S(2)}, u32[]{:S(2)}) %collective-permute-start.2) | collective-permute-done | bytes 1048608 | tf_op jit(solution)/shard_map/ppermute | solution.py:25
  69.1 2.5 %multiply_reduce_fusion.3 = (f32[1024]{0:T(1024)S(1)}, f32[1024]{0:T(1024)S(1)}, f32[16,8,8,128]{3,1,2,0:T(8,128)S(1)}, bf16[1,1,128,1024]{3,2,1,0:T(8,128)(2,1)}) fusion(f32[256,1024]{1,0:T(8,128)S(1)} %copy-done.10, f32[16,8,8,128]{3,2,1,0:T(8,128)S(1)} %bitcast.126, bf16[2,128,1024]{2,1,0:T(8,128)(2,1)} %collective-permute-done, ...), kind=kLoop, calls=%fused_computation.35 | loop fusion | flops 1439744 | bytes 4988928 | tf_op jit(solution)/shard_map/reduce_sum | solution.py:141
  71.7 0.7 broadcast_in_dim.2
  72.3 25.3 %all-to-all-start = ((f32[128,2,128]{2,1,0:T(2,128)}), f32[128,2,128]{2,1,0:T(2,128)S(1)}, u32[]{:S(2)}, u32[]{:S(2)}) async-start(f32[128,2,128]{2,1,0:T(2,128)} %broadcast_in_dim.2), calls=%async_computation | async-start | bytes 262144 | tf_op jit(solution)/shard_map/all_to_all | solution.py:19
  97.6 0.0 copy-start.18
  97.6 0.1 copy.39
  97.7 0.5 copy-done.18
  98.3 1.0 copy-done.7
  99.3 0.4 multiply_reduce_fusion.5
  99.7 0.1 copy.27
  99.9 0.2 mul.241
  100.1 0.1 mul.242
  100.2 0.9 copy-done.13
  101.1 2.0 %fusion.11 = bf16[1,1,128,1024]{3,2,1,0:T(8,128)(2,1)} fusion(f32[1,1,128,1024]{3,2,1,0:T(8,128)S(1)} %copy-done.13, f32[1,1,128,1024]{3,2,1,0:T(8,128)S(1)} %mul.242, bf16[1,1,128,1024]{3,2,1,0:T(8,128)(2,1)S(1)} %copy-done.5, f32[1024]{0:T(1024)S(1)} %broadcast_bitcast_fusion.1, f32[2,128,1024]{2,1,0:T(8,128)} %collective-permute-done.2, ...), kind=kLoop, calls=%fused_computation.25 | loop fusion | flops 1048576 | bytes 2625536 | tf_op jit(solution)/shard_map/convert_element_type | solution.py:146
  103.1 11.8 %all-to-all-done = f32[128,2,128]{2,1,0:T(2,128)S(1)} async-done(((f32[128,2,128]{2,1,0:T(2,128)}), f32[128,2,128]{2,1,0:T(2,128)S(1)}, u32[]{:S(2)}, u32[]{:S(2)}) %all-to-all-start) | async-done | bytes 131104 | tf_op jit(solution)/shard_map/all_to_all | solution.py:19
  114.8 0.1 reduce_sum.116
  115.0 0.5 fusion.17
  (42 shorter events, 0.4 us)
Async XLA Ops:
  0.6 9.8 %copy-start.5 = (bf16[1,1,128,1024]{3,2,1,0:T(8,128)(2,1)S(1)}, bf16[1,1,128,1024]{3,2,1,0:T(8,128)(2,1)}, u32[]{:S(2)}) copy-start(bf16[1,1,128,1024]{3,2,1,0:T(8,128)(2,1)} %param.8) | copy-start | bytes 786436
  2.6 16.7 %collective-permute-start = (bf16[2,128,1024]{2,1,0:T(8,128)(2,1)}, bf16[2,128,1024]{2,1,0:T(8,128)(2,1)}, u32[]{:S(2)}, u32[]{:S(2)}) collective-permute-start(bf16[2,128,1024]{2,1,0:T(8,128)(2,1)} %pad_maximum_fusion.1), channel_id=1, source_target_pairs={{0,1},{1,2},{2,3},{3,4},{4,5},{5,6},{6,7},{8,9},{9,10},{10,11},{11... | collective-permute-start | bytes 1572872 | tf_op jit(solution)/shard_map/ppermute | solution.py:25
  8.5 19.5 %collective-permute-start.1 = (bf16[128,2048]{1,0:T(8,128)(2,1)}, bf16[128,2048]{1,0:T(8,128)(2,1)}, u32[]{:S(2)}, u32[]{:S(2)}) collective-permute-start(bf16[128,2048]{1,0:T(8,128)(2,1)} %bitcast.12), channel_id=1, source_target_pairs={{0,56},{8,0},{16,8},{24,16},{32,24},{40,32},{48,40},{56,48},{1,57}... | collective-permute-start | bytes 1572872 | tf_op jit(solution)/shard_map/ppermute | solution.py:115
  10.6 0.8 copy-start.6
  10.6 1.8 %copy-start.3 = (bf16[1,1,128,2048]{3,2,1,0:T(8,128)(2,1)S(1)}, bf16[1,1,128,2048]{3,2,1,0:T(8,128)(2,1)}, u32[]{:S(2)}) copy-start(bf16[1,1,128,2048]{3,2,1,0:T(8,128)(2,1)} %param.7) | copy-start | bytes 1572868
  11.7 0.7 copy-start.17
  13.1 0.7 copy-start.16
  15.4 8.5 %copy-start.1 = (f32[128,8,128]{2,1,0:T(8,128)}, f32[128,8,128]{2,1,0:T(8,128)S(1)}, u32[]{:S(2)}) copy-start(f32[128,8,128]{2,1,0:T(8,128)S(1)} %mul.218) | copy-start | bytes 1572868
  23.9 1.5 %copy-start.8 = (f32[128,8,128]{2,1,0:T(8,128)}, f32[128,8,128]{2,1,0:T(8,128)S(1)}, u32[]{:S(2)}) copy-start(f32[128,8,128]{2,1,0:T(8,128)S(1)} %mul.209) | copy-start | bytes 1572868
  26.2 1.0 copy-start.15
  39.5 2.4 %copy-start = (f32[128,2048]{1,0:T(8,128)S(1)}, f32[128,2048]{1,0:T(8,128)}, u32[]{:S(2)}) copy-start(f32[128,2048]{1,0:T(8,128)} %get-tuple-element.8) | copy-start | bytes 3145732
  40.6 28.5 %collective-permute-start.2 = (f32[2,128,1024]{2,1,0:T(8,128)}, f32[2,128,1024]{2,1,0:T(8,128)}, u32[]{:S(2)}, u32[]{:S(2)}) collective-permute-start(f32[2,128,1024]{2,1,0:T(8,128)} %pad_maximum_fusion), channel_id=1, source_target_pairs={{1,0},{2,1},{3,2},{4,3},{5,4},{6,5},{7,6},{9,8},{10,9},{11,10},{12... | collective-permute-start | bytes 3145736 | tf_op jit(solution)/shard_map/ppermute | solution.py:25
  44.2 2.4 %copy-start.4 = (bf16[1,1,128,2048]{3,2,1,0:T(8,128)(2,1)S(1)}, bf16[1,1,128,2048]{3,2,1,0:T(8,128)(2,1)}, u32[]{:S(2)}) copy-start(bf16[1,1,128,2048]{3,2,1,0:T(8,128)(2,1)} %param.7) | copy-start | bytes 1572868
  46.6 1.2 %copy-start.11 = (f32[1,1,128,2048]{3,2,1,0:T(8,128)S(1)}, f32[1,1,128,2048]{3,2,1,0:T(8,128)}, u32[]{:S(2)}) copy-start(f32[1,1,128,2048]{3,2,1,0:T(8,128)} %mul.198) | copy-start | bytes 3145732
  46.6 1.5 %copy-start.12 = (f32[1,1,128,2048]{3,2,1,0:T(8,128)S(1)}, f32[1,1,128,2048]{3,2,1,0:T(8,128)}, u32[]{:S(2)}) copy-start(f32[1,1,128,2048]{3,2,1,0:T(8,128)} %mul.230) | copy-start | bytes 3145732
  48.2 20.9 %copy-start.2 = (f32[128,8,128]{2,1,0:T(8,128)S(1)}, f32[128,8,128]{2,1,0:T(8,128)}, u32[]{:S(2)}) copy-start(f32[128,8,128]{2,1,0:T(8,128)} %copy-done.1) | copy-start | bytes 1572868
  48.2 20.9 %copy-start.9 = (f32[128,8,128]{2,1,0:T(8,128)S(1)}, f32[128,8,128]{2,1,0:T(8,128)}, u32[]{:S(2)}) copy-start(f32[128,8,128]{2,1,0:T(8,128)} %copy-done.8) | copy-start | bytes 1572868
  48.2 20.9 %copy-start.10 = (f32[256,1024]{1,0:T(8,128)S(1)}, f32[256,1024]{1,0:T(8,128)}, u32[]{:S(2)}) copy-start(f32[256,1024]{1,0:T(8,128)} %get-tuple-element.9) | copy-start | bytes 3145732
  48.2 20.9 %copy-start.14 = (f32[256,1024]{1,0:T(8,128)S(1)}, f32[256,1024]{1,0:T(8,128)}, u32[]{:S(2)}) copy-start(f32[256,1024]{1,0:T(8,128)} %get-tuple-element.10) | copy-start | bytes 3145732
  72.3 42.5 %all-to-all-start = ((f32[128,2,128]{2,1,0:T(2,128)}), f32[128,2,128]{2,1,0:T(2,128)S(1)}, u32[]{:S(2)}, u32[]{:S(2)}) async-start(f32[128,2,128]{2,1,0:T(2,128)} %broadcast_in_dim.2), calls=%async_computation | async-start | bytes 262144 | tf_op jit(solution)/shard_map/all_to_all | solution.py:19
  97.6 0.7 copy-start.18
  98.3 1.0 copy-start.7
  100.1 1.0 copy-start.13

commit v4 on v3

v4 whole, which is shorter than its diff:
```python
import functools

import jax
import jax.numpy as jnp
from jax import lax
from jax.experimental import pallas as pl
from jax.sharding import PartitionSpec as P

epsilon = 1e-06
score_scale = 168.0 ** (-0.5)


def summed_over(x, axes):
    devices = 1
    for axis in axes:
        devices *= lax.axis_size(axis)
    copies = jnp.broadcast_to(x[None], (devices,) + x.shape)
    return jnp.sum(lax.all_to_all(copies, axes, 0, 0, tiled=True), axis=0)


def shifted(x, axis, by):
    devices = lax.axis_size(axis)
    pairs = [(i, i + by) for i in range(devices) if 0 <= i + by < devices]
    return lax.ppermute(x, axis, pairs)


def normalize(values, gain):
    inverse = lax.rsqrt(jnp.mean(values * values, axis=-1, keepdims=True) + epsilon)
    unit = values * inverse
    return (unit, inverse, (unit * gain).astype(jnp.bfloat16))


def norm_back(grad_normed, unit, inverse, gain):
    grad_unit = grad_normed * gain
    centered = grad_unit - unit * jnp.mean(grad_unit * unit, axis=-1, keepdims=True)
    return inverse * centered


def window_kernel(ratio, head_dim, lo_ref, qgain_ref, kgain_ref, q_ref, k_ref, v_ref, halo_ref, up_ref,
                  qgrad_ref, own_ref, send_ref, gains_ref):
    rows = q_ref.shape[0]
    qgain = qgain_ref[...]
    kgain = kgain_ref[...]
    key_raw = jnp.concatenate([halo_ref[0], k_ref[...]], axis=0).astype(jnp.float32)
    values = jnp.concatenate([halo_ref[1], v_ref[...]], axis=0)
    keys = key_raw.shape[0]
    key_unit, _, key_normed = normalize(key_raw, kgain)
    col = lax.broadcasted_iota(jnp.int32, (rows, keys), 1)
    row = lax.broadcasted_iota(jnp.int32, (rows, keys), 0)
    visible = (col >= lo_ref[...]) & (col <= row + (keys - rows))
    dk = jnp.zeros((keys, head_dim), jnp.float32)
    dv = jnp.zeros((keys, head_dim), jnp.float32)
    qterm = jnp.zeros((1, head_dim), jnp.float32)
    for h in range(ratio):
        cols = slice(h * head_dim, (h + 1) * head_dim)
        query_unit, query_inverse, q = normalize(q_ref[:, cols].astype(jnp.float32), qgain)
        up = up_ref[:, cols]
        scores = lax.dot_general(q, key_normed, (((1,), (1,)), ((), ())), preferred_element_type=jnp.float32) * score_scale
        exp_scores = jnp.where(visible, jnp.exp(scores), 0.0)
        weights = exp_scores / jnp.sum(exp_scores, axis=-1, keepdims=True)
        weights_low = weights.astype(jnp.bfloat16)
        attended = jnp.dot(weights_low, values, preferred_element_type=jnp.float32)
        delta = jnp.sum(up.astype(jnp.float32) * attended, axis=-1, keepdims=True)
        prob_grad = lax.dot_general(up, values, (((1,), (1,)), ((), ())), preferred_element_type=jnp.float32)
        score_grad = weights * (prob_grad - delta) * score_scale
        dq = jnp.dot(score_grad.astype(jnp.bfloat16), key_normed, preferred_element_type=jnp.float32)
        qgrad_ref[:, cols] = norm_back(dq, query_unit, query_inverse, qgain).astype(qgrad_ref.dtype)
        qterm = qterm + jnp.sum(dq * query_unit, axis=0, keepdims=True)
        dk = dk + jnp.dot(score_grad.T.astype(jnp.bfloat16), q, preferred_element_type=jnp.float32)
        dv = dv + jnp.dot(weights.T.astype(jnp.bfloat16), up, preferred_element_type=jnp.float32)
    kterm = jnp.sum(dk * key_unit, axis=0, keepdims=True)
    own_ref[0] = dk[rows:]
    own_ref[1] = dv[rows:]
    send_ref[0] = dk[:rows].astype(send_ref.dtype)
    send_ref[1] = dv[:rows].astype(send_ref.dtype)

    @pl.when(pl.program_id(0) == 0)
    def _():
        gains_ref[...] = jnp.zeros_like(gains_ref)

    gains_ref[...] += jnp.concatenate([qterm, kterm], axis=0)


def window_attention(lo_rel, query_gain, key_gain, query_local, key_local, value_local, halo, upstream, ratio, head_dim):
    rows, query_width = query_local.shape
    key_width = key_local.shape[1]
    groups = key_width // head_dim
    qw = ratio * head_dim
    keys = 2 * rows
    flops = 12 * rows * keys * head_dim * ratio * groups
    return pl.pallas_call(
        functools.partial(window_kernel, ratio, head_dim),
        grid=(groups,),
        in_specs=[
            pl.BlockSpec((rows, 1), lambda g: (0, 0)),
            pl.BlockSpec((1, head_dim), lambda g: (0, 0)),
            pl.BlockSpec((1, head_dim), lambda g: (0, 0)),
            pl.BlockSpec((rows, qw), lambda g: (0, g)),
            pl.BlockSpec((rows, head_dim), lambda g: (0, g)),
            pl.BlockSpec((rows, head_dim), lambda g: (0, g)),
            pl.BlockSpec((2, rows, head_dim), lambda g: (0, 0, g)),
            pl.BlockSpec((rows, qw), lambda g: (0, g)),
        ],
        out_specs=[
            pl.BlockSpec((rows, qw), lambda g: (0, g)),
            pl.BlockSpec((2, rows, head_dim), lambda g: (0, 0, g)),
            pl.BlockSpec((2, rows, head_dim), lambda g: (0, 0, g)),
            pl.BlockSpec((2, head_dim), lambda g: (0, 0)),
        ],
        out_shape=[
            jax.ShapeDtypeStruct((rows, query_width), jnp.bfloat16),
            jax.ShapeDtypeStruct((2, rows, key_width), jnp.float32),
            jax.ShapeDtypeStruct((2, rows, key_width), jnp.bfloat16),
            jax.ShapeDtypeStruct((2, head_dim), jnp.float32),
        ],
        cost_estimate=pl.CostEstimate(
            flops=flops,
            transcendentals=rows * keys * ratio * groups,
            bytes_accessed=2 * (4 * rows * query_width + 6 * rows * key_width) + 8 * rows * key_width,
        ),
    )(lo_rel, query_gain, key_gain, query_local, key_local, value_local, halo, upstream)


def on_device(query_proj, key_proj, value_proj, out_grad, lowest_key_index, query_gain, key_gain):
    rows = query_proj.shape[2]
    query_width = query_proj.shape[3]
    key_width = key_proj.shape[3]
    head_dim = query_gain.shape[1]
    groups = key_width // head_dim
    heads = query_width // head_dim
    ratio = heads // groups
    query_local = query_proj.reshape(rows, query_width)
    key_local = key_proj.reshape(rows, key_width)
    value_local = value_proj.reshape(rows, key_width)
    pipe_devices = lax.axis_size("pipe")
    upstream = lax.ppermute(
        out_grad.reshape(rows, query_width), "pipe", [(i, (i - 1) % pipe_devices) for i in range(pipe_devices)]
    )
    halo = shifted(jnp.stack([key_local, value_local]), "seq", 1)
    block = lax.axis_index("seq")
    first = block * rows
    lo_rel = (lax.dynamic_slice(lowest_key_index.reshape(-1), (first,), (rows,)) - (first - rows)).reshape(rows, 1)
    query_grad, own, send, gain_terms = window_attention(
        lo_rel, query_gain, key_gain, query_local, key_local, value_local, halo, upstream, ratio, head_dim
    )
    back = shifted(send, "seq", -1)
    both = summed_over(gain_terms, ("dp", "seq"))
    key_scale = key_gain.reshape(head_dim)
    key_unit, key_inverse, _ = normalize(key_local.astype(jnp.float32).reshape(rows, groups, head_dim), key_scale)
    key_normed_grad = (own[0] + back[0].astype(jnp.float32)).reshape(rows, groups, head_dim)
    value_rows = own[1] + back[1].astype(jnp.float32)
    key_grad = norm_back(key_normed_grad, key_unit, key_inverse, key_scale).astype(jnp.bfloat16)
    value_grad = value_rows.astype(jnp.bfloat16)
    return (
        query_grad.reshape(1, 1, rows, query_width),
        key_grad.reshape(1, 1, rows, key_width),
        value_grad.reshape(1, 1, rows, key_width),
        both[0].reshape(1, head_dim),
        both[1].reshape(1, head_dim),
    )


def solution(mesh):
    return jax.shard_map(
        on_device,
        mesh=mesh,
        in_specs=(
            P("pipe", "dp", "seq", None),
            P("pipe", "dp", "seq", None),
            P("pipe", "dp", "seq", None),
            P("pipe", "dp", "seq", None),
            P("pipe", "dp", None),
            P("pipe", None),
            P("pipe", None),
        ),
        out_specs=(
            P("pipe", "dp", "seq", None),
            P("pipe", "dp", "seq", None),
            P("pipe", "dp", "seq", None),
            P("pipe", None),
            P("pipe", None),
        ),
        check_vma=False,
    )
```

time: 117 us -> 82 us (0.70)
  local copies, waits for them, and re-layouts: 20.3 us -> 5.03 us
  other arithmetic: 18.1 us -> 4.37 us
  waiting for transfers between devices: 31.6 us -> 23.7 us
  starting transfers between devices: 34.4 us -> 36.7 us
    ppermute x2, waiting for transfers between devices: 19.8 us -> 7.42 us  [shifted(): return lax.ppermute(x, axis, pairs)]
    all_to_all x1, waiting for transfers between devices: 11.8 us -> 16.2 us  [summed_over(): return jnp.sum(lax.all_to_all(copies, axes, 0, 0, tiled=True), axis=0)]
    unnamed x43 -> x16, local copies, waits for them, and re-layouts: 6.32 us -> 2.51 us
    mul x4 -> x2, local copies, waits for them, and re-layouts: 4.04 us -> 0.28 us  [norm_back(): unit * jnp.mean(grad_unit * unit, axis=-1, keepdims=True)]
    reduce_sum x5 -> x0, other arithmetic: 3.05 us -> none  [the longest x2 2.48 us: on_device(): jnp.sum(key_parts[:rows].reshape(rows, groups, head_dim) * prev_unit, axi...]
    all_to_all x1, starting transfers between devices: 25.3 us -> 28.3 us  [summed_over(): return jnp.sum(lax.all_to_all(copies, axes, 0, 0, tiled=True), axis=0)]
    convert_element_type x3 -> x1, other arithmetic: 3.79 us -> 0.84 us  [on_device(): value_grad = value_rows.astype(jnp.bfloat16)]
    mul x5 -> x1, local copies, waits for them, and re-layouts: 2.3 us -> 0.01 us  [norm_back(): grad_unit = grad_normed * gain]
  transfers between devices with their start and end apart: 4 -> 4, of which waited for: 3 -> 2; matrix products, arithmetic and copies ran while one was open for 21% -> 4% of each run, Pallas kernels for 0% -> 0%
where the time goes in v4:
time: 82 us; the launch traced here: 81.7 us
  starting transfers between devices  36.7 us (45%)
  waiting for transfers between devices  23.7 us (29%)
  Pallas kernels  11.1 us (14%)
  local copies, waits for them, and re-layouts  5.03 us (6%)
  other arithmetic  4.37 us (5%)
    all_to_all x1, starting transfers between devices, summed_over(): return jnp.sum(lax.all_to_all(copies, axes, 0, 0, tiled=True), axis=0)  28.3 us
    all_to_all x1, waiting for transfers between devices, summed_over(): return jnp.sum(lax.all_to_all(copies, axes, 0, 0, tiled=True), axis=0)  16.2 us
    pallas_call x1, Pallas kernels, window_attention(): pl.pallas_call(functools.partial(window_kernel, ratio, head_dim), grid=(g...  11.1 us
    ppermute x2, waiting for transfers between devices, shifted(): return lax.ppermute(x, axis, pairs)  7.42 us
    ppermute x2, starting transfers between devices, shifted(): return lax.ppermute(x, axis, pairs)  6.51 us
    unnamed x16, local copies, waits for them, and re-layouts  2.51 us
    ppermute x1, starting transfers between devices, on_device(): lax.ppermute(out_grad.reshape(rows, query_width), 'pipe', [(i, (i - 1) %...  1.92 us
  transfers between devices with their start and end apart: 4, of which 2 were waited for; matrix products, arithmetic and copies ran while one was open for 4% of the time, Pallas kernels for 0%

profile of v4, /device:TPU:2, one launch (start us, length us, event | category | flops | bytes accessed | tf_op | source)
XLA Modules:
  0.0 81.7 jit_solution(4035384241970076596)
XLA Ops:
  0.6 0.0 copy-start.5
  0.6 0.0 copy-start
  0.7 1.1 %pad_maximum_fusion = bf16[2,128,1024]{2,1,0:T(8,128)(2,1)S(1)} fusion(bf16[1,128,1024]{2,1,0:T(8,128)(2,1)} %bitcast.32, bf16[1,128,1024]{2,1,0:T(8,128)(2,1)} %bitcast.30), kind=kLoop, calls=%fused_computation.7 | loop fusion | flops 262144 | bytes 1048576 | tf_op jit(solution)/shard_map/stack | solution.py:139
  1.8 5.2 %collective-permute-start = (bf16[2,128,1024]{2,1,0:T(8,128)(2,1)S(1)}, bf16[2,128,1024]{2,1,0:T(8,128)(2,1)S(1)}, u32[]{:S(2)}, u32[]{:S(2)}) collective-permute-start(bf16[2,128,1024]{2,1,0:T(8,128)(2,1)S(1)} %pad_maximum_fusion), channel_id=1, source_target_pairs={{0,1},{1,2},{2,3},{3,4},{4,5},{5,6},{6,7},{8,9},{9,10},{10,11},{11... | collective-permute-start | bytes 1572872 | tf_op jit(solution)/shard_map/ppermute | solution.py:24
  7.0 0.0 copy-done.5
  7.0 1.9 %collective-permute-start.1 = (bf16[128,2048]{1,0:T(8,128)(2,1)S(1)}, bf16[128,2048]{1,0:T(8,128)(2,1)}, u32[]{:S(2)}, u32[]{:S(2)}) collective-permute-start(bf16[128,2048]{1,0:T(8,128)(2,1)S(1)} %bitcast.36), channel_id=1, source_target_pairs={{0,56},{8,0},{16,8},{24,16},{32,24},{40,32},{48,40},{56,48},{1,57}... | collective-permute-start | bytes 1572872 | tf_op jit(solution)/shard_map/ppermute | solution.py:136
  9.0 0.7 subtract_bitcast_fusion
  9.6 0.7 copy.14.lo_ref
  10.4 0.0 copy-done
  10.4 0.1 copy.19
  10.5 0.2 multiply_reduce_fusion.1
  10.8 7.4 %collective-permute-done.halo_ref = bf16[2,128,1024]{2,1,0:T(8,128)(2,1)S(1)} collective-permute-done((bf16[2,128,1024]{2,1,0:T(8,128)(2,1)S(1)}, bf16[2,128,1024]{2,1,0:T(8,128)(2,1)S(1)}, u32[]{:S(2)}, u32[]{:S(2)}) %collective-permute-start) | collective-permute-done | bytes 524320 | tf_op jit(solution)/shard_map/ppermute | solution.py:24
  18.2 0.0 copy-start.6
  18.2 0.0 collective-permute-done.1.up_ref
  18.2 0.8 copy-done.6
  19.0 11.1 %shard_map.110 = (bf16[128,2048]{1,0:T(8,128)(2,1)}, f32[2,128,1024]{2,1,0:T(8,128)}, bf16[2,128,1024]{2,1,0:T(8,128)(2,1)}, f32[2,128]{1,0:T(2,128)}) custom-call(s32[128,1]{1,0:T(8,128)} %copy.14.lo_ref, f32[1,128]{1,0:T(1,128)} %qgain_ref.1, f32[1,128]{1,0:T(1,128)} %kgain_ref.1, bf16[128,2048]{1,0:T(8,128)(2,1)} %bitcast.37, bf16[128,1024]{1,0:T(8,128)(2,1)} %bitcast.31, ...), custom_call_target="tpu_custom_call" | custom-call | flops 805306368 | bytes 4718592 | tf_op jit(solution)/shard_map/pallas_call | solution.py:91
  30.1 0.0 copy-start.4
  30.1 1.3 %collective-permute-start.2 = (bf16[2,128,1024]{2,1,0:T(8,128)(2,1)}, bf16[2,128,1024]{2,1,0:T(8,128)(2,1)S(1)}, u32[]{:S(2)}, u32[]{:S(2)}) collective-permute-start(bf16[2,128,1024]{2,1,0:T(8,128)(2,1)} %get-tuple-element.11), channel_id=1, source_target_pairs={{1,0},{2,1},{3,2},{4,3},{5,4},{6,5},{7,6},{9,8},{10,9},{11,10},{12... | collective-permute-start | bytes 1572872 | tf_op jit(solution)/shard_map/ppermute | solution.py:24
  31.4 0.0 copy-done.4
  31.4 0.7 broadcast_in_dim.2
  32.1 0.0 copy-start.2
  32.1 28.3 %all-to-all-start = ((f32[128,2,128]{2,1,0:T(2,128)}), f32[128,2,128]{2,1,0:T(2,128)S(1)}, u32[]{:S(2)}, u32[]{:S(2)}) async-start(f32[128,2,128]{2,1,0:T(2,128)} %broadcast_in_dim.2), calls=%async_computation | async-start | bytes 262144 | tf_op jit(solution)/shard_map/all_to_all | solution.py:18
  60.4 0.2 mul.83
  60.6 0.1 mul.84
  60.7 0.0 copy-start.3
  60.7 0.6 copy-done.3
  61.3 16.2 %all-to-all-done = f32[128,2,128]{2,1,0:T(2,128)S(1)} async-done(((f32[128,2,128]{2,1,0:T(2,128)}), f32[128,2,128]{2,1,0:T(2,128)S(1)}, u32[]{:S(2)}, u32[]{:S(2)}) %all-to-all-start) | async-done | bytes 131104 | tf_op jit(solution)/shard_map/all_to_all | solution.py:18
  77.6 0.1 reduce_sum.29
  77.7 0.5 fusion.6
  78.2 0.0 collective-permute-done.2
  78.2 0.0 copy-done.2
  78.3 0.8 %fusion.5 = (bf16[1,1,128,1024]{3,2,1,0:T(8,128)(2,1)}, f32[16,8,8,128]{3,1,2,0:T(8,128)S(1)}) fusion(f32[2,128,1024]{2,1,0:T(8,128)S(1)} %copy-done.2, bf16[2,128,1024]{2,1,0:T(8,128)(2,1)S(1)} %collective-permute-done.2), kind=kLoop, calls=%fused_computation.14 | loop fusion | flops 655360 | bytes 2359296 | tf_op jit(solution)/shard_map/convert_element_type | solution.py:153
  79.1 0.1 copy.20
  79.2 0.4 multiply_reduce_fusion
  79.6 0.2 mul.95
  79.8 0.0 copy-start.1
  79.8 0.1 mul.96
  79.9 0.9 %copy-done.1 = bf16[1,1,128,1024]{3,2,1,0:T(8,128)(2,1)S(1)} copy-done((bf16[1,1,128,1024]{3,2,1,0:T(8,128)(2,1)S(1)}, bf16[1,1,128,1024]{3,2,1,0:T(8,128)(2,1)}, u32[]{:S(2)}) %copy-start.1) | copy-done | bytes 262168
  80.8 0.9 %fusion.3 = bf16[1,1,128,1024]{3,2,1,0:T(8,128)(2,1)} fusion(f32[1,1,128,1024]{3,2,1,0:T(8,128)S(1)} %mul.84, f32[1,1,128,1024]{3,2,1,0:T(8,128)S(1)} %mul.96, bf16[1,1,128,1024]{3,2,1,0:T(8,128)(2,1)S(1)} %copy-done.1, f32[2,128,1024]{2,1,0:T(8,128)S(1)} %copy-done.2, f32[1024]{0:T(1024)S(1)} %broadcast_bitcast_fusion, ...), kind=kLoop, calls=%fused_computation.5 | loop fusion | flops 1179648 | bytes 2363392 | tf_op jit(solution)/shard_map/convert_element_type | solution.py:152
  (5 shorter events, 0.1 us)
Async XLA Ops:
  0.6 6.4 %copy-start.5 = (bf16[1,1,128,2048]{3,2,1,0:T(8,128)(2,1)S(1)}, bf16[1,1,128,2048]{3,2,1,0:T(8,128)(2,1)}, u32[]{:S(2)}) copy-start(bf16[1,1,128,2048]{3,2,1,0:T(8,128)(2,1)} %param.10) | copy-start | bytes 1572868
  0.6 9.7 %copy-start = (bf16[1,1,128,1024]{3,2,1,0:T(8,128)(2,1)S(1)}, bf16[1,1,128,1024]{3,2,1,0:T(8,128)(2,1)}, u32[]{:S(2)}) copy-start(bf16[1,1,128,1024]{3,2,1,0:T(8,128)(2,1)} %param.8) | copy-start | bytes 786436
  1.8 16.4 %collective-permute-start = (bf16[2,128,1024]{2,1,0:T(8,128)(2,1)S(1)}, bf16[2,128,1024]{2,1,0:T(8,128)(2,1)S(1)}, u32[]{:S(2)}, u32[]{:S(2)}) collective-permute-start(bf16[2,128,1024]{2,1,0:T(8,128)(2,1)S(1)} %pad_maximum_fusion), channel_id=1, source_target_pairs={{0,1},{1,2},{2,3},{3,4},{4,5},{5,6},{6,7},{8,9},{9,10},{10,11},{11... | collective-permute-start | bytes 1572872 | tf_op jit(solution)/shard_map/ppermute | solution.py:24
  7.0 11.1 %collective-permute-start.1 = (bf16[128,2048]{1,0:T(8,128)(2,1)S(1)}, bf16[128,2048]{1,0:T(8,128)(2,1)}, u32[]{:S(2)}, u32[]{:S(2)}) collective-permute-start(bf16[128,2048]{1,0:T(8,128)(2,1)S(1)} %bitcast.36), channel_id=1, source_target_pairs={{0,56},{8,0},{16,8},{24,16},{32,24},{40,32},{48,40},{56,48},{1,57}... | collective-permute-start | bytes 1572872 | tf_op jit(solution)/shard_map/ppermute | solution.py:136
  18.2 0.8 copy-start.6
  30.1 1.3 %copy-start.4 = (f32[2,128]{1,0:T(2,128)S(1)}, f32[2,128]{1,0:T(2,128)}, u32[]{:S(2)}) copy-start(f32[2,128]{1,0:T(2,128)} %get-tuple-element.12) | copy-start | bytes 3076
  30.1 48.2 %collective-permute-start.2 = (bf16[2,128,1024]{2,1,0:T(8,128)(2,1)}, bf16[2,128,1024]{2,1,0:T(8,128)(2,1)S(1)}, u32[]{:S(2)}, u32[]{:S(2)}) collective-permute-start(bf16[2,128,1024]{2,1,0:T(8,128)(2,1)} %get-tuple-element.11), channel_id=1, source_target_pairs={{1,0},{2,1},{3,2},{4,3},{5,4},{6,5},{7,6},{9,8},{10,9},{11,10},{12... | collective-permute-start | bytes 1572872 | tf_op jit(solution)/shard_map/ppermute | solution.py:24
  32.1 46.2 %copy-start.2 = (f32[2,128,1024]{2,1,0:T(8,128)S(1)}, f32[2,128,1024]{2,1,0:T(8,128)}, u32[]{:S(2)}) copy-start(f32[2,128,1024]{2,1,0:T(8,128)} %get-tuple-element.10) | copy-start | bytes 3145732
  32.1 45.5 %all-to-all-start = ((f32[128,2,128]{2,1,0:T(2,128)}), f32[128,2,128]{2,1,0:T(2,128)S(1)}, u32[]{:S(2)}, u32[]{:S(2)}) async-start(f32[128,2,128]{2,1,0:T(2,128)} %broadcast_in_dim.2), calls=%async_computation | async-start | bytes 262144 | tf_op jit(solution)/shard_map/all_to_all | solution.py:18
  60.7 0.7 copy-start.3
  79.8 1.0 %copy-start.1 = (bf16[1,1,128,1024]{3,2,1,0:T(8,128)(2,1)S(1)}, bf16[1,1,128,1024]{3,2,1,0:T(8,128)(2,1)}, u32[]{:S(2)}) copy-start(bf16[1,1,128,1024]{3,2,1,0:T(8,128)(2,1)} %param.8) | copy-start | bytes 786436

commit v5 on v4

--- a/solution.py
+++ b/solution.py
@@ -36,75 +36,89 @@
     return inverse * centered
 
 
-def window_kernel(ratio, head_dim, lo_ref, qgain_ref, kgain_ref, q_ref, k_ref, v_ref, halo_ref, up_ref,
+def window_kernel(ratio, head_dim, per_step, lo_ref, qgain_ref, kgain_ref, q_ref, k_ref, v_ref, halo_ref, up_ref,
                   qgrad_ref, own_ref, send_ref, gains_ref):
-    rows = q_ref.shape[0]
-    qgain = qgain_ref[...]
-    kgain = kgain_ref[...]
-    key_raw = jnp.concatenate([halo_ref[0], k_ref[...]], axis=0).astype(jnp.float32)
-    values = jnp.concatenate([halo_ref[1], v_ref[...]], axis=0)
-    keys = key_raw.shape[0]
-    key_unit, _, key_normed = normalize(key_raw, kgain)
-    col = lax.broadcasted_iota(jnp.int32, (rows, keys), 1)
-    row = lax.broadcasted_iota(jnp.int32, (rows, keys), 0)
-    visible = (col >= lo_ref[...]) & (col <= row + (keys - rows))
-    dk = jnp.zeros((keys, head_dim), jnp.float32)
-    dv = jnp.zeros((keys, head_dim), jnp.float32)
-    qterm = jnp.zeros((1, head_dim), jnp.float32)
-    for h in range(ratio):
-        cols = slice(h * head_dim, (h + 1) * head_dim)
-        query_unit, query_inverse, q = normalize(q_ref[:, cols].astype(jnp.float32), qgain)
-        up = up_ref[:, cols]
-        scores = lax.dot_general(q, key_normed, (((1,), (1,)), ((), ())), preferred_element_type=jnp.float32) * score_scale
-        exp_scores = jnp.where(visible, jnp.exp(scores), 0.0)
-        weights = exp_scores / jnp.sum(exp_scores, axis=-1, keepdims=True)
-        weights_low = weights.astype(jnp.bfloat16)
-        attended = jnp.dot(weights_low, values, preferred_element_type=jnp.float32)
-        delta = jnp.sum(up.astype(jnp.float32) * attended, axis=-1, keepdims=True)
-        prob_grad = lax.dot_general(up, values, (((1,), (1,)), ((), ())), preferred_element_type=jnp.float32)
-        score_grad = weights * (prob_grad - delta) * score_scale
-        dq = jnp.dot(score_grad.astype(jnp.bfloat16), key_normed, preferred_element_type=jnp.float32)
-        qgrad_ref[:, cols] = norm_back(dq, query_unit, query_inverse, qgain).astype(qgrad_ref.dtype)
-        qterm = qterm + jnp.sum(dq * query_unit, axis=0, keepdims=True)
-        dk = dk + jnp.dot(score_grad.T.astype(jnp.bfloat16), q, preferred_element_type=jnp.float32)
-        dv = dv + jnp.dot(weights.T.astype(jnp.bfloat16), up, preferred_element_type=jnp.float32)
-    kterm = jnp.sum(dk * key_unit, axis=0, keepdims=True)
-    own_ref[0] = dk[rows:]
-    own_ref[1] = dv[rows:]
-    send_ref[0] = dk[:rows].astype(send_ref.dtype)
-    send_ref[1] = dv[:rows].astype(send_ref.dtype)
-
     @pl.when(pl.program_id(0) == 0)
     def _():
         gains_ref[...] = jnp.zeros_like(gains_ref)
 
+    for g in range(per_step):
+        one_group(ratio, head_dim, g, lo_ref, qgain_ref, kgain_ref, q_ref, k_ref, v_ref, halo_ref, up_ref,
+                  qgrad_ref, own_ref, send_ref, gains_ref)
+
+
+def one_group(ratio, head_dim, g, lo_ref, qgain_ref, kgain_ref, q_ref, k_ref, v_ref, halo_ref, up_ref,
+              qgrad_ref, own_ref, send_ref, gains_ref):
+    rows = q_ref.shape[0]
+    qgain = qgain_ref[...]
+    kgain = kgain_ref[...]
+    kc = slice(g * head_dim, (g + 1) * head_dim)
+    key_raw = jnp.concatenate([halo_ref[0, :, kc], k_ref[:, kc]], axis=0).astype(jnp.float32)
+    values = jnp.concatenate([halo_ref[1, :, kc], v_ref[:, kc]], axis=0)
+    keys = key_raw.shape[0]
+    key_unit, _, key_normed = normalize(key_raw, kgain)
+    heads = [slice((g * ratio + h) * head_dim, (g * ratio + h + 1) * head_dim) for h in range(ratio)]
+    query_unit, query_inverse, q = normalize(
+        jnp.concatenate([q_ref[:, c] for c in heads], axis=0).astype(jnp.float32), qgain
+    )
+    up = jnp.concatenate([up_ref[:, c] for c in heads], axis=0)
+    stacked = ratio * rows
+    col = lax.broadcasted_iota(jnp.int32, (stacked, keys), 1)
+    row = lax.broadcasted_iota(jnp.int32, (stacked, keys), 0) % rows
+    lo = jnp.concatenate([lo_ref[...]] * ratio, axis=0)
+    visible = (col >= lo) & (col <= row + (keys - rows))
+    scores = lax.dot_general(q, key_normed, (((1,), (1,)), ((), ())), preferred_element_type=jnp.float32) * score_scale
+    exp_scores = jnp.where(visible, jnp.exp(scores), 0.0)
+    weights = exp_scores / jnp.sum(exp_scores, axis=-1, keepdims=True)
+    weights_low = weights.astype(jnp.bfloat16)
+    attended = jnp.dot(weights_low, values, preferred_element_type=jnp.float32)
+    delta = jnp.sum(up.astype(jnp.float32) * attended, axis=-1, keepdims=True)
+    prob_grad = lax.dot_general(up, values, (((1,), (1,)), ((), ())), preferred_element_type=jnp.float32)
+    score_grad = weights * (prob_grad - delta) * score_scale
+    dq = jnp.dot(score_grad.astype(jnp.bfloat16), key_normed, preferred_element_type=jnp.float32)
+    query_grad = norm_back(dq, query_unit, query_inverse, qgain).astype(qgrad_ref.dtype)
+    for h, c in enumerate(heads):
+        qgrad_ref[:, c] = query_grad[h * rows:(h + 1) * rows]
+    qterm = jnp.sum(dq * query_unit, axis=0, keepdims=True)
+    dk = jnp.dot(score_grad.T.astype(jnp.bfloat16), q, preferred_element_type=jnp.float32)
+    dv = jnp.dot(weights.T.astype(jnp.bfloat16), up, preferred_element_type=jnp.float32)
+    kterm = jnp.sum(dk * key_unit, axis=0, keepdims=True)
+    own_ref[0, :, kc] = dk[rows:]
+    own_ref[1, :, kc] = dv[rows:]
+    send_ref[0, :, kc] = dk[:rows].astype(send_ref.dtype)
+    send_ref[1, :, kc] = dv[:rows].astype(send_ref.dtype)
     gains_ref[...] += jnp.concatenate([qterm, kterm], axis=0)
+
+
+GROUPS_PER_STEP = 1
 
 
 def window_attention(lo_rel, query_gain, key_gain, query_local, key_local, value_local, halo, upstream, ratio, head_dim):
     rows, query_width = query_local.shape
     key_width = key_local.shape[1]
-    groups = key_width // head_dim
-    qw = ratio * head_dim
+    per_step = GROUPS_PER_STEP
+    groups = key_width // (head_dim * per_step)
+    kw = head_dim * per_step
+    qw = ratio * kw
     keys = 2 * rows
-    flops = 12 * rows * keys * head_dim * ratio * groups
+    flops = 12 * rows * keys * head_dim * ratio * groups * per_step
     return pl.pallas_call(
-        functools.partial(window_kernel, ratio, head_dim),
+        functools.partial(window_kernel, ratio, head_dim, per_step),
         grid=(groups,),
         in_specs=[
             pl.BlockSpec((rows, 1), lambda g: (0, 0)),
             pl.BlockSpec((1, head_dim), lambda g: (0, 0)),
             pl.BlockSpec((1, head_dim), lambda g: (0, 0)),
             pl.BlockSpec((rows, qw), lambda g: (0, g)),
-            pl.BlockSpec((rows, head_dim), lambda g: (0, g)),
-            pl.BlockSpec((rows, head_dim), lambda g: (0, g)),
-            pl.BlockSpec((2, rows, head_dim), lambda g: (0, 0, g)),
+            pl.BlockSpec((rows, kw), lambda g: (0, g)),
+            pl.BlockSpec((rows, kw), lambda g: (0, g)),
+            pl.BlockSpec((2, rows, kw), lambda g: (0, 0, g)),
             pl.BlockSpec((rows, qw), lambda g: (0, g)),
         ],
         out_specs=[
             pl.BlockSpec((rows, qw), lambda g: (0, g)),
-            pl.BlockSpec((2, rows, head_dim), lambda g: (0, 0, g)),
-            pl.BlockSpec((2, rows, head_dim), lambda g: (0, 0, g)),
+            pl.BlockSpec((2, rows, kw), lambda g: (0, 0, g)),
+            pl.BlockSpec((2, rows, kw), lambda g: (0, 0, g)),
             pl.BlockSpec((2, head_dim), lambda g: (0, 0)),
         ],
         out_shape=[
@@ -115,7 +129,7 @@
         ],
         cost_estimate=pl.CostEstimate(
             flops=flops,
-            transcendentals=rows * keys * ratio * groups,
+            transcendentals=rows * keys * ratio * groups * per_step,
             bytes_accessed=2 * (4 * rows * query_width + 6 * rows * key_width) + 8 * rows * key_width,
         ),
     )(lo_rel, query_gain, key_gain, query_local, key_local, value_local, halo, upstream)

time: 82 us -> 80.5 us (0.982)
  Pallas kernels: 11.1 us -> 9.19 us
    pallas_call x1, Pallas kernels: 11.1 us -> 9.19 us  [window_attention(): pl.pallas_call(functools.partial(window_kernel, ratio, head_dim, per_step...]
where the time goes in v5:
time: 80.5 us; the launch traced here: 79.8 us
  starting transfers between devices  36.7 us (46%)
  waiting for transfers between devices  23.7 us (29%)
  Pallas kernels  9.19 us (11%)
  local copies, waits for them, and re-layouts  5.03 us (6%)
  other arithmetic  4.37 us (5%)
    all_to_all x1, starting transfers between devices, summed_over(): return jnp.sum(lax.all_to_all(copies, axes, 0, 0, tiled=True), axis=0)  28.3 us
    all_to_all x1, waiting for transfers between devices, summed_over(): return jnp.sum(lax.all_to_all(copies, axes, 0, 0, tiled=True), axis=0)  16.2 us
    pallas_call x1, Pallas kernels, window_attention(): pl.pallas_call(functools.partial(window_kernel, ratio, head_dim, per_step...  9.19 us
    ppermute x2, waiting for transfers between devices, shifted(): return lax.ppermute(x, axis, pairs)  7.42 us
    ppermute x2, starting transfers between devices, shifted(): return lax.ppermute(x, axis, pairs)  6.51 us
    unnamed x16, local copies, waits for them, and re-layouts  2.51 us
    ppermute x1, starting transfers between devices, on_device(): lax.ppermute(out_grad.reshape(rows, query_width), 'pipe', [(i, (i - 1) %...  1.92 us
  transfers between devices with their start and end apart: 4, of which 2 were waited for; matrix products, arithmetic and copies ran while one was open for 4% of the time, Pallas kernels for 0%

profile of v5, /device:TPU:2, one launch (start us, length us, event | category | flops | bytes accessed | tf_op | source)
XLA Modules:
  0.0 79.8 jit_solution(6170707780616347525)
XLA Ops:
  0.6 0.0 copy-start.5
  0.6 0.0 copy-start
  0.7 1.1 %pad_maximum_fusion = bf16[2,128,1024]{2,1,0:T(8,128)(2,1)S(1)} fusion(bf16[1,128,1024]{2,1,0:T(8,128)(2,1)} %bitcast.32, bf16[1,128,1024]{2,1,0:T(8,128)(2,1)} %bitcast.30), kind=kLoop, calls=%fused_computation.7 | loop fusion | flops 262144 | bytes 1048576 | tf_op jit(solution)/shard_map/stack | solution.py:153
  1.8 5.2 %collective-permute-start = (bf16[2,128,1024]{2,1,0:T(8,128)(2,1)S(1)}, bf16[2,128,1024]{2,1,0:T(8,128)(2,1)S(1)}, u32[]{:S(2)}, u32[]{:S(2)}) collective-permute-start(bf16[2,128,1024]{2,1,0:T(8,128)(2,1)S(1)} %pad_maximum_fusion), channel_id=1, source_target_pairs={{0,1},{1,2},{2,3},{3,4},{4,5},{5,6},{6,7},{8,9},{9,10},{10,11},{11... | collective-permute-start | bytes 1572872 | tf_op jit(solution)/shard_map/ppermute | solution.py:24
  7.0 0.0 copy-done.5
  7.0 1.9 %collective-permute-start.1 = (bf16[128,2048]{1,0:T(8,128)(2,1)S(1)}, bf16[128,2048]{1,0:T(8,128)(2,1)}, u32[]{:S(2)}, u32[]{:S(2)}) collective-permute-start(bf16[128,2048]{1,0:T(8,128)(2,1)S(1)} %bitcast.36), channel_id=1, source_target_pairs={{0,56},{8,0},{16,8},{24,16},{32,24},{40,32},{48,40},{56,48},{1,57}... | collective-permute-start | bytes 1572872 | tf_op jit(solution)/shard_map/ppermute | solution.py:150
  9.0 0.7 subtract_bitcast_fusion
  9.6 0.7 copy.14.lo_ref
  10.4 0.0 copy-done
  10.4 0.1 copy.19
  10.5 0.2 multiply_reduce_fusion.1
  10.8 7.4 %collective-permute-done.halo_ref = bf16[2,128,1024]{2,1,0:T(8,128)(2,1)S(1)} collective-permute-done((bf16[2,128,1024]{2,1,0:T(8,128)(2,1)S(1)}, bf16[2,128,1024]{2,1,0:T(8,128)(2,1)S(1)}, u32[]{:S(2)}, u32[]{:S(2)}) %collective-permute-start) | collective-permute-done | bytes 524320 | tf_op jit(solution)/shard_map/ppermute | solution.py:24
  18.2 0.0 copy-start.6
  18.2 0.0 collective-permute-done.1.up_ref
  18.2 0.8 copy-done.6
  19.0 9.2 %shard_map.110 = (bf16[128,2048]{1,0:T(8,128)(2,1)}, f32[2,128,1024]{2,1,0:T(8,128)}, bf16[2,128,1024]{2,1,0:T(8,128)(2,1)}, f32[2,128]{1,0:T(2,128)}) custom-call(s32[128,1]{1,0:T(8,128)} %copy.14.lo_ref, f32[1,128]{1,0:T(1,128)} %qgain_ref.1, f32[1,128]{1,0:T(1,128)} %kgain_ref.1, bf16[128,2048]{1,0:T(8,128)(2,1)} %bitcast.37, bf16[128,1024]{1,0:T(8,128)(2,1)} %bitcast.31, ...), custom_call_target="tpu_custom_call" | custom-call | flops 805306368 | bytes 4718592 | tf_op jit(solution)/shard_map/pallas_call | solution.py:105
  28.2 0.0 copy-start.4
  28.2 1.3 %collective-permute-start.2 = (bf16[2,128,1024]{2,1,0:T(8,128)(2,1)}, bf16[2,128,1024]{2,1,0:T(8,128)(2,1)S(1)}, u32[]{:S(2)}, u32[]{:S(2)}) collective-permute-start(bf16[2,128,1024]{2,1,0:T(8,128)(2,1)} %get-tuple-element.11), channel_id=1, source_target_pairs={{1,0},{2,1},{3,2},{4,3},{5,4},{6,5},{7,6},{9,8},{10,9},{11,10},{12... | collective-permute-start | bytes 1572872 | tf_op jit(solution)/shard_map/ppermute | solution.py:24
  29.5 0.0 copy-done.4
  29.5 0.7 broadcast_in_dim.2
  30.2 0.0 copy-start.2
  30.2 28.3 %all-to-all-start = ((f32[128,2,128]{2,1,0:T(2,128)}), f32[128,2,128]{2,1,0:T(2,128)S(1)}, u32[]{:S(2)}, u32[]{:S(2)}) async-start(f32[128,2,128]{2,1,0:T(2,128)} %broadcast_in_dim.2), calls=%async_computation | async-start | bytes 262144 | tf_op jit(solution)/shard_map/all_to_all | solution.py:18
  58.5 0.2 mul.83
  58.7 0.1 mul.84
  58.8 0.0 copy-start.3
  58.8 0.6 copy-done.3
  59.4 16.2 %all-to-all-done = f32[128,2,128]{2,1,0:T(2,128)S(1)} async-done(((f32[128,2,128]{2,1,0:T(2,128)}), f32[128,2,128]{2,1,0:T(2,128)S(1)}, u32[]{:S(2)}, u32[]{:S(2)}) %all-to-all-start) | async-done | bytes 131104 | tf_op jit(solution)/shard_map/all_to_all | solution.py:18
  75.7 0.1 reduce_sum.29
  75.8 0.5 fusion.6
  76.3 0.0 collective-permute-done.2
  76.3 0.0 copy-done.2
  76.3 0.8 %fusion.5 = (bf16[1,1,128,1024]{3,2,1,0:T(8,128)(2,1)}, f32[16,8,8,128]{3,1,2,0:T(8,128)S(1)}) fusion(f32[2,128,1024]{2,1,0:T(8,128)S(1)} %copy-done.2, bf16[2,128,1024]{2,1,0:T(8,128)(2,1)S(1)} %collective-permute-done.2), kind=kLoop, calls=%fused_computation.14 | loop fusion | flops 655360 | bytes 2359296 | tf_op jit(solution)/shard_map/convert_element_type | solution.py:167
  77.2 0.1 copy.20
  77.3 0.4 multiply_reduce_fusion
  77.7 0.2 mul.95
  77.9 0.0 copy-start.1
  77.9 0.1 mul.96
  78.0 0.9 %copy-done.1 = bf16[1,1,128,1024]{3,2,1,0:T(8,128)(2,1)S(1)} copy-done((bf16[1,1,128,1024]{3,2,1,0:T(8,128)(2,1)S(1)}, bf16[1,1,128,1024]{3,2,1,0:T(8,128)(2,1)}, u32[]{:S(2)}) %copy-start.1) | copy-done | bytes 262168
  78.9 0.9 %fusion.3 = bf16[1,1,128,1024]{3,2,1,0:T(8,128)(2,1)} fusion(f32[1,1,128,1024]{3,2,1,0:T(8,128)S(1)} %mul.84, f32[1,1,128,1024]{3,2,1,0:T(8,128)S(1)} %mul.96, bf16[1,1,128,1024]{3,2,1,0:T(8,128)(2,1)S(1)} %copy-done.1, f32[2,128,1024]{2,1,0:T(8,128)S(1)} %copy-done.2, f32[1024]{0:T(1024)S(1)} %broadcast_bitcast_fusion, ...), kind=kLoop, calls=%fused_computation.5 | loop fusion | flops 1179648 | bytes 2363392 | tf_op jit(solution)/shard_map/convert_element_type | solution.py:166
  (5 shorter events, 0.1 us)
Async XLA Ops:
  0.6 6.4 %copy-start.5 = (bf16[1,1,128,2048]{3,2,1,0:T(8,128)(2,1)S(1)}, bf16[1,1,128,2048]{3,2,1,0:T(8,128)(2,1)}, u32[]{:S(2)}) copy-start(bf16[1,1,128,2048]{3,2,1,0:T(8,128)(2,1)} %param.10) | copy-start | bytes 1572868
  0.6 9.7 %copy-start = (bf16[1,1,128,1024]{3,2,1,0:T(8,128)(2,1)S(1)}, bf16[1,1,128,1024]{3,2,1,0:T(8,128)(2,1)}, u32[]{:S(2)}) copy-start(bf16[1,1,128,1024]{3,2,1,0:T(8,128)(2,1)} %param.8) | copy-start | bytes 786436
  1.8 16.4 %collective-permute-start = (bf16[2,128,1024]{2,1,0:T(8,128)(2,1)S(1)}, bf16[2,128,1024]{2,1,0:T(8,128)(2,1)S(1)}, u32[]{:S(2)}, u32[]{:S(2)}) collective-permute-start(bf16[2,128,1024]{2,1,0:T(8,128)(2,1)S(1)} %pad_maximum_fusion), channel_id=1, source_target_pairs={{0,1},{1,2},{2,3},{3,4},{4,5},{5,6},{6,7},{8,9},{9,10},{10,11},{11... | collective-permute-start | bytes 1572872 | tf_op jit(solution)/shard_map/ppermute | solution.py:24
  7.0 11.1 %collective-permute-start.1 = (bf16[128,2048]{1,0:T(8,128)(2,1)S(1)}, bf16[128,2048]{1,0:T(8,128)(2,1)}, u32[]{:S(2)}, u32[]{:S(2)}) collective-permute-start(bf16[128,2048]{1,0:T(8,128)(2,1)S(1)} %bitcast.36), channel_id=1, source_target_pairs={{0,56},{8,0},{16,8},{24,16},{32,24},{40,32},{48,40},{56,48},{1,57}... | collective-permute-start | bytes 1572872 | tf_op jit(solution)/shard_map/ppermute | solution.py:150
  18.2 0.8 %copy-start.6 = (bf16[2,128,1024]{2,1,0:T(8,128)(2,1)}, bf16[2,128,1024]{2,1,0:T(8,128)(2,1)S(1)}, u32[]{:S(2)}) copy-start(bf16[2,128,1024]{2,1,0:T(8,128)(2,1)S(1)} %collective-permute-done.halo_ref) | copy-start | bytes 1572868
  28.2 1.3 %copy-start.4 = (f32[2,128]{1,0:T(2,128)S(1)}, f32[2,128]{1,0:T(2,128)}, u32[]{:S(2)}) copy-start(f32[2,128]{1,0:T(2,128)} %get-tuple-element.12) | copy-start | bytes 3076
  28.2 48.2 %collective-permute-start.2 = (bf16[2,128,1024]{2,1,0:T(8,128)(2,1)}, bf16[2,128,1024]{2,1,0:T(8,128)(2,1)S(1)}, u32[]{:S(2)}, u32[]{:S(2)}) collective-permute-start(bf16[2,128,1024]{2,1,0:T(8,128)(2,1)} %get-tuple-element.11), channel_id=1, source_target_pairs={{1,0},{2,1},{3,2},{4,3},{5,4},{6,5},{7,6},{9,8},{10,9},{11,10},{12... | collective-permute-start | bytes 1572872 | tf_op jit(solution)/shard_map/ppermute | solution.py:24
  30.2 46.2 %copy-start.2 = (f32[2,128,1024]{2,1,0:T(8,128)S(1)}, f32[2,128,1024]{2,1,0:T(8,128)}, u32[]{:S(2)}) copy-start(f32[2,128,1024]{2,1,0:T(8,128)} %get-tuple-element.10) | copy-start | bytes 3145732
  30.2 45.5 %all-to-all-start = ((f32[128,2,128]{2,1,0:T(2,128)}), f32[128,2,128]{2,1,0:T(2,128)S(1)}, u32[]{:S(2)}, u32[]{:S(2)}) async-start(f32[128,2,128]{2,1,0:T(2,128)} %broadcast_in_dim.2), calls=%async_computation | async-start | bytes 262144 | tf_op jit(solution)/shard_map/all_to_all | solution.py:18
  58.8 0.7 copy-start.3
  77.9 1.0 %copy-start.1 = (bf16[1,1,128,1024]{3,2,1,0:T(8,128)(2,1)S(1)}, bf16[1,1,128,1024]{3,2,1,0:T(8,128)(2,1)}, u32[]{:S(2)}) copy-start(bf16[1,1,128,1024]{3,2,1,0:T(8,128)(2,1)} %param.8) | copy-start | bytes 786436

commit v6 on v5

--- a/solution.py
+++ b/solution.py
@@ -10,12 +10,12 @@
 score_scale = 168.0 ** (-0.5)
 
 
-def summed_over(x, axes):
+def gathered_over(x, axes):
     devices = 1
     for axis in axes:
         devices *= lax.axis_size(axis)
     copies = jnp.broadcast_to(x[None], (devices,) + x.shape)
-    return jnp.sum(lax.all_to_all(copies, axes, 0, 0, tiled=True), axis=0)
+    return lax.all_to_all(copies, axes, 0, 0, tiled=True)
 
 
 def shifted(x, axis, by):
@@ -154,17 +154,20 @@
     block = lax.axis_index("seq")
     first = block * rows
     lo_rel = (lax.dynamic_slice(lowest_key_index.reshape(-1), (first,), (rows,)) - (first - rows)).reshape(rows, 1)
+    key_scale = key_gain.reshape(head_dim)
+    key_unit, key_inverse, _ = normalize(key_local.astype(jnp.float32).reshape(rows, groups, head_dim), key_scale)
+    key_unit, key_inverse, query_local = lax.optimization_barrier((key_unit, key_inverse, query_local))
     query_grad, own, send, gain_terms = window_attention(
         lo_rel, query_gain, key_gain, query_local, key_local, value_local, halo, upstream, ratio, head_dim
     )
     back = shifted(send, "seq", -1)
-    both = summed_over(gain_terms, ("dp", "seq"))
-    key_scale = key_gain.reshape(head_dim)
-    key_unit, key_inverse, _ = normalize(key_local.astype(jnp.float32).reshape(rows, groups, head_dim), key_scale)
+    received = gathered_over(gain_terms, ("dp", "seq"))
     key_normed_grad = (own[0] + back[0].astype(jnp.float32)).reshape(rows, groups, head_dim)
     value_rows = own[1] + back[1].astype(jnp.float32)
     key_grad = norm_back(key_normed_grad, key_unit, key_inverse, key_scale).astype(jnp.bfloat16)
     value_grad = value_rows.astype(jnp.bfloat16)
+    key_grad, value_grad, received = lax.optimization_barrier((key_grad, value_grad, received))
+    both = jnp.sum(received, axis=0)
     return (
         query_grad.reshape(1, 1, rows, query_width),
         key_grad.reshape(1, 1, rows, key_width),

time: 80.5 us -> 78 us (0.969)
  waiting for transfers between devices: 23.7 us -> 21 us
    all_to_all x1, waiting for transfers between devices: 16.2 us -> 13.8 us  [gathered_over(): return lax.all_to_all(copies, axes, 0, 0, tiled=True)]
    convert_element_type x1, other arithmetic: 0.84 us -> 2.04 us  [on_device(): value_grad = value_rows.astype(jnp.bfloat16)]
    reshape x0 -> x1, local copies, waits for them, and re-layouts: none -> 0.82 us  [on_device(): key_grad.reshape(1, 1, rows, key_width)]
    unnamed x16 -> x14, local copies, waits for them, and re-layouts: 2.51 us -> 1.89 us
  transfers between devices with their start and end apart: 4 -> 4, of which waited for: 2 -> 2; matrix products, arithmetic and copies ran while one was open for 4% -> 7% of each run, Pallas kernels for 0% -> 0%
where the time goes in v6:
time: 78 us; the launch traced here: 77.3 us
  starting transfers between devices  36.6 us (47%)
  waiting for transfers between devices  21 us (27%)
  Pallas kernels  9.19 us (12%)
  other arithmetic  5.06 us (6%)
  local copies, waits for them, and re-layouts  4.66 us (6%)
  between operations  0.8 us (1%)
    all_to_all x1, starting transfers between devices, gathered_over(): return lax.all_to_all(copies, axes, 0, 0, tiled=True)  28.1 us
    all_to_all x1, waiting for transfers between devices, gathered_over(): return lax.all_to_all(copies, axes, 0, 0, tiled=True)  13.8 us
    pallas_call x1, Pallas kernels, window_attention(): pl.pallas_call(functools.partial(window_kernel, ratio, head_dim, per_step...  9.19 us
    ppermute x2, waiting for transfers between devices, shifted(): return lax.ppermute(x, axis, pairs)  7.18 us
    ppermute x2, starting transfers between devices, shifted(): return lax.ppermute(x, axis, pairs)  6.51 us
    convert_element_type x1, other arithmetic, on_device(): value_grad = value_rows.astype(jnp.bfloat16)  2.04 us
    ppermute x1, starting transfers between devices, on_device(): lax.ppermute(out_grad.reshape(rows, query_width), 'pipe', [(i, (i - 1) %...  1.92 us
    unnamed x14, local copies, waits for them, and re-layouts  1.89 us
  transfers between devices with their start and end apart: 4, of which 2 were waited for; matrix products, arithmetic and copies ran while one was open for 7% of the time, Pallas kernels for 0%

profile of v6, /device:TPU:2, one launch (start us, length us, event | category | flops | bytes accessed | tf_op | source)
XLA Modules:
  0.0 77.3 jit_solution(10967537065667334414)
XLA Ops:
  0.6 0.0 copy-start.3
  0.6 0.0 copy-start
  0.7 1.1 %pad_maximum_fusion = bf16[2,128,1024]{2,1,0:T(8,128)(2,1)S(1)} fusion(bf16[1,128,1024]{2,1,0:T(8,128)(2,1)} %bitcast.33, bf16[1,128,1024]{2,1,0:T(8,128)(2,1)} %bitcast.30), kind=kLoop, calls=%fused_computation.1 | loop fusion | flops 262144 | bytes 1048576 | tf_op jit(solution)/shard_map/stack | solution.py:153
  1.8 5.2 %collective-permute-start = (bf16[2,128,1024]{2,1,0:T(8,128)(2,1)S(1)}, bf16[2,128,1024]{2,1,0:T(8,128)(2,1)S(1)}, u32[]{:S(2)}, u32[]{:S(2)}) collective-permute-start(bf16[2,128,1024]{2,1,0:T(8,128)(2,1)S(1)} %pad_maximum_fusion), channel_id=1, source_target_pairs={{0,1},{1,2},{2,3},{3,4},{4,5},{5,6},{6,7},{8,9},{9,10},{10,11},{11... | collective-permute-start | bytes 1572872 | tf_op jit(solution)/shard_map/ppermute | solution.py:24
  7.0 0.0 copy-done.3
  7.0 1.9 %collective-permute-start.1 = (bf16[128,2048]{1,0:T(8,128)(2,1)S(1)}, bf16[128,2048]{1,0:T(8,128)(2,1)S(1)}, u32[]{:S(2)}, u32[]{:S(2)}) collective-permute-start(bf16[128,2048]{1,0:T(8,128)(2,1)S(1)} %bitcast.38), channel_id=1, source_target_pairs={{0,56},{8,0},{16,8},{24,16},{32,24},{40,32},{48,40},{56,48},{1,57}... | collective-permute-start | bytes 1572872 | tf_op jit(solution)/shard_map/ppermute | solution.py:150
  9.0 0.0 copy-done
  9.0 0.1 copy.13
  9.1 0.2 multiply_reduce_fusion.1
  9.4 0.7 subtract_bitcast_fusion
  10.0 0.7 copy.12.lo_ref
  10.8 0.2 broadcast_multiply_fusion
  11.0 7.2 %collective-permute-done.halo_ref = bf16[2,128,1024]{2,1,0:T(8,128)(2,1)S(1)} collective-permute-done((bf16[2,128,1024]{2,1,0:T(8,128)(2,1)S(1)}, bf16[2,128,1024]{2,1,0:T(8,128)(2,1)S(1)}, u32[]{:S(2)}, u32[]{:S(2)}) %collective-permute-start) | collective-permute-done | bytes 524320 | tf_op jit(solution)/shard_map/ppermute | solution.py:24
  18.2 0.0 copy-start.4
  18.2 0.0 collective-permute-done.1.up_ref
  18.2 0.0 copy-start.5
  18.2 0.8 %copy-done.4 = bf16[2,128,1024]{2,1,0:T(8,128)(2,1)} copy-done((bf16[2,128,1024]{2,1,0:T(8,128)(2,1)}, bf16[2,128,1024]{2,1,0:T(8,128)(2,1)S(1)}, u32[]{:S(2)}) %copy-start.4) | copy-done | bytes 524312
  19.0 0.2 copy-done.5
  19.2 9.2 %shard_map.110 = (bf16[128,2048]{1,0:T(8,128)(2,1)}, f32[2,128,1024]{2,1,0:T(8,128)}, bf16[2,128,1024]{2,1,0:T(8,128)(2,1)}, f32[2,128]{1,0:T(2,128)}) custom-call(s32[128,1]{1,0:T(8,128)} %copy.12.lo_ref, f32[1,128]{1,0:T(1,128)} %qgain_ref.1, f32[1,128]{1,0:T(1,128)} %kgain_ref.1, bf16[128,2048]{1,0:T(8,128)(2,1)} %bitcast.39, bf16[128,1024]{1,0:T(8,128)(2,1)} %bitcast.31, ...), custom_call_target="tpu_custom_call" | custom-call | flops 805306368 | bytes 4718592 | tf_op jit(solution)/shard_map/pallas_call | solution.py:105
  28.4 0.0 copy-start.2
  28.4 1.3 %collective-permute-start.2 = (bf16[2,128,1024]{2,1,0:T(8,128)(2,1)}, bf16[2,128,1024]{2,1,0:T(8,128)(2,1)S(1)}, u32[]{:S(2)}, u32[]{:S(2)}) collective-permute-start(bf16[2,128,1024]{2,1,0:T(8,128)(2,1)} %get-tuple-element.19), channel_id=1, source_target_pairs={{1,0},{2,1},{3,2},{4,3},{5,4},{6,5},{7,6},{9,8},{10,9},{11,10},{12... | collective-permute-start | bytes 1572872 | tf_op jit(solution)/shard_map/ppermute | solution.py:24
  29.7 0.0 copy-done.2
  29.7 0.7 broadcast_in_dim.2
  30.4 28.1 %all-to-all-start = ((f32[128,2,128]{2,1,0:T(2,128)}), f32[128,2,128]{2,1,0:T(2,128)S(1)}, u32[]{:S(2)}, u32[]{:S(2)}) async-start(f32[128,2,128]{2,1,0:T(2,128)} %broadcast_in_dim.2), calls=%async_computation | async-start | bytes 262144 | tf_op jit(solution)/shard_map/all_to_all | solution.py:18
  58.5 0.0 collective-permute-done.2
  58.6 2.0 %fusion = (bf16[128,1024]{1,0:T(8,128)(2,1)}, f32[16,8,8,128]{3,1,2,0:T(8,128)S(1)}) fusion(f32[2,128,1024]{2,1,0:T(8,128)} %get-tuple-element.18, bf16[2,128,1024]{2,1,0:T(8,128)(2,1)S(1)} %collective-permute-done.2), kind=kLoop, calls=%fused_computation.8 | loop fusion | flops 655360 | bytes 2359296 | tf_op jit(solution)/shard_map/convert_element_type | solution.py:168
  60.6 0.1 copy.14
  60.7 0.0 copy-start.1
  60.7 0.6 copy-done.1
  61.4 0.2 multiply_reduce_fusion
  61.6 0.3 multiply_convert_fusion
  62.0 13.8 %all-to-all-done = f32[128,2,128]{2,1,0:T(2,128)S(1)} async-done(((f32[128,2,128]{2,1,0:T(2,128)}), f32[128,2,128]{2,1,0:T(2,128)S(1)}, u32[]{:S(2)}, u32[]{:S(2)}) %all-to-all-start) | async-done | bytes 131104 | tf_op jit(solution)/shard_map/all_to_all | solution.py:18
  75.8 0.8 %reshape.90 = bf16[1,1,128,1024]{3,2,1,0:T(8,128)(2,1)} reshape(bf16[128,8,128]{2,1,0:T(8,128)(2,1)S(1)} %multiply_convert_fusion) | data formatting | bytes 524288 | tf_op jit(solution)/shard_map/reshape | solution.py:173
  76.6 0.1 reduce_sum.29
  76.7 0.5 fusion.2
  (4 shorter events, 0.1 us)
Async XLA Ops:
  0.6 6.4 %copy-start.3 = (bf16[1,1,128,2048]{3,2,1,0:T(8,128)(2,1)S(1)}, bf16[1,1,128,2048]{3,2,1,0:T(8,128)(2,1)}, u32[]{:S(2)}) copy-start(bf16[1,1,128,2048]{3,2,1,0:T(8,128)(2,1)} %param.10) | copy-start | bytes 1572868
  0.6 8.3 %copy-start = (bf16[1,1,128,1024]{3,2,1,0:T(8,128)(2,1)S(1)}, bf16[1,1,128,1024]{3,2,1,0:T(8,128)(2,1)}, u32[]{:S(2)}) copy-start(bf16[1,1,128,1024]{3,2,1,0:T(8,128)(2,1)} %param.8) | copy-start | bytes 786436
  1.8 16.4 %collective-permute-start = (bf16[2,128,1024]{2,1,0:T(8,128)(2,1)S(1)}, bf16[2,128,1024]{2,1,0:T(8,128)(2,1)S(1)}, u32[]{:S(2)}, u32[]{:S(2)}) collective-permute-start(bf16[2,128,1024]{2,1,0:T(8,128)(2,1)S(1)} %pad_maximum_fusion), channel_id=1, source_target_pairs={{0,1},{1,2},{2,3},{3,4},{4,5},{5,6},{6,7},{8,9},{9,10},{10,11},{11... | collective-permute-start | bytes 1572872 | tf_op jit(solution)/shard_map/ppermute | solution.py:24
  7.0 11.1 %collective-permute-start.1 = (bf16[128,2048]{1,0:T(8,128)(2,1)S(1)}, bf16[128,2048]{1,0:T(8,128)(2,1)S(1)}, u32[]{:S(2)}, u32[]{:S(2)}) collective-permute-start(bf16[128,2048]{1,0:T(8,128)(2,1)S(1)} %bitcast.38), channel_id=1, source_target_pairs={{0,56},{8,0},{16,8},{24,16},{32,24},{40,32},{48,40},{56,48},{1,57}... | collective-permute-start | bytes 1572872 | tf_op jit(solution)/shard_map/ppermute | solution.py:150
  18.2 0.8 %copy-start.4 = (bf16[2,128,1024]{2,1,0:T(8,128)(2,1)}, bf16[2,128,1024]{2,1,0:T(8,128)(2,1)S(1)}, u32[]{:S(2)}) copy-start(bf16[2,128,1024]{2,1,0:T(8,128)(2,1)S(1)} %collective-permute-done.halo_ref) | copy-start | bytes 1572868
  18.2 1.0 %copy-start.5 = (bf16[128,2048]{1,0:T(8,128)(2,1)}, bf16[128,2048]{1,0:T(8,128)(2,1)S(1)}, u32[]{:S(2)}) copy-start(bf16[128,2048]{1,0:T(8,128)(2,1)S(1)} %collective-permute-done.1.up_ref) | copy-start | bytes 1572868
  28.4 1.3 %copy-start.2 = (f32[2,128]{1,0:T(2,128)S(1)}, f32[2,128]{1,0:T(2,128)}, u32[]{:S(2)}) copy-start(f32[2,128]{1,0:T(2,128)} %get-tuple-element.21) | copy-start | bytes 3076
  28.4 30.2 %collective-permute-start.2 = (bf16[2,128,1024]{2,1,0:T(8,128)(2,1)}, bf16[2,128,1024]{2,1,0:T(8,128)(2,1)S(1)}, u32[]{:S(2)}, u32[]{:S(2)}) collective-permute-start(bf16[2,128,1024]{2,1,0:T(8,128)(2,1)} %get-tuple-element.19), channel_id=1, source_target_pairs={{1,0},{2,1},{3,2},{4,3},{5,4},{6,5},{7,6},{9,8},{10,9},{11,10},{12... | collective-permute-start | bytes 1572872 | tf_op jit(solution)/shard_map/ppermute | solution.py:24
  30.4 45.4 %all-to-all-start = ((f32[128,2,128]{2,1,0:T(2,128)}), f32[128,2,128]{2,1,0:T(2,128)S(1)}, u32[]{:S(2)}, u32[]{:S(2)}) async-start(f32[128,2,128]{2,1,0:T(2,128)} %broadcast_in_dim.2), calls=%async_computation | async-start | bytes 262144 | tf_op jit(solution)/shard_map/all_to_all | solution.py:18
  60.7 0.7 copy-start.1

commit v7 on v6

--- a/solution.py
+++ b/solution.py
@@ -36,25 +36,25 @@
     return inverse * centered
 
 
-def window_kernel(ratio, head_dim, per_step, lo_ref, qgain_ref, kgain_ref, q_ref, k_ref, v_ref, halo_ref, up_ref,
-                  qgrad_ref, own_ref, send_ref, gains_ref):
+def window_kernel(ratio, head_dim, per_step, lo_ref, qgain_ref, kgain_ref, q_ref, k_ref, v_ref, kh_ref, vh_ref,
+                  up_ref, qgrad_ref, own_ref, send_ref, gains_ref):
     @pl.when(pl.program_id(0) == 0)
     def _():
         gains_ref[...] = jnp.zeros_like(gains_ref)
 
     for g in range(per_step):
-        one_group(ratio, head_dim, g, lo_ref, qgain_ref, kgain_ref, q_ref, k_ref, v_ref, halo_ref, up_ref,
+        one_group(ratio, head_dim, g, lo_ref, qgain_ref, kgain_ref, q_ref, k_ref, v_ref, kh_ref, vh_ref, up_ref,
                   qgrad_ref, own_ref, send_ref, gains_ref)
 
 
-def one_group(ratio, head_dim, g, lo_ref, qgain_ref, kgain_ref, q_ref, k_ref, v_ref, halo_ref, up_ref,
+def one_group(ratio, head_dim, g, lo_ref, qgain_ref, kgain_ref, q_ref, k_ref, v_ref, kh_ref, vh_ref, up_ref,
               qgrad_ref, own_ref, send_ref, gains_ref):
     rows = q_ref.shape[0]
     qgain = qgain_ref[...]
     kgain = kgain_ref[...]
     kc = slice(g * head_dim, (g + 1) * head_dim)
-    key_raw = jnp.concatenate([halo_ref[0, :, kc], k_ref[:, kc]], axis=0).astype(jnp.float32)
-    values = jnp.concatenate([halo_ref[1, :, kc], v_ref[:, kc]], axis=0)
+    key_raw = jnp.concatenate([kh_ref[:, kc], k_ref[:, kc]], axis=0).astype(jnp.float32)
+    values = jnp.concatenate([vh_ref[:, kc], v_ref[:, kc]], axis=0)
     keys = key_raw.shape[0]
     key_unit, _, key_normed = normalize(key_raw, kgain)
     heads = [slice((g * ratio + h) * head_dim, (g * ratio + h + 1) * head_dim) for h in range(ratio)]
@@ -90,10 +90,11 @@
     gains_ref[...] += jnp.concatenate([qterm, kterm], axis=0)
 
 
-GROUPS_PER_STEP = 1
-
-
-def window_attention(lo_rel, query_gain, key_gain, query_local, key_local, value_local, halo, upstream, ratio, head_dim):
+GROUPS_PER_STEP = 2
+
+
+def window_attention(lo_rel, query_gain, key_gain, query_local, key_local, value_local, key_halo, value_halo, upstream,
+                     ratio, head_dim):
     rows, query_width = query_local.shape
     key_width = key_local.shape[1]
     per_step = GROUPS_PER_STEP
@@ -112,7 +113,8 @@
             pl.BlockSpec((rows, qw), lambda g: (0, g)),
             pl.BlockSpec((rows, kw), lambda g: (0, g)),
             pl.BlockSpec((rows, kw), lambda g: (0, g)),
-            pl.BlockSpec((2, rows, kw), lambda g: (0, 0, g)),
+            pl.BlockSpec((rows, kw), lambda g: (0, g)),
+            pl.BlockSpec((rows, kw), lambda g: (0, g)),
             pl.BlockSpec((rows, qw), lambda g: (0, g)),
         ],
         out_specs=[
@@ -132,7 +134,7 @@
             transcendentals=rows * keys * ratio * groups * per_step,
             bytes_accessed=2 * (4 * rows * query_width + 6 * rows * key_width) + 8 * rows * key_width,
         ),
-    )(lo_rel, query_gain, key_gain, query_local, key_local, value_local, halo, upstream)
+    )(lo_rel, query_gain, key_gain, query_local, key_local, value_local, key_halo, value_halo, upstream)
 
 
 def on_device(query_proj, key_proj, value_proj, out_grad, lowest_key_index, query_gain, key_gain):
@@ -150,7 +152,8 @@
     upstream = lax.ppermute(
         out_grad.reshape(rows, query_width), "pipe", [(i, (i - 1) % pipe_devices) for i in range(pipe_devices)]
     )
-    halo = shifted(jnp.stack([key_local, value_local]), "seq", 1)
+    key_halo = shifted(key_local, "seq", 1)
+    value_halo = shifted(value_local, "seq", 1)
     block = lax.axis_index("seq")
     first = block * rows
     lo_rel = (lax.dynamic_slice(lowest_key_index.reshape(-1), (first,), (rows,)) - (first - rows)).reshape(rows, 1)
@@ -158,7 +161,7 @@
     key_unit, key_inverse, _ = normalize(key_local.astype(jnp.float32).reshape(rows, groups, head_dim), key_scale)
     key_unit, key_inverse, query_local = lax.optimization_barrier((key_unit, key_inverse, query_local))
     query_grad, own, send, gain_terms = window_attention(
-        lo_rel, query_gain, key_gain, query_local, key_local, value_local, halo, upstream, ratio, head_dim
+        lo_rel, query_gain, key_gain, query_local, key_local, value_local, key_halo, value_halo, upstream, ratio, head_dim
     )
     back = shifted(send, "seq", -1)
     received = gathered_over(gain_terms, ("dp", "seq"))

time: 78 us -> 76.8 us (0.985)
  the two profiles are of different devices: /device:TPU:2 before, /device:TPU:1 now
where the time goes in v7:
time: 76.8 us; the launch traced here: 76.4 us
  starting transfers between devices  45.4 us (59%)
  waiting for transfers between devices  12.4 us (16%)
  Pallas kernels  8.05 us (10%)
  local copies, waits for them, and re-layouts  4.89 us (6%)
  other arithmetic  4.85 us (6%)
  between operations  0.81 us (1%)
    all_to_all x1, starting transfers between devices, gathered_over(): return lax.all_to_all(copies, axes, 0, 0, tiled=True)  25.5 us
    all_to_all x1, waiting for transfers between devices, gathered_over(): return lax.all_to_all(copies, axes, 0, 0, tiled=True)  12.1 us
    ppermute x3, starting transfers between devices, shifted(): return lax.ppermute(x, axis, pairs)  12 us
    pallas_call x1, Pallas kernels, window_attention(): pl.pallas_call(functools.partial(window_kernel, ratio, head_dim, per_step...  8.05 us
    ppermute x1, starting transfers between devices, on_device(): lax.ppermute(out_grad.reshape(rows, query_width), 'pipe', [(i, (i - 1) %...  8.01 us
    unnamed x12, local copies, waits for them, and re-layouts  2.13 us
    convert_element_type x1, other arithmetic, on_device(): value_grad = value_rows.astype(jnp.bfloat16)  2.04 us
  transfers between devices with their start and end apart: 5, of which 2 were waited for; matrix products, arithmetic and copies ran while one was open for 8% of the time, Pallas kernels for 0%

profile of v7, /device:TPU:1, one launch (start us, length us, event | category | flops | bytes accessed | tf_op | source)
XLA Modules:
  0.0 76.4 jit_solution(14126905907785804947)
XLA Ops:
  0.6 5.8 %collective-permute-start.1 = (bf16[128,1024]{1,0:T(8,128)(2,1)}, bf16[128,1024]{1,0:T(8,128)(2,1)S(1)}, u32[]{:S(2)}, u32[]{:S(2)}) collective-permute-start(bf16[128,1024]{1,0:T(8,128)(2,1)} %bitcast.36), channel_id=1, source_target_pairs={{0,1},{1,2},{2,3},{3,4},{4,5},{5,6},{6,7},{8,9},{9,10},{10,11},{11... | collective-permute-start | bytes 786440 | tf_op jit(solution)/shard_map/ppermute | solution.py:24
  6.4 4.9 %collective-permute-start = (bf16[128,1024]{1,0:T(8,128)(2,1)}, bf16[128,1024]{1,0:T(8,128)(2,1)S(1)}, u32[]{:S(2)}, u32[]{:S(2)}) collective-permute-start(bf16[128,1024]{1,0:T(8,128)(2,1)} %bitcast.28), channel_id=1, source_target_pairs={{0,1},{1,2},{2,3},{3,4},{4,5},{5,6},{6,7},{8,9},{9,10},{10,11},{11... | collective-permute-start | bytes 786440 | tf_op jit(solution)/shard_map/ppermute | solution.py:24
  11.3 8.0 %collective-permute-start.2 = (bf16[128,2048]{1,0:T(8,128)(2,1)}, bf16[128,2048]{1,0:T(8,128)(2,1)S(1)}, u32[]{:S(2)}, u32[]{:S(2)}) collective-permute-start(bf16[128,2048]{1,0:T(8,128)(2,1)} %bitcast.34), channel_id=1, source_target_pairs={{0,56},{8,0},{16,8},{24,16},{32,24},{40,32},{48,40},{56,48},{1,57}... | collective-permute-start | bytes 1572872 | tf_op jit(solution)/shard_map/ppermute | solution.py:152
  19.3 1.0 %convert_bitcast_fusion = f32[16,8,8,128]{3,1,2,0:T(8,128)S(1)} fusion(bf16[1,1,128,1024]{3,2,1,0:T(8,128)(2,1)} %param.8), kind=kLoop, calls=%fused_computation.1 | loop fusion | flops 131072 | bytes 786432
  20.3 0.1 copy.13
  20.4 0.2 multiply_reduce_fusion.1
  20.7 0.7 subtract_bitcast_fusion
  21.4 0.7 copy.12.lo_ref
  22.1 0.2 broadcast_multiply_fusion
  22.3 0.0 collective-permute-done.1.vh_ref
  22.3 0.0 copy-start.3
  22.3 0.0 collective-permute-done.kh_ref
  22.3 0.0 copy-start.4
  22.3 0.3 collective-permute-done.2.up_ref
  22.6 0.4 copy-done.3
  23.0 0.1 copy-done.4
  23.1 0.0 copy-start.2
  23.1 0.8 %copy-done.2 = bf16[128,2048]{1,0:T(8,128)(2,1)} copy-done((bf16[128,2048]{1,0:T(8,128)(2,1)}, bf16[128,2048]{1,0:T(8,128)(2,1)S(1)}, u32[]{:S(2)}) %copy-start.2) | copy-done | bytes 524312
  23.9 8.1 %shard_map.110 = (bf16[128,2048]{1,0:T(8,128)(2,1)}, f32[2,128,1024]{2,1,0:T(8,128)}, bf16[2,128,1024]{2,1,0:T(8,128)(2,1)}, f32[2,128]{1,0:T(2,128)}) custom-call(s32[128,1]{1,0:T(8,128)} %copy.12.lo_ref, f32[1,128]{1,0:T(1,128)} %qgain_ref.1, f32[1,128]{1,0:T(1,128)} %kgain_ref.1, bf16[128,2048]{1,0:T(8,128)(2,1)} %bitcast.35, bf16[128,1024]{1,0:T(8,128)(2,1)} %bitcast.29, ...), custom_call_target="tpu_custom_call" | custom-call | flops 805306368 | bytes 4718592 | tf_op jit(solution)/shard_map/pallas_call | solution.py:106
  32.0 0.0 copy-start.1
  32.0 1.3 %collective-permute-start.3 = (bf16[2,128,1024]{2,1,0:T(8,128)(2,1)}, bf16[2,128,1024]{2,1,0:T(8,128)(2,1)S(1)}, u32[]{:S(2)}, u32[]{:S(2)}) collective-permute-start(bf16[2,128,1024]{2,1,0:T(8,128)(2,1)} %get-tuple-element.19), channel_id=1, source_target_pairs={{1,0},{2,1},{3,2},{4,3},{5,4},{6,5},{7,6},{9,8},{10,9},{11,10},{12... | collective-permute-start | bytes 1572872 | tf_op jit(solution)/shard_map/ppermute | solution.py:24
  33.3 0.0 copy-done.1
  33.3 0.7 broadcast_in_dim.2
  34.0 25.5 %all-to-all-start = ((f32[128,2,128]{2,1,0:T(2,128)}), f32[128,2,128]{2,1,0:T(2,128)S(1)}, u32[]{:S(2)}, u32[]{:S(2)}) async-start(f32[128,2,128]{2,1,0:T(2,128)} %broadcast_in_dim.2), calls=%async_computation | async-start | bytes 262144 | tf_op jit(solution)/shard_map/all_to_all | solution.py:18
  59.4 0.0 collective-permute-done.3
  59.4 2.0 %fusion = (bf16[128,1024]{1,0:T(8,128)(2,1)}, f32[16,8,8,128]{3,1,2,0:T(8,128)S(1)}) fusion(f32[2,128,1024]{2,1,0:T(8,128)} %get-tuple-element.18, bf16[2,128,1024]{2,1,0:T(8,128)(2,1)S(1)} %collective-permute-done.3), kind=kLoop, calls=%fused_computation.7 | loop fusion | flops 655360 | bytes 2359296 | tf_op jit(solution)/shard_map/convert_element_type | solution.py:171
  61.5 0.1 copy.14
  61.6 0.0 copy-start
  61.6 0.6 copy-done
  62.3 0.2 multiply_reduce_fusion
  62.5 0.3 multiply_convert_fusion
  62.8 12.1 %all-to-all-done = f32[128,2,128]{2,1,0:T(2,128)S(1)} async-done(((f32[128,2,128]{2,1,0:T(2,128)}), f32[128,2,128]{2,1,0:T(2,128)S(1)}, u32[]{:S(2)}, u32[]{:S(2)}) %all-to-all-start) | async-done | bytes 131104 | tf_op jit(solution)/shard_map/all_to_all | solution.py:18
  74.9 0.8 %reshape.90 = bf16[1,1,128,1024]{3,2,1,0:T(8,128)(2,1)} reshape(bf16[128,8,128]{2,1,0:T(8,128)(2,1)S(1)} %multiply_convert_fusion) | data formatting | bytes 524288 | tf_op jit(solution)/shard_map/reshape | solution.py:176
  75.7 0.1 reduce_sum.29
  75.9 0.5 fusion.2
  (3 shorter events, 0.1 us)
Async XLA Ops:
  0.6 21.7 %collective-permute-start.1 = (bf16[128,1024]{1,0:T(8,128)(2,1)}, bf16[128,1024]{1,0:T(8,128)(2,1)S(1)}, u32[]{:S(2)}, u32[]{:S(2)}) collective-permute-start(bf16[128,1024]{1,0:T(8,128)(2,1)} %bitcast.36), channel_id=1, source_target_pairs={{0,1},{1,2},{2,3},{3,4},{4,5},{5,6},{6,7},{8,9},{9,10},{10,11},{11... | collective-permute-start | bytes 786440 | tf_op jit(solution)/shard_map/ppermute | solution.py:24
  6.4 15.9 %collective-permute-start = (bf16[128,1024]{1,0:T(8,128)(2,1)}, bf16[128,1024]{1,0:T(8,128)(2,1)S(1)}, u32[]{:S(2)}, u32[]{:S(2)}) collective-permute-start(bf16[128,1024]{1,0:T(8,128)(2,1)} %bitcast.28), channel_id=1, source_target_pairs={{0,1},{1,2},{2,3},{3,4},{4,5},{5,6},{6,7},{8,9},{9,10},{10,11},{11... | collective-permute-start | bytes 786440 | tf_op jit(solution)/shard_map/ppermute | solution.py:24
  11.3 11.3 %collective-permute-start.2 = (bf16[128,2048]{1,0:T(8,128)(2,1)}, bf16[128,2048]{1,0:T(8,128)(2,1)S(1)}, u32[]{:S(2)}, u32[]{:S(2)}) collective-permute-start(bf16[128,2048]{1,0:T(8,128)(2,1)} %bitcast.34), channel_id=1, source_target_pairs={{0,56},{8,0},{16,8},{24,16},{32,24},{40,32},{48,40},{56,48},{1,57}... | collective-permute-start | bytes 1572872 | tf_op jit(solution)/shard_map/ppermute | solution.py:152
  22.3 0.7 copy-start.3
  22.3 0.8 %copy-start.4 = (bf16[128,1024]{1,0:T(8,128)(2,1)}, bf16[128,1024]{1,0:T(8,128)(2,1)S(1)}, u32[]{:S(2)}) copy-start(bf16[128,1024]{1,0:T(8,128)(2,1)S(1)} %collective-permute-done.kh_ref) | copy-start | bytes 786436
  23.1 0.8 %copy-start.2 = (bf16[128,2048]{1,0:T(8,128)(2,1)}, bf16[128,2048]{1,0:T(8,128)(2,1)S(1)}, u32[]{:S(2)}) copy-start(bf16[128,2048]{1,0:T(8,128)(2,1)S(1)} %collective-permute-done.2.up_ref) | copy-start | bytes 1572868
  32.0 1.3 %copy-start.1 = (f32[2,128]{1,0:T(2,128)S(1)}, f32[2,128]{1,0:T(2,128)}, u32[]{:S(2)}) copy-start(f32[2,128]{1,0:T(2,128)} %get-tuple-element.21) | copy-start | bytes 3076
  32.0 27.5 %collective-permute-start.3 = (bf16[2,128,1024]{2,1,0:T(8,128)(2,1)}, bf16[2,128,1024]{2,1,0:T(8,128)(2,1)S(1)}, u32[]{:S(2)}, u32[]{:S(2)}) collective-permute-start(bf16[2,128,1024]{2,1,0:T(8,128)(2,1)} %get-tuple-element.19), channel_id=1, source_target_pairs={{1,0},{2,1},{3,2},{4,3},{5,4},{6,5},{7,6},{9,8},{10,9},{11,10},{12... | collective-permute-start | bytes 1572872 | tf_op jit(solution)/shard_map/ppermute | solution.py:24
  34.0 41.0 %all-to-all-start = ((f32[128,2,128]{2,1,0:T(2,128)}), f32[128,2,128]{2,1,0:T(2,128)S(1)}, u32[]{:S(2)}, u32[]{:S(2)}) async-start(f32[128,2,128]{2,1,0:T(2,128)} %broadcast_in_dim.2), calls=%async_computation | async-start | bytes 262144 | tf_op jit(solution)/shard_map/all_to_all | solution.py:18
  61.6 0.7 copy-start

commit v8 on v7

--- a/solution.py
+++ b/solution.py
@@ -90,7 +90,7 @@
     gains_ref[...] += jnp.concatenate([qterm, kterm], axis=0)
 
 
-GROUPS_PER_STEP = 2
+GROUPS_PER_STEP = 4
 
 
 def window_attention(lo_rel, query_gain, key_gain, query_local, key_local, value_local, key_halo, value_halo, upstream,

time: 76.8 us -> 76.5 us (level)
  no operation moved by 1% of the time
where the time goes in v8:
time: 76.5 us; the launch traced here: 76.1 us
  starting transfers between devices  45.4 us (59%)
  waiting for transfers between devices  12.4 us (16%)
  Pallas kernels  7.78 us (10%)
  local copies, waits for them, and re-layouts  4.89 us (6%)
  other arithmetic  4.85 us (6%)
  between operations  0.82 us (1%)
    all_to_all x1, starting transfers between devices, gathered_over(): return lax.all_to_all(copies, axes, 0, 0, tiled=True)  25.5 us
    all_to_all x1, waiting for transfers between devices, gathered_over(): return lax.all_to_all(copies, axes, 0, 0, tiled=True)  12.1 us
    ppermute x3, starting transfers between devices, shifted(): return lax.ppermute(x, axis, pairs)  12 us
    ppermute x1, starting transfers between devices, on_device(): lax.ppermute(out_grad.reshape(rows, query_width), 'pipe', [(i, (i - 1) %...  8.01 us
    pallas_call x1, Pallas kernels, window_attention(): pl.pallas_call(functools.partial(window_kernel, ratio, head_dim, per_step...  7.78 us
    unnamed x12, local copies, waits for them, and re-layouts  2.13 us
    convert_element_type x1, other arithmetic, on_device(): value_grad = value_rows.astype(jnp.bfloat16)  2.04 us
  transfers between devices with their start and end apart: 5, of which 2 were waited for; matrix products, arithmetic and copies ran while one was open for 8% of the time, Pallas kernels for 0%

profile of v8, /device:TPU:1, one launch (start us, length us, event | category | flops | bytes accessed | tf_op | source)
XLA Modules:
  0.0 76.1 jit_solution(11994280629911441162)
XLA Ops:
  0.6 5.8 %collective-permute-start.1 = (bf16[128,1024]{1,0:T(8,128)(2,1)}, bf16[128,1024]{1,0:T(8,128)(2,1)S(1)}, u32[]{:S(2)}, u32[]{:S(2)}) collective-permute-start(bf16[128,1024]{1,0:T(8,128)(2,1)} %bitcast.36), channel_id=1, source_target_pairs={{0,1},{1,2},{2,3},{3,4},{4,5},{5,6},{6,7},{8,9},{9,10},{10,11},{11... | collective-permute-start | bytes 786440 | tf_op jit(solution)/shard_map/ppermute | solution.py:24
  6.4 4.9 %collective-permute-start = (bf16[128,1024]{1,0:T(8,128)(2,1)}, bf16[128,1024]{1,0:T(8,128)(2,1)S(1)}, u32[]{:S(2)}, u32[]{:S(2)}) collective-permute-start(bf16[128,1024]{1,0:T(8,128)(2,1)} %bitcast.28), channel_id=1, source_target_pairs={{0,1},{1,2},{2,3},{3,4},{4,5},{5,6},{6,7},{8,9},{9,10},{10,11},{11... | collective-permute-start | bytes 786440 | tf_op jit(solution)/shard_map/ppermute | solution.py:24
  11.3 8.0 %collective-permute-start.2 = (bf16[128,2048]{1,0:T(8,128)(2,1)}, bf16[128,2048]{1,0:T(8,128)(2,1)S(1)}, u32[]{:S(2)}, u32[]{:S(2)}) collective-permute-start(bf16[128,2048]{1,0:T(8,128)(2,1)} %bitcast.34), channel_id=1, source_target_pairs={{0,56},{8,0},{16,8},{24,16},{32,24},{40,32},{48,40},{56,48},{1,57}... | collective-permute-start | bytes 1572872 | tf_op jit(solution)/shard_map/ppermute | solution.py:152
  19.3 1.0 %convert_bitcast_fusion = f32[16,8,8,128]{3,1,2,0:T(8,128)S(1)} fusion(bf16[1,1,128,1024]{3,2,1,0:T(8,128)(2,1)} %param.8), kind=kLoop, calls=%fused_computation.1 | loop fusion | flops 131072 | bytes 786432
  20.3 0.1 copy.13
  20.4 0.2 multiply_reduce_fusion.1
  20.7 0.7 subtract_bitcast_fusion
  21.4 0.7 copy.12.lo_ref
  22.1 0.2 broadcast_multiply_fusion
  22.3 0.0 collective-permute-done.1.vh_ref
  22.3 0.0 copy-start.3
  22.3 0.0 collective-permute-done.kh_ref
  22.3 0.0 copy-start.4
  22.3 0.3 collective-permute-done.2.up_ref
  22.6 0.4 copy-done.3
  23.0 0.1 copy-done.4
  23.1 0.0 copy-start.2
  23.1 0.8 %copy-done.2 = bf16[128,2048]{1,0:T(8,128)(2,1)} copy-done((bf16[128,2048]{1,0:T(8,128)(2,1)}, bf16[128,2048]{1,0:T(8,128)(2,1)S(1)}, u32[]{:S(2)}) %copy-start.2) | copy-done | bytes 524312
  23.9 7.8 %shard_map.110 = (bf16[128,2048]{1,0:T(8,128)(2,1)}, f32[2,128,1024]{2,1,0:T(8,128)}, bf16[2,128,1024]{2,1,0:T(8,128)(2,1)}, f32[2,128]{1,0:T(2,128)}) custom-call(s32[128,1]{1,0:T(8,128)} %copy.12.lo_ref, f32[1,128]{1,0:T(1,128)} %qgain_ref.1, f32[1,128]{1,0:T(1,128)} %kgain_ref.1, bf16[128,2048]{1,0:T(8,128)(2,1)} %bitcast.35, bf16[128,1024]{1,0:T(8,128)(2,1)} %bitcast.29, ...), custom_call_target="tpu_custom_call" | custom-call | flops 805306368 | bytes 4718592 | tf_op jit(solution)/shard_map/pallas_call | solution.py:106
  31.7 0.0 copy-start.1
  31.7 1.3 %collective-permute-start.3 = (bf16[2,128,1024]{2,1,0:T(8,128)(2,1)}, bf16[2,128,1024]{2,1,0:T(8,128)(2,1)S(1)}, u32[]{:S(2)}, u32[]{:S(2)}) collective-permute-start(bf16[2,128,1024]{2,1,0:T(8,128)(2,1)} %get-tuple-element.19), channel_id=1, source_target_pairs={{1,0},{2,1},{3,2},{4,3},{5,4},{6,5},{7,6},{9,8},{10,9},{11,10},{12... | collective-permute-start | bytes 1572872 | tf_op jit(solution)/shard_map/ppermute | solution.py:24
  33.0 0.0 copy-done.1
  33.0 0.7 broadcast_in_dim.2
  33.7 25.5 %all-to-all-start = ((f32[128,2,128]{2,1,0:T(2,128)}), f32[128,2,128]{2,1,0:T(2,128)S(1)}, u32[]{:S(2)}, u32[]{:S(2)}) async-start(f32[128,2,128]{2,1,0:T(2,128)} %broadcast_in_dim.2), calls=%async_computation | async-start | bytes 262144 | tf_op jit(solution)/shard_map/all_to_all | solution.py:18
  59.2 0.0 collective-permute-done.3
  59.2 2.0 %fusion = (bf16[128,1024]{1,0:T(8,128)(2,1)}, f32[16,8,8,128]{3,1,2,0:T(8,128)S(1)}) fusion(f32[2,128,1024]{2,1,0:T(8,128)} %get-tuple-element.18, bf16[2,128,1024]{2,1,0:T(8,128)(2,1)S(1)} %collective-permute-done.3), kind=kLoop, calls=%fused_computation.7 | loop fusion | flops 655360 | bytes 2359296 | tf_op jit(solution)/shard_map/convert_element_type | solution.py:171
  61.2 0.1 copy.14
  61.3 0.0 copy-start
  61.3 0.6 copy-done
  62.0 0.2 multiply_reduce_fusion
  62.2 0.3 multiply_convert_fusion
  62.6 12.1 %all-to-all-done = f32[128,2,128]{2,1,0:T(2,128)S(1)} async-done(((f32[128,2,128]{2,1,0:T(2,128)}), f32[128,2,128]{2,1,0:T(2,128)S(1)}, u32[]{:S(2)}, u32[]{:S(2)}) %all-to-all-start) | async-done | bytes 131104 | tf_op jit(solution)/shard_map/all_to_all | solution.py:18
  74.7 0.8 %reshape.90 = bf16[1,1,128,1024]{3,2,1,0:T(8,128)(2,1)} reshape(bf16[128,8,128]{2,1,0:T(8,128)(2,1)S(1)} %multiply_convert_fusion) | data formatting | bytes 524288 | tf_op jit(solution)/shard_map/reshape | solution.py:176
  75.5 0.1 reduce_sum.29
  75.6 0.5 fusion.2
  (3 shorter events, 0.1 us)
Async XLA Ops:
  0.6 21.7 %collective-permute-start.1 = (bf16[128,1024]{1,0:T(8,128)(2,1)}, bf16[128,1024]{1,0:T(8,128)(2,1)S(1)}, u32[]{:S(2)}, u32[]{:S(2)}) collective-permute-start(bf16[128,1024]{1,0:T(8,128)(2,1)} %bitcast.36), channel_id=1, source_target_pairs={{0,1},{1,2},{2,3},{3,4},{4,5},{5,6},{6,7},{8,9},{9,10},{10,11},{11... | collective-permute-start | bytes 786440 | tf_op jit(solution)/shard_map/ppermute | solution.py:24
  6.4 15.9 %collective-permute-start = (bf16[128,1024]{1,0:T(8,128)(2,1)}, bf16[128,1024]{1,0:T(8,128)(2,1)S(1)}, u32[]{:S(2)}, u32[]{:S(2)}) collective-permute-start(bf16[128,1024]{1,0:T(8,128)(2,1)} %bitcast.28), channel_id=1, source_target_pairs={{0,1},{1,2},{2,3},{3,4},{4,5},{5,6},{6,7},{8,9},{9,10},{10,11},{11... | collective-permute-start | bytes 786440 | tf_op jit(solution)/shard_map/ppermute | solution.py:24
  11.3 11.3 %collective-permute-start.2 = (bf16[128,2048]{1,0:T(8,128)(2,1)}, bf16[128,2048]{1,0:T(8,128)(2,1)S(1)}, u32[]{:S(2)}, u32[]{:S(2)}) collective-permute-start(bf16[128,2048]{1,0:T(8,128)(2,1)} %bitcast.34), channel_id=1, source_target_pairs={{0,56},{8,0},{16,8},{24,16},{32,24},{40,32},{48,40},{56,48},{1,57}... | collective-permute-start | bytes 1572872 | tf_op jit(solution)/shard_map/ppermute | solution.py:152
  22.3 0.7 copy-start.3
  22.3 0.8 %copy-start.4 = (bf16[128,1024]{1,0:T(8,128)(2,1)}, bf16[128,1024]{1,0:T(8,128)(2,1)S(1)}, u32[]{:S(2)}) copy-start(bf16[128,1024]{1,0:T(8,128)(2,1)S(1)} %collective-permute-done.kh_ref) | copy-start | bytes 786436
  23.1 0.8 %copy-start.2 = (bf16[128,2048]{1,0:T(8,128)(2,1)}, bf16[128,2048]{1,0:T(8,128)(2,1)S(1)}, u32[]{:S(2)}) copy-start(bf16[128,2048]{1,0:T(8,128)(2,1)S(1)} %collective-permute-done.2.up_ref) | copy-start | bytes 1572868
  31.7 1.3 %copy-start.1 = (f32[2,128]{1,0:T(2,128)S(1)}, f32[2,128]{1,0:T(2,128)}, u32[]{:S(2)}) copy-start(f32[2,128]{1,0:T(2,128)} %get-tuple-element.21) | copy-start | bytes 3076
  31.7 27.5 %collective-permute-start.3 = (bf16[2,128,1024]{2,1,0:T(8,128)(2,1)}, bf16[2,128,1024]{2,1,0:T(8,128)(2,1)S(1)}, u32[]{:S(2)}, u32[]{:S(2)}) collective-permute-start(bf16[2,128,1024]{2,1,0:T(8,128)(2,1)} %get-tuple-element.19), channel_id=1, source_target_pairs={{1,0},{2,1},{3,2},{4,3},{5,4},{6,5},{7,6},{9,8},{10,9},{11,10},{12... | collective-permute-start | bytes 1572872 | tf_op jit(solution)/shard_map/ppermute | solution.py:24
  33.7 41.0 %all-to-all-start = ((f32[128,2,128]{2,1,0:T(2,128)}), f32[128,2,128]{2,1,0:T(2,128)S(1)}, u32[]{:S(2)}, u32[]{:S(2)}) async-start(f32[128,2,128]{2,1,0:T(2,128)} %broadcast_in_dim.2), calls=%async_computation | async-start | bytes 262144 | tf_op jit(solution)/shard_map/all_to_all | solution.py:18
  61.3 0.7 copy-start

commit v9 on v8

--- a/solution.py
+++ b/solution.py
@@ -4,17 +4,14 @@
 import jax.numpy as jnp
 from jax import lax
 from jax.experimental import pallas as pl
+from jax.experimental.pallas import tpu as pltpu
 from jax.sharding import PartitionSpec as P
 
 epsilon = 1e-06
 score_scale = 168.0 ** (-0.5)
 
 
-def gathered_over(x, axes):
-    devices = 1
-    for axis in axes:
-        devices *= lax.axis_size(axis)
-    copies = jnp.broadcast_to(x[None], (devices,) + x.shape)
+def gathered_over(copies, axes):
     return lax.all_to_all(copies, axes, 0, 0, tiled=True)
 
 
@@ -37,7 +34,7 @@
 
 
 def window_kernel(ratio, head_dim, per_step, lo_ref, qgain_ref, kgain_ref, q_ref, k_ref, v_ref, kh_ref, vh_ref,
-                  up_ref, qgrad_ref, own_ref, send_ref, gains_ref):
+                  up_ref, qgrad_ref, own_ref, send_ref, copies_ref, gains_ref):
     @pl.when(pl.program_id(0) == 0)
     def _():
         gains_ref[...] = jnp.zeros_like(gains_ref)
@@ -45,6 +42,10 @@
     for g in range(per_step):
         one_group(ratio, head_dim, g, lo_ref, qgain_ref, kgain_ref, q_ref, k_ref, v_ref, kh_ref, vh_ref, up_ref,
                   qgrad_ref, own_ref, send_ref, gains_ref)
+
+    @pl.when(pl.program_id(0) == pl.num_programs(0) - 1)
+    def _():
+        copies_ref[...] = jnp.broadcast_to(gains_ref[...][None], copies_ref.shape)
 
 
 def one_group(ratio, head_dim, g, lo_ref, qgain_ref, kgain_ref, q_ref, k_ref, v_ref, kh_ref, vh_ref, up_ref,
@@ -94,7 +95,7 @@
 
 
 def window_attention(lo_rel, query_gain, key_gain, query_local, key_local, value_local, key_halo, value_halo, upstream,
-                     ratio, head_dim):
+                     ratio, head_dim, copies):
     rows, query_width = query_local.shape
     key_width = key_local.shape[1]
     per_step = GROUPS_PER_STEP
@@ -121,14 +122,15 @@
             pl.BlockSpec((rows, qw), lambda g: (0, g)),
             pl.BlockSpec((2, rows, kw), lambda g: (0, 0, g)),
             pl.BlockSpec((2, rows, kw), lambda g: (0, 0, g)),
-            pl.BlockSpec((2, head_dim), lambda g: (0, 0)),
+            pl.BlockSpec((copies, 2, head_dim), lambda g: (0, 0, 0)),
         ],
         out_shape=[
             jax.ShapeDtypeStruct((rows, query_width), jnp.bfloat16),
             jax.ShapeDtypeStruct((2, rows, key_width), jnp.float32),
             jax.ShapeDtypeStruct((2, rows, key_width), jnp.bfloat16),
-            jax.ShapeDtypeStruct((2, head_dim), jnp.float32),
+            jax.ShapeDtypeStruct((copies, 2, head_dim), jnp.float32),
         ],
+        scratch_shapes=[pltpu.VMEM((2, head_dim), jnp.float32)],
         cost_estimate=pl.CostEstimate(
             flops=flops,
             transcendentals=rows * keys * ratio * groups * per_step,
@@ -161,7 +163,8 @@
     key_unit, key_inverse, _ = normalize(key_local.astype(jnp.float32).reshape(rows, groups, head_dim), key_scale)
     key_unit, key_inverse, query_local = lax.optimization_barrier((key_unit, key_inverse, query_local))
     query_grad, own, send, gain_terms = window_attention(
-        lo_rel, query_gain, key_gain, query_local, key_local, value_local, key_halo, value_halo, upstream, ratio, head_dim
+        lo_rel, query_gain, key_gain, query_local, key_local, value_local, key_halo, value_halo, upstream, ratio, head_dim,
+        lax.axis_size("dp") * lax.axis_size("seq"),
     )
     back = shifted(send, "seq", -1)
     received = gathered_over(gain_terms, ("dp", "seq"))

time: 76.5 us -> 75.9 us (level)
  the two profiles are of different devices: /device:TPU:1 before, /device:TPU:2 now
where the time goes in v9:
time: 75.9 us; the launch traced here: 75.2 us
  starting transfers between devices  40.1 us (53%)
  waiting for transfers between devices  17.9 us (24%)
  Pallas kernels  7.87 us (10%)
  other arithmetic  4.85 us (6%)
  local copies, waits for them, and re-layouts  3.73 us (5%)
  between operations  0.79 us (1%)
    all_to_all x1, starting transfers between devices, gathered_over(): return lax.all_to_all(copies, axes, 0, 0, tiled=True)  26.5 us
    all_to_all x1, waiting for transfers between devices, gathered_over(): return lax.all_to_all(copies, axes, 0, 0, tiled=True)  13.9 us
    ppermute x3, starting transfers between devices, shifted(): return lax.ppermute(x, axis, pairs)  11.7 us
    pallas_call x1, Pallas kernels, window_attention(): pl.pallas_call(functools.partial(window_kernel, ratio, head_dim, per_step...  7.87 us
    ppermute x1, waiting for transfers between devices, on_device(): lax.ppermute(out_grad.reshape(rows, query_width), 'pipe', [(i, (i - 1) %...  2.65 us
    convert_element_type x1, other arithmetic, on_device(): value_grad = value_rows.astype(jnp.bfloat16)  2.04 us
    ppermute x1, starting transfers between devices, on_device(): lax.ppermute(out_grad.reshape(rows, query_width), 'pipe', [(i, (i - 1) %...  1.92 us
    unnamed x10, local copies, waits for them, and re-layouts  1.66 us
  transfers between devices with their start and end apart: 5, of which 3 were waited for; matrix products, arithmetic and copies ran while one was open for 8% of the time, Pallas kernels for 0%

profile of v9, /device:TPU:2, one launch (start us, length us, event | category | flops | bytes accessed | tf_op | source)
XLA Modules:
  0.0 75.2 jit_solution(10141831149166292978)
XLA Ops:
  0.6 5.2 %collective-permute-start.1 = (bf16[128,1024]{1,0:T(8,128)(2,1)}, bf16[128,1024]{1,0:T(8,128)(2,1)S(1)}, u32[]{:S(2)}, u32[]{:S(2)}) collective-permute-start(bf16[128,1024]{1,0:T(8,128)(2,1)} %bitcast.36), channel_id=1, source_target_pairs={{0,1},{1,2},{2,3},{3,4},{4,5},{5,6},{6,7},{8,9},{9,10},{10,11},{11... | collective-permute-start | bytes 786440 | tf_op jit(solution)/shard_map/ppermute | solution.py:21
  5.8 5.2 %collective-permute-start = (bf16[128,1024]{1,0:T(8,128)(2,1)}, bf16[128,1024]{1,0:T(8,128)(2,1)S(1)}, u32[]{:S(2)}, u32[]{:S(2)}) collective-permute-start(bf16[128,1024]{1,0:T(8,128)(2,1)} %bitcast.28), channel_id=1, source_target_pairs={{0,1},{1,2},{2,3},{3,4},{4,5},{5,6},{6,7},{8,9},{9,10},{10,11},{11... | collective-permute-start | bytes 786440 | tf_op jit(solution)/shard_map/ppermute | solution.py:21
  11.0 1.9 %collective-permute-start.2 = (bf16[128,2048]{1,0:T(8,128)(2,1)}, bf16[128,2048]{1,0:T(8,128)(2,1)S(1)}, u32[]{:S(2)}, u32[]{:S(2)}) collective-permute-start(bf16[128,2048]{1,0:T(8,128)(2,1)} %bitcast.34), channel_id=1, source_target_pairs={{0,56},{8,0},{16,8},{24,16},{32,24},{40,32},{48,40},{56,48},{1,57}... | collective-permute-start | bytes 1572872 | tf_op jit(solution)/shard_map/ppermute | solution.py:154
  13.0 1.0 %convert_bitcast_fusion = f32[16,8,8,128]{3,1,2,0:T(8,128)S(1)} fusion(bf16[1,1,128,1024]{3,2,1,0:T(8,128)(2,1)} %param.8), kind=kLoop, calls=%fused_computation.1 | loop fusion | flops 131072 | bytes 786432
  14.0 0.1 copy.13
  14.1 0.2 multiply_reduce_fusion.1
  14.3 0.7 subtract_bitcast_fusion
  15.0 0.7 copy.12.lo_ref
  15.7 0.2 broadcast_multiply_fusion
  15.9 0.0 collective-permute-done.1.vh_ref
  15.9 0.0 copy-start.2
  16.0 1.4 %collective-permute-done.kh_ref = bf16[128,1024]{1,0:T(8,128)(2,1)S(1)} collective-permute-done((bf16[128,1024]{1,0:T(8,128)(2,1)}, bf16[128,1024]{1,0:T(8,128)(2,1)S(1)}, u32[]{:S(2)}, u32[]{:S(2)}) %collective-permute-start) | collective-permute-done | bytes 262176 | tf_op jit(solution)/shard_map/ppermute | solution.py:21
  17.3 0.0 copy-start.3
  17.3 2.7 %collective-permute-done.2.up_ref = bf16[128,2048]{1,0:T(8,128)(2,1)S(1)} collective-permute-done((bf16[128,2048]{1,0:T(8,128)(2,1)}, bf16[128,2048]{1,0:T(8,128)(2,1)S(1)}, u32[]{:S(2)}, u32[]{:S(2)}) %collective-permute-start.2) | collective-permute-done | bytes 524320 | tf_op jit(solution)/shard_map/ppermute | solution.py:154
  20.0 0.0 copy-done.2
  20.0 0.0 copy-done.3
  20.0 0.0 copy-start.1
  20.0 0.8 %copy-done.1 = bf16[128,2048]{1,0:T(8,128)(2,1)} copy-done((bf16[128,2048]{1,0:T(8,128)(2,1)}, bf16[128,2048]{1,0:T(8,128)(2,1)S(1)}, u32[]{:S(2)}) %copy-start.1) | copy-done | bytes 524312
  20.8 7.9 %shard_map.110 = (bf16[128,2048]{1,0:T(8,128)(2,1)}, f32[2,128,1024]{2,1,0:T(8,128)}, bf16[2,128,1024]{2,1,0:T(8,128)(2,1)}, f32[128,2,128]{2,1,0:T(2,128)}) custom-call(s32[128,1]{1,0:T(8,128)} %copy.12.lo_ref, f32[1,128]{1,0:T(1,128)} %qgain_ref.1, f32[1,128]{1,0:T(1,128)} %kgain_ref.1, bf16[128,2048]{1,0:T(8,128)(2,1)} %bitcast.35, ...), custom_call_target="tpu_custom_call" | custom-call | flops 805306368 | bytes 4718592 | tf_op jit(solution)/shard_map/pallas_call | solution.py:107
  28.7 1.3 %collective-permute-start.3 = (bf16[2,128,1024]{2,1,0:T(8,128)(2,1)}, bf16[2,128,1024]{2,1,0:T(8,128)(2,1)S(1)}, u32[]{:S(2)}, u32[]{:S(2)}) collective-permute-start(bf16[2,128,1024]{2,1,0:T(8,128)(2,1)} %get-tuple-element.19), channel_id=1, source_target_pairs={{1,0},{2,1},{3,2},{4,3},{5,4},{6,5},{7,6},{9,8},{10,9},{11,10},{12... | collective-permute-start | bytes 1572872 | tf_op jit(solution)/shard_map/ppermute | solution.py:21
  30.0 26.5 %all-to-all-start = ((f32[128,2,128]{2,1,0:T(2,128)}), f32[128,2,128]{2,1,0:T(2,128)S(1)}, u32[]{:S(2)}, u32[]{:S(2)}) async-start(f32[128,2,128]{2,1,0:T(2,128)} %get-tuple-element.21), calls=%async_computation | async-start | bytes 262144 | tf_op jit(solution)/shard_map/all_to_all | solution.py:15
  56.5 0.0 collective-permute-done.3
  56.5 2.0 %fusion = (bf16[128,1024]{1,0:T(8,128)(2,1)}, f32[16,8,8,128]{3,1,2,0:T(8,128)S(1)}) fusion(f32[2,128,1024]{2,1,0:T(8,128)} %get-tuple-element.18, bf16[2,128,1024]{2,1,0:T(8,128)(2,1)S(1)} %collective-permute-done.3), kind=kLoop, calls=%fused_computation.7 | loop fusion | flops 655360 | bytes 2359296 | tf_op jit(solution)/shard_map/convert_element_type | solution.py:174
  58.5 0.1 copy.14
  58.6 0.0 copy-start
  58.6 0.6 copy-done
  59.3 0.2 multiply_reduce_fusion
  59.5 0.3 multiply_convert_fusion
  59.9 13.9 %all-to-all-done = f32[128,2,128]{2,1,0:T(2,128)S(1)} async-done(((f32[128,2,128]{2,1,0:T(2,128)}), f32[128,2,128]{2,1,0:T(2,128)S(1)}, u32[]{:S(2)}, u32[]{:S(2)}) %all-to-all-start) | async-done | bytes 131104 | tf_op jit(solution)/shard_map/all_to_all | solution.py:15
  73.8 0.8 %reshape.89 = bf16[1,1,128,1024]{3,2,1,0:T(8,128)(2,1)} reshape(bf16[128,8,128]{2,1,0:T(8,128)(2,1)S(1)} %multiply_convert_fusion) | data formatting | bytes 524288 | tf_op jit(solution)/shard_map/reshape | solution.py:179
  74.6 0.1 reduce_sum.29
  74.7 0.5 fusion.2
  (3 shorter events, 0.1 us)
Async XLA Ops:
  0.6 15.3 %collective-permute-start.1 = (bf16[128,1024]{1,0:T(8,128)(2,1)}, bf16[128,1024]{1,0:T(8,128)(2,1)S(1)}, u32[]{:S(2)}, u32[]{:S(2)}) collective-permute-start(bf16[128,1024]{1,0:T(8,128)(2,1)} %bitcast.36), channel_id=1, source_target_pairs={{0,1},{1,2},{2,3},{3,4},{4,5},{5,6},{6,7},{8,9},{9,10},{10,11},{11... | collective-permute-start | bytes 786440 | tf_op jit(solution)/shard_map/ppermute | solution.py:21
  5.8 11.5 %collective-permute-start = (bf16[128,1024]{1,0:T(8,128)(2,1)}, bf16[128,1024]{1,0:T(8,128)(2,1)S(1)}, u32[]{:S(2)}, u32[]{:S(2)}) collective-permute-start(bf16[128,1024]{1,0:T(8,128)(2,1)} %bitcast.28), channel_id=1, source_target_pairs={{0,1},{1,2},{2,3},{3,4},{4,5},{5,6},{6,7},{8,9},{9,10},{10,11},{11... | collective-permute-start | bytes 786440 | tf_op jit(solution)/shard_map/ppermute | solution.py:21
  11.0 8.9 %collective-permute-start.2 = (bf16[128,2048]{1,0:T(8,128)(2,1)}, bf16[128,2048]{1,0:T(8,128)(2,1)S(1)}, u32[]{:S(2)}, u32[]{:S(2)}) collective-permute-start(bf16[128,2048]{1,0:T(8,128)(2,1)} %bitcast.34), channel_id=1, source_target_pairs={{0,56},{8,0},{16,8},{24,16},{32,24},{40,32},{48,40},{56,48},{1,57}... | collective-permute-start | bytes 1572872 | tf_op jit(solution)/shard_map/ppermute | solution.py:154
  15.9 4.0 %copy-start.2 = (bf16[128,1024]{1,0:T(8,128)(2,1)}, bf16[128,1024]{1,0:T(8,128)(2,1)S(1)}, u32[]{:S(2)}) copy-start(bf16[128,1024]{1,0:T(8,128)(2,1)S(1)} %collective-permute-done.1.vh_ref) | copy-start | bytes 786436
  17.3 2.7 %copy-start.3 = (bf16[128,1024]{1,0:T(8,128)(2,1)}, bf16[128,1024]{1,0:T(8,128)(2,1)S(1)}, u32[]{:S(2)}) copy-start(bf16[128,1024]{1,0:T(8,128)(2,1)S(1)} %collective-permute-done.kh_ref) | copy-start | bytes 786436
  20.0 0.8 %copy-start.1 = (bf16[128,2048]{1,0:T(8,128)(2,1)}, bf16[128,2048]{1,0:T(8,128)(2,1)S(1)}, u32[]{:S(2)}) copy-start(bf16[128,2048]{1,0:T(8,128)(2,1)S(1)} %collective-permute-done.2.up_ref) | copy-start | bytes 1572868
  28.7 27.8 %collective-permute-start.3 = (bf16[2,128,1024]{2,1,0:T(8,128)(2,1)}, bf16[2,128,1024]{2,1,0:T(8,128)(2,1)S(1)}, u32[]{:S(2)}, u32[]{:S(2)}) collective-permute-start(bf16[2,128,1024]{2,1,0:T(8,128)(2,1)} %get-tuple-element.19), channel_id=1, source_target_pairs={{1,0},{2,1},{3,2},{4,3},{5,4},{6,5},{7,6},{9,8},{10,9},{11,10},{12... | collective-permute-start | bytes 1572872 | tf_op jit(solution)/shard_map/ppermute | solution.py:21
  30.0 43.8 %all-to-all-start = ((f32[128,2,128]{2,1,0:T(2,128)}), f32[128,2,128]{2,1,0:T(2,128)S(1)}, u32[]{:S(2)}, u32[]{:S(2)}) async-start(f32[128,2,128]{2,1,0:T(2,128)} %get-tuple-element.21), calls=%async_computation | async-start | bytes 262144 | tf_op jit(solution)/shard_map/all_to_all | solution.py:15
  58.6 0.7 copy-start
